TPU v7x, 256 devices: a whole 4x4x8 slice. The times are simulated.
256 devices in a mesh: seq: 8 (over x, core), dp: 32 (over y, z).
Axes of the slice: x: 4, y: 4, z: 8, core: 2. Of those that a mesh axis runs over, the one named last changes fastest.
Arguments:
- queries: bfloat16 [32, 1024, 4096], P('dp', 'seq'), may hold values from -4.5 to 4.5
- rotated_key_matrix: bfloat16 [32, 1024, 1024], P('dp', 'seq'), may hold values from -4.5 to 4.5
- value_matrix: bfloat16 [32, 1024, 1024], P('dp', 'seq'), may hold values from -6 to 6
- out_weight: bfloat16 [4096, 2048], P('seq'), may hold values from -0.09375 to 0.09375
- out_grad: bfloat16 [32, 1024, 2048], P('dp', 'seq'), may hold values from -6 to 6
- lengths: int32 [32, 16], P('dp'), may hold values from 1 to 256, 1024 in all within a row
- pack_order: int32 [32, 16], P('dp'), may hold values from 0 to 15, each once within a row
Outputs:
- layer_out: bfloat16 [32, 1024, 2048], P('dp', 'seq')
- query_grad: bfloat16 [32, 1024, 4096], P('dp', 'seq')
- key_grad: bfloat16 [32, 1024, 1024], P('dp', 'seq')
- value_grad: bfloat16 [32, 1024, 1024], P('dp', 'seq')
- weight_grad: float32 [4096, 2048], P('seq', 'dp')
Inputs may be any that keep to these rules, and one draw needn't show every extreme that they name: The 16 lengths of a window sum to 1024; the longest is 256. `pack_order`: each row names every sample once.
All inputs are finite; a program needn't handle non-finite values.
Results may differ from a plain program's by a relative error of at most 0.017.
Values may be sent and summed in bfloat16 or wider, within the bound.
No kernel may reach another device: no remote copies, remote signals or barrier semaphores. Data moves between devices by JAX's collectives and lax.ppermute only.
A program may use at most 128 MiB of HBM per device.

v0:
```python
import jax
import jax.numpy as jnp
from jax import lax
from jax.sharding import PartitionSpec as P

QUERY_HEADS = 32
KEY_VALUE_HEADS = 8
HEAD_SIZE = 128


def row_starts(lengths, pack_order, win_rows):
    samples = lengths.shape[0]
    picked = jnp.sum(
        jnp.where(
            pack_order[:, None] == jnp.arange(samples, dtype=jnp.int32)[None, :],
            lengths[None, :],
            0,
        ),
        axis=1,
        dtype=jnp.int32,
    )
    seg_ends = jnp.cumsum(picked, dtype=jnp.int32)
    places = jnp.arange(win_rows, dtype=jnp.int32)
    return jnp.sum(
        jnp.where(seg_ends[None, :] <= places[:, None], picked[None, :], 0), axis=1, dtype=jnp.int32
    )


def local(queries, rotated_key_matrix, value_matrix, out_weight, out_grad, lengths, pack_order):
    row_total_count = queries.shape[1]
    head_scale = HEAD_SIZE ** (-0.5)
    q_tok = queries.reshape(row_total_count, QUERY_HEADS, HEAD_SIZE)
    key_token_rows = rotated_key_matrix.reshape(row_total_count, KEY_VALUE_HEADS, HEAD_SIZE)
    value_token_rows = value_matrix.reshape(row_total_count, KEY_VALUE_HEADS, HEAD_SIZE)
    q_loc, k_loc, v_loc = (
        lax.all_to_all(q_tok, "seq", split_axis=1, concat_axis=0, tiled=True),
        lax.all_to_all(key_token_rows, "seq", split_axis=1, concat_axis=0, tiled=True),
        lax.all_to_all(value_token_rows, "seq", split_axis=1, concat_axis=0, tiled=True),
    )
    win_rows = q_loc.shape[0]
    kv_local = k_loc.shape[1]
    group_width = q_loc.shape[1] // kv_local
    query_head_rows = q_loc.reshape(win_rows, kv_local, group_width, HEAD_SIZE)
    starts = row_starts(lengths[0], pack_order[0], win_rows)
    block_rows = min(512, win_rows)
    blk_count = win_rows // block_rows

    def blk_bounds():
        return (jnp.int32(0), jnp.int32(blk_count))

    def score_tile(q_blk, q_start, k_start):
        k_tile = lax.dynamic_slice_in_dim(k_loc, k_start, block_rows, 0)
        scores = (
            jnp.einsum("qkgd,skd->kgqs", q_blk, k_tile, preferred_element_type=jnp.float32)
            * head_scale
        )
        rows_at = q_start + jnp.arange(block_rows, dtype=jnp.int32)
        cols_at = k_start + jnp.arange(block_rows, dtype=jnp.int32)
        first_at = lax.dynamic_slice_in_dim(starts, q_start, block_rows, 0)
        visible = (cols_at[None, :] >= first_at[:, None]) & (cols_at[None, :] <= rows_at[:, None])
        return (scores, visible)

    def forward_block(blk_index):
        q_start = blk_index * block_rows
        q_blk = lax.dynamic_slice_in_dim(query_head_rows, q_start, block_rows, 0)
        lower_blk, upper_blk = blk_bounds()

        def gather_stats(k_blk, running):
            row_max, row_sum = running
            scores, visible = score_tile(q_blk, q_start, k_blk * block_rows)
            tile_max = jnp.max(jnp.where(visible, scores, -1e30), axis=-1, keepdims=True)
            new_max = jnp.maximum(row_max, tile_max)
            row_sum = row_sum * jnp.exp(row_max - new_max) + jnp.sum(
                jnp.where(visible, jnp.exp(scores - new_max), 0.0), axis=-1, keepdims=True
            )
            return (new_max, row_sum)

        stat_shape = (kv_local, group_width, block_rows, 1)
        row_max, row_sum = lax.fori_loop(
            lower_blk,
            upper_blk,
            gather_stats,
            (jnp.full(stat_shape, -1e30, jnp.float32), jnp.zeros(stat_shape, jnp.float32)),
        )

        def weigh(k_blk, summed):
            k_start = k_blk * block_rows
            scores, visible = score_tile(q_blk, q_start, k_start)
            half_probability = (
                jnp.where(visible, jnp.exp(scores - row_max), 0.0) / row_sum
            ).astype(jnp.bfloat16)
            v_tile = lax.dynamic_slice_in_dim(v_loc, k_start, block_rows, 0)
            return summed + jnp.einsum(
                "kgqs,skd->qkgd", half_probability, v_tile, preferred_element_type=jnp.float32
            )

        summed = lax.fori_loop(
            lower_blk,
            upper_blk,
            weigh,
            jnp.zeros((block_rows, kv_local, group_width, HEAD_SIZE), jnp.float32),
        )
        return (summed.astype(jnp.bfloat16), row_max, row_sum)

    attn_out, max_all, sum_all = lax.map(forward_block, jnp.arange(blk_count, dtype=jnp.int32))
    attn_out = attn_out.reshape(win_rows, kv_local, group_width, HEAD_SIZE)
    a_head = attn_out.reshape(win_rows, kv_local * group_width * HEAD_SIZE)
    grad_rows = out_grad.reshape(row_total_count, out_grad.shape[2])
    a_rows = a_head
    product = jnp.dot(a_rows, out_weight, preferred_element_type=jnp.float32)
    y_out = lax.psum_scatter(
        lax.optimization_barrier(product.astype(jnp.bfloat16))
        .astype(jnp.float32)
        .astype(jnp.bfloat16),
        "seq",
        scatter_dimension=0,
        tiled=True,
    )
    incoming = lax.all_gather(grad_rows, "seq", axis=0, tiled=True)
    a_rows = a_head
    wo_grad = lax.dot_general(
        a_rows, incoming, (((0,), (0,)), ((), ())), preferred_element_type=jnp.float32
    )
    d_rows = lax.dot_general(
        incoming, out_weight, (((1,), (1,)), ((), ())), preferred_element_type=jnp.float32
    )
    d_all, wo_grad = (d_rows, wo_grad)
    attention_grad = d_all.astype(jnp.bfloat16).reshape(win_rows, kv_local, group_width, HEAD_SIZE)

    def back_block(blk_index, running):
        dq_all, dk_acc, dv_acc = running
        q_start = blk_index * block_rows
        q_blk = lax.dynamic_slice_in_dim(query_head_rows, q_start, block_rows, 0)
        g_blk = lax.dynamic_slice_in_dim(attention_grad, q_start, block_rows, 0)
        o_blk = lax.dynamic_slice_in_dim(attn_out, q_start, block_rows, 0)
        row_max = max_all[blk_index]
        row_sum = sum_all[blk_index]
        row_dot = jnp.sum(g_blk.astype(jnp.float32) * o_blk.astype(jnp.float32), axis=-1)
        row_dot = jnp.transpose(row_dot, (1, 2, 0))[..., None]
        lower_blk, upper_blk = blk_bounds()

        def per_tile(k_blk, inner):
            dq_acc, dk_run, dv_run = inner
            k_start = k_blk * block_rows
            scores, visible = score_tile(q_blk, q_start, k_start)
            attn_prob = jnp.where(visible, jnp.exp(scores - row_max), 0.0) / row_sum
            k_tile = lax.dynamic_slice_in_dim(k_loc, k_start, block_rows, 0)
            v_tile = lax.dynamic_slice_in_dim(v_loc, k_start, block_rows, 0)
            d_prob = jnp.einsum("qkgd,skd->kgqs", g_blk, v_tile, preferred_element_type=jnp.float32)
            score_gradient = (attn_prob * (d_prob - row_dot) * head_scale).astype(jnp.bfloat16)
            dq_acc = dq_acc + jnp.einsum(
                "kgqs,skd->qkgd", score_gradient, k_tile, preferred_element_type=jnp.float32
            )
            dk_part = jnp.einsum(
                "ubnh,nubr->hur", score_gradient, q_blk, preferred_element_type=jnp.float32
            )
            dv_part = jnp.einsum(
                "ubnh,nubr->hur",
                attn_prob.astype(jnp.bfloat16),
                g_blk,
                preferred_element_type=jnp.float32,
            )
            dk_run = lax.dynamic_update_slice_in_dim(
                dk_run,
                lax.dynamic_slice_in_dim(dk_run, k_start, block_rows, 0) + dk_part,
                k_start,
                0,
            )
            dv_run = lax.dynamic_update_slice_in_dim(
                dv_run,
                lax.dynamic_slice_in_dim(dv_run, k_start, block_rows, 0) + dv_part,
                k_start,
                0,
            )
            return (dq_acc, dk_run, dv_run)

        dq_blk, dk_acc, dv_acc = lax.fori_loop(
            lower_blk,
            upper_blk,
            per_tile,
            (
                jnp.zeros((block_rows, kv_local, group_width, HEAD_SIZE), jnp.float32),
                dk_acc,
                dv_acc,
            ),
        )
        dq_all = lax.dynamic_update_slice_in_dim(dq_all, dq_blk.astype(jnp.bfloat16), q_start, 0)
        return (dq_all, dk_acc, dv_acc)

    dq_all, dk_acc, dv_acc = lax.fori_loop(
        0,
        blk_count,
        back_block,
        (
            jnp.zeros((win_rows, kv_local, group_width, HEAD_SIZE), jnp.bfloat16),
            jnp.zeros((win_rows, kv_local, HEAD_SIZE), jnp.float32),
            jnp.zeros((win_rows, kv_local, HEAD_SIZE), jnp.float32),
        ),
    )
    d_q = dq_all.reshape(win_rows, kv_local * group_width, HEAD_SIZE)
    d_q, key_gradient, value_gradient = (
        lax.all_to_all(d_q, "seq", split_axis=0, concat_axis=1, tiled=True),
        lax.all_to_all(dk_acc.astype(jnp.bfloat16), "seq", split_axis=0, concat_axis=1, tiled=True),
        lax.all_to_all(dv_acc.astype(jnp.bfloat16), "seq", split_axis=0, concat_axis=1, tiled=True),
    )
    weight_grad = lax.psum_scatter(wo_grad, "dp", scatter_dimension=1, tiled=True)
    return (
        y_out.reshape(1, row_total_count, y_out.shape[1]),
        d_q.reshape(1, row_total_count, QUERY_HEADS * HEAD_SIZE),
        key_gradient.reshape(1, row_total_count, KEY_VALUE_HEADS * HEAD_SIZE),
        value_gradient.reshape(1, row_total_count, KEY_VALUE_HEADS * HEAD_SIZE),
        weight_grad,
    )


def solution(mesh):
    in_specs = (
        P("dp", "seq", None),
        P("dp", "seq", None),
        P("dp", "seq", None),
        P("seq", None),
        P("dp", "seq", None),
        P("dp", None),
        P("dp", None),
    )
    out_specs = (
        P("dp", "seq", None),
        P("dp", "seq", None),
        P("dp", "seq", None),
        P("dp", "seq", None),
        P("seq", "dp"),
    )
    return jax.shard_map(local, mesh=mesh, in_specs=in_specs, out_specs=out_specs, check_vma=False)
```

profile of v0, /device:TPU:2, one launch (start us, length us, event | category | flops | bytes accessed | tf_op | source)
XLA Modules:
  0.0 368.9 jit_solution(395930045681051977)
XLA Ops:
  7.2 1.1 copy.142
  9.1 5.6 %all-to-all-start.2 = ((bf16[128,8,128]{2,0,1:T(8,128)(2,1)}), bf16[128,8,128]{2,0,1:T(8,128)(2,1)S(1)}, u32[]{:S(2)}, u32[]{:S(2)}) async-start(bf16[128,8,128]{2,0,1:T(8,128)(2,1)} %copy.118), calls=%async_computation.2 | async-start | bytes 524288 | tf_op jit(solution)/shard_map/all_to_all | solution.py:38
  14.7 2.3 copy.113
  16.9 3.8 %all-to-all-done.2 = bf16[128,8,128]{2,0,1:T(8,128)(2,1)S(1)} async-done(((bf16[128,8,128]{2,0,1:T(8,128)(2,1)}), bf16[128,8,128]{2,0,1:T(8,128)(2,1)S(1)}, u32[]{:S(2)}, u32[]{:S(2)}) %all-to-all-start.2) | async-done | bytes 262176 | tf_op jit(solution)/shard_map/all_to_all | solution.py:38
  20.8 5.6 %all-to-all-start = ((bf16[128,32,128]{0,2,1:T(8,128)(2,1)}), bf16[128,32,128]{0,2,1:T(8,128)(2,1)}, u32[]{:S(2)}, u32[]{:S(2)}) async-start(bf16[128,32,128]{0,2,1:T(8,128)(2,1)} %bitcast.336), calls=%async_computation | async-start | bytes 2097152 | tf_op jit(solution)/shard_map/all_to_all | solution.py:36
  27.9 13.1 %all-to-all-done = bf16[128,32,128]{0,2,1:T(8,128)(2,1)} async-done(((bf16[128,32,128]{0,2,1:T(8,128)(2,1)}), bf16[128,32,128]{0,2,1:T(8,128)(2,1)}, u32[]{:S(2)}, u32[]{:S(2)}) %all-to-all-start) | async-done | bytes 1048608 | tf_op jit(solution)/shard_map/all_to_all | solution.py:36
  40.9 4.8 %all-to-all-start.1 = ((bf16[128,8,128]{2,0,1:T(8,128)(2,1)}), bf16[128,8,128]{2,0,1:T(8,128)(2,1)S(1)}, u32[]{:S(2)}, u32[]{:S(2)}) async-start(bf16[128,8,128]{2,0,1:T(8,128)(2,1)} %copy.117), calls=%async_computation.1 | async-start | bytes 524288 | tf_op jit(solution)/shard_map/all_to_all | solution.py:37
  46.4 2.3 copy.115
  48.7 6.3 %all-to-all-done.1 = bf16[128,8,128]{2,0,1:T(8,128)(2,1)S(1)} async-done(((bf16[128,8,128]{2,0,1:T(8,128)(2,1)}), bf16[128,8,128]{2,0,1:T(8,128)(2,1)S(1)}, u32[]{:S(2)}, u32[]{:S(2)}) %all-to-all-start.1) | async-done | bytes 262176 | tf_op jit(solution)/shard_map/all_to_all | solution.py:37
  55.0 31.5 %while.94 = (s32[]{:T(128)}, bf16[2,512,1,4,128]{1,4,3,2,0:T(8,128)(2,1)}, f32[2,1,4,512,1]{3,2,4,1,0:T(4,128)S(1)}, f32[2,1,4,512,1]{3,2,4,1,0:T(4,128)S(1)}, s...) while((s32[]{:T(128)}, ...), condition=%wide.region_10.11_spmd, body=%wide.region_3.10_spmd.sunk | while | flops 820260864 | bytes 16042333 | solution.py:105
  57.3 4.3 %while.97 = (s32[]{:T(128)}, f32[1,4,512,1]{2,1,3,0:T(4,128)S(1)}, f32[1,4,512,1]{2,1,3,0:T(4,128)S(1)}, s32[512]{0:T(512)S(1)}, s32[]{:T(128)}, /*index=5*/bf16...) while((s32[]{:T(128)}, f32[1,4,512,1]{2,1,3,0:T(4,128)S(1)}, ...), condition=%wide.region_7.7_spmd.clone, body=%wide.region_4.6_spmd.clone.sunk | while | flops 276573184 | bytes 9947322 | solution.py:79
  61.7 7.0 %while.98 = (s32[]{:T(128)}, f32[512,1,4,128]{0,3,2,1:T(8,128)}, bf16[1024,1,128]{0,2,1:T(8,128)(2,1)S(1)}, s32[512]{0:T(512)S(1)}, s32[]{:T(128)}, /*index=5*/b...) while((s32[]{:T(128)}, f32[512,1,4,128]{0,3,2,1:T(8,128)}, ...), condition=%wide.region_9.9_spmd.clone, body=%wide.region_8.8_spmd.clone.sunk | while | flops 543425536 | bytes 3436228 | solution.py:97
  62.0 2.6 fusion.139
  64.9 3.8 %fusion.139 = f32[512,1,4,128]{0,3,2,1:T(8,128)} fusion(f32[4,512]{1,0:T(4,128)S(1)} %bitcast.333, f32[4,512]{1,0:T(4,128)S(1)} %bitcast.329, pred[512,512]{0,1:T(8,128)(4,1)S(1)} %compare_and_fusion.8, f32[512,1,4,128]{0,3,2,1:T(8,128)} %get-tuple-element.1481, bf16[512,1,4,128]{3,0,2,1:T(8,128)(2,1)S(1)} %get-tuple-element.1499, ...), kind=kOutput, calls=%fused_computation.25.clone.1 | convolution fusion | flops 542638080 | bytes 3163648 | tf_op jit(solution)/shard_map/while/body/eval_jaxpr/while/body/kgqs,skd->qkgd/dot_general | solution.py:93
  68.7 2.1 bitcast_dynamic-update-slice_fusion.5
  73.1 4.3 %while.97 = (s32[]{:T(128)}, f32[1,4,512,1]{2,1,3,0:T(4,128)S(1)}, f32[1,4,512,1]{2,1,3,0:T(4,128)S(1)}, s32[512]{0:T(512)S(1)}, s32[]{:T(128)}, /*index=5*/bf16...) while((s32[]{:T(128)}, f32[1,4,512,1]{2,1,3,0:T(4,128)S(1)}, ...), condition=%wide.region_7.7_spmd.clone, body=%wide.region_4.6_spmd.clone.sunk | while | flops 276573184 | bytes 9947322 | solution.py:79
  77.4 7.0 %while.98 = (s32[]{:T(128)}, f32[512,1,4,128]{0,3,2,1:T(8,128)}, bf16[1024,1,128]{0,2,1:T(8,128)(2,1)S(1)}, s32[512]{0:T(512)S(1)}, s32[]{:T(128)}, /*index=5*/b...) while((s32[]{:T(128)}, f32[512,1,4,128]{0,3,2,1:T(8,128)}, ...), condition=%wide.region_9.9_spmd.clone, body=%wide.region_8.8_spmd.clone.sunk | while | flops 543425536 | bytes 3436228 | solution.py:97
  77.7 2.6 fusion.139
  80.6 3.8 %fusion.139 = f32[512,1,4,128]{0,3,2,1:T(8,128)} fusion(f32[4,512]{1,0:T(4,128)S(1)} %bitcast.333, f32[4,512]{1,0:T(4,128)S(1)} %bitcast.329, pred[512,512]{0,1:T(8,128)(4,1)S(1)} %compare_and_fusion.8, f32[512,1,4,128]{0,3,2,1:T(8,128)} %get-tuple-element.1481, bf16[512,1,4,128]{3,0,2,1:T(8,128)(2,1)S(1)} %get-tuple-element.1499, ...), kind=kOutput, calls=%fused_computation.25.clone.1 | convolution fusion | flops 542638080 | bytes 3163648 | tf_op jit(solution)/shard_map/while/body/eval_jaxpr/while/body/kgqs,skd->qkgd/dot_general | solution.py:93
  84.5 2.1 bitcast_dynamic-update-slice_fusion.5
  86.5 1.7 copy.120
  89.2 4.3 %convolution_convert_fusion = bf16[1024,2048]{1,0:T(8,128)(2,1)} fusion(bf16[512,2048]{1,0:T(8,128)(2,1)S(1)} %copy-done, bf16[128,8,4,128]{3,2,1,0:T(4,128)(2,1)S(1)} %bitcast.340), kind=kOutput, calls=%fused_computation.90 | convolution fusion | flops 2149580800 | bytes 7340032 | tf_op jit(solution)/shard_map/dot_general | solution.py:110
  94.7 1.3 copy.121
  96.0 6.9 %fusion.83 = f32[512,2048]{0,1:T(8,128)} fusion(bf16[1,1024,2048]{2,1,0:T(8,128)(2,1)} %all-gather.3.cloned.1.call-done, bf16[128,8,4,128]{3,2,1,0:T(4,128)(2,1)} %bitcast.341), kind=kOutput, calls=%fused_computation.86 | convolution fusion | flops 2147483648 | bytes 9437184 | tf_op jit(solution)/shard_map/dot_general | solution.py:121
  102.9 5.5 %fusion.87 = bf16[1024,512]{0,1:T(8,128)(2,1)} fusion(bf16[512,2048]{1,0:T(8,128)(2,1)S(1)} %copy-done, bf16[1,1024,2048]{2,1,0:T(8,128)(2,1)} %all-gather.3.cloned.1.call-done), kind=kOutput, calls=%fused_computation.91 | convolution fusion | flops 2148007936 | bytes 7340032 | tf_op jit(solution)/shard_map/dot_general | solution.py:124
  110.1 1.2 broadcast_in_dim.120.clone
  111.4 38.8 %while.96 = (s32[]{:T(128)}, bf16[1024,1,4,128]{3,2,0,1:T(4,128)(2,1)}, f32[1024,1,128]{2,0,1:T(8,128)}, f32[1024,1,128]{2,0,1:T(8,128)}, bf16[1024,1,4,128]{3,0...) while((s32[]{:T(128)}, ...), condition=%wide.region_16.17_spmd, body=%wide.region_12.16_spmd.sunk | while | flops 1354365952 | bytes 50805580 | solution.py:190
  112.8 1.4 multiply_reduce_fusion.2
  115.3 12.9 %while.99 = (s32[]{:T(128)}, f32[512,1,4,128]{0,3,2,1:T(8,128)}, f32[1024,1,128]{2,0,1:T(8,128)}, f32[1024,1,128]{2,0,1:T(8,128)}, bf16[1024,1,128]{2,0,1:T(8,12...) while((s32[]{:T(128)}, f32[512,1,4,128]{0,3,2,1:T(8,128)}, ...), condition=%wide.region_15.15_spmd.clone, body=%wide.region_14.14_spmd.clone.sunk | while | flops 1353057280 | bytes 42895804 | solution.py:177
  115.7 1.3 fusion.128
  122.1 1.3 fusion.128
  128.2 1.3 convert_element_type.95
  132.2 1.4 multiply_reduce_fusion.2
  134.7 12.8 %while.99 = (s32[]{:T(128)}, f32[512,1,4,128]{0,3,2,1:T(8,128)}, f32[1024,1,128]{2,0,1:T(8,128)}, f32[1024,1,128]{2,0,1:T(8,128)}, bf16[1024,1,128]{2,0,1:T(8,12...) while((s32[]{:T(128)}, f32[512,1,4,128]{0,3,2,1:T(8,128)}, ...), condition=%wide.region_15.15_spmd.clone, body=%wide.region_14.14_spmd.clone.sunk | while | flops 1353057280 | bytes 42895804 | solution.py:177
  135.1 1.3 fusion.128
  141.5 1.3 fusion.128
  147.6 1.3 convert_element_type.95
  153.4 4.8 %all-to-all-start.5 = ((bf16[8,2,8192]{2,1,0:T(2,128)(2,1)}), bf16[8,2,8192]{2,1,0:T(2,128)(2,1)S(1)}, u32[]{:S(2)}, u32[]{:S(2)}) async-start(bf16[8,2,8192]{2,1,0:T(2,128)(2,1)} %reshape.272), calls=%async_computation.6 | async-start | bytes 524288 | tf_op jit(solution)/shard_map/all_to_all | solution.py:204
  160.1 4.1 %all-to-all-done.5 = bf16[8,2,8192]{2,1,0:T(2,128)(2,1)S(1)} async-done(((bf16[8,2,8192]{2,1,0:T(2,128)(2,1)}), bf16[8,2,8192]{2,1,0:T(2,128)(2,1)S(1)}, u32[]{:S(2)}, u32[]{:S(2)}) %all-to-all-start.5) | async-done | bytes 262176 | tf_op jit(solution)/shard_map/all_to_all | solution.py:204
  164.3 10.5 %all_to_all.96 = bf16[8,2,8192]{2,1,0:T(2,128)(2,1)} all-to-all(bf16[8,2,8192]{2,1,0:T(2,128)(2,1)S(1)} %reshape.270), channel_id=1, replica_groups=mesh['seq'=8,'dp'=32] {'seq'}, dimensions={0} | all-to-all | bytes 524288 | tf_op jit(solution)/shard_map/all_to_all | solution.py:203
  174.8 4.9 %all-to-all-start.3 = ((bf16[1024,4,128]{2,1,0:T(4,128)(2,1)}), bf16[1024,4,128]{2,1,0:T(4,128)(2,1)S(1)}, u32[]{:S(2)}, u32[]{:S(2)}) async-start(bf16[1024,4,128]{2,1,0:T(4,128)(2,1)} %bitcast.337), calls=%async_computation.4 | async-start | bytes 2097152 | tf_op jit(solution)/shard_map/all_to_all | solution.py:202
  182.6 1.8 copy.130
  184.4 1.9 reshape.271
  188.3 1.8 copy.129
  190.1 4.2 %all-to-all-done.3 = bf16[1024,4,128]{2,1,0:T(4,128)(2,1)S(1)} async-done(((bf16[1024,4,128]{2,1,0:T(4,128)(2,1)}), bf16[1024,4,128]{2,1,0:T(4,128)(2,1)S(1)}, u32[]{:S(2)}, u32[]{:S(2)}) %all-to-all-start.3) | async-done | bytes 1048608 | tf_op jit(solution)/shard_map/all_to_all | solution.py:202
  194.2 1.4 copy.124
  195.7 2.6 reshape.245
  198.3 164.1 %reduce-scatter.5.cloned.1.call-done = f32[512,64]{0,1:T(8,128)} async-done(((f32[512,2048]{0,1:T(8,128)}), f32[512,64]{0,1:T(8,128)}) %reduce-scatter.5.cloned.1.call-update) | async-done | bytes 131088 | tf_op jit(solution)/shard_map/reduce_scatter | solution.py:206
  (195 shorter events, 57.4 us)
Async XLA Ops:
  7.2 82.1 %copy-start = (bf16[512,2048]{1,0:T(8,128)(2,1)S(1)}, bf16[512,2048]{1,0:T(8,128)(2,1)}, u32[]{:S(2)}) copy-start(bf16[512,2048]{1,0:T(8,128)(2,1)} %param.20) | copy-start | bytes 6291460
  7.2 19.9 %copy-start.11 = (bf16[1,128,1024]{2,1,0:T(8,128)(2,1)S(1)}, bf16[1,128,1024]{2,1,0:T(8,128)(2,1)}, u32[]{:S(2)}) copy-start(bf16[1,128,1024]{2,1,0:T(8,128)(2,1)} %param.18) | copy-start | bytes 786436
  7.2 38.5 %copy-start.13 = (s32[1,16]{1,0:T(1,128)S(1)}, s32[1,16]{1,0:T(1,128)}, u32[]{:S(2)}) copy-start(s32[1,16]{1,0:T(1,128)} %param.23) | copy-start | bytes 196
  7.2 38.5 %copy-start.12 = (s32[1,16]{1,0:T(1,128)S(1)}, s32[1,16]{1,0:T(1,128)}, u32[]{:S(2)}) copy-start(s32[1,16]{1,0:T(1,128)} %param.22) | copy-start | bytes 196
  9.1 11.6 %all-to-all-start.2 = ((bf16[128,8,128]{2,0,1:T(8,128)(2,1)}), bf16[128,8,128]{2,0,1:T(8,128)(2,1)S(1)}, u32[]{:S(2)}, u32[]{:S(2)}) async-start(bf16[128,8,128]{2,0,1:T(8,128)(2,1)} %copy.118), calls=%async_computation.2 | async-start | bytes 524288 | tf_op jit(solution)/shard_map/all_to_all | solution.py:38
  20.8 34.3 %copy-start.7 = (bf16[128,8,128]{2,0,1:T(8,128)(2,1)}, bf16[128,8,128]{2,0,1:T(8,128)(2,1)S(1)}, u32[]{:S(2)}) copy-start(bf16[128,8,128]{2,0,1:T(8,128)(2,1)S(1)} %all-to-all-done.2) | copy-start | bytes 786436
  20.8 20.2 %all-to-all-start = ((bf16[128,32,128]{0,2,1:T(8,128)(2,1)}), bf16[128,32,128]{0,2,1:T(8,128)(2,1)}, u32[]{:S(2)}, u32[]{:S(2)}) async-start(bf16[128,32,128]{0,2,1:T(8,128)(2,1)} %bitcast.336), calls=%async_computation | async-start | bytes 2097152 | tf_op jit(solution)/shard_map/all_to_all | solution.py:36
  26.3 69.7 %all-gather.3.cloned.1.call-start = ((), (), s32[]{:S(2)}) async-start(), calls=%async_computation.10 | async-start | bytes 4718592 | tf_op jit(solution)/shard_map/all_gather | solution.py:119
  40.9 14.1 %all-to-all-start.1 = ((bf16[128,8,128]{2,0,1:T(8,128)(2,1)}), bf16[128,8,128]{2,0,1:T(8,128)(2,1)S(1)}, u32[]{:S(2)}, u32[]{:S(2)}) async-start(bf16[128,8,128]{2,0,1:T(8,128)(2,1)} %copy.117), calls=%async_computation.1 | async-start | bytes 524288 | tf_op jit(solution)/shard_map/all_to_all | solution.py:37
  45.7 152.6 %reduce-scatter.3.cloned.1.call-start = ((), (), s32[]{:S(2)}) async-start(), calls=%async_computation.8 | async-start | bytes 4718592 | tf_op jit(solution)/shard_map/reduce_scatter | solution.py:111
  88.2 1.0 copy-start.10
  93.5 1.2 copy-start.9
  93.5 268.8 %reduce-scatter.5.cloned.1.call-start = ((), (), s32[]{:S(2)}) async-start(), calls=%async_computation.9 | async-start | bytes 4325376 | tf_op jit(solution)/shard_map/reduce_scatter | solution.py:206
  115.7 1.3 copy-start.5
  117.0 1.0 copy-start.8
  117.9 2.0 copy-start.6
  118.0 1.2 copy-start.3
  118.0 2.0 copy-start.1
  119.9 0.8 copy-start.4
  120.7 1.1 copy-start.2
  122.1 1.3 copy-start.5
  123.4 1.0 copy-start.8
  124.4 2.0 copy-start.6
  124.4 1.2 copy-start.3
  124.4 2.0 copy-start.1
  126.3 0.8 copy-start.4
  127.1 1.1 copy-start.2
  135.1 1.3 copy-start.5
  136.4 1.0 copy-start.8
  137.3 1.9 copy-start.6
  137.3 1.2 copy-start.3
  137.3 2.0 copy-start.1
  139.3 0.8 copy-start.4
  140.1 1.1 copy-start.2
  141.5 1.3 copy-start.5
  142.8 1.0 copy-start.8
  143.8 1.9 copy-start.6
  143.8 1.2 copy-start.3
  143.8 2.0 copy-start.1
  145.7 0.8 copy-start.4
  146.5 1.1 copy-start.2
  153.4 10.9 %all-to-all-start.5 = ((bf16[8,2,8192]{2,1,0:T(2,128)(2,1)}), bf16[8,2,8192]{2,1,0:T(2,128)(2,1)S(1)}, u32[]{:S(2)}, u32[]{:S(2)}) async-start(bf16[8,2,8192]{2,1,0:T(2,128)(2,1)} %reshape.272), calls=%async_computation.6 | async-start | bytes 524288 | tf_op jit(solution)/shard_map/all_to_all | solution.py:204
  174.8 19.4 %all-to-all-start.3 = ((bf16[1024,4,128]{2,1,0:T(4,128)(2,1)}), bf16[1024,4,128]{2,1,0:T(4,128)(2,1)S(1)}, u32[]{:S(2)}, u32[]{:S(2)}) async-start(bf16[1024,4,128]{2,1,0:T(4,128)(2,1)} %bitcast.337), calls=%async_computation.4 | async-start | bytes 2097152 | tf_op jit(solution)/shard_map/all_to_all | solution.py:202
Sparse Core Ops, SparseCore 0:
  29.0 38.5 all-gather.2
  93.7 38.1 reduce-scatter.2
  136.4 225.9 reduce-scatter.4
where the time goes:
time: 371 us; the launch traced here: 369 us
  waiting for transfers between devices  196 us (53%)
  local copies, waits for them, and re-layouts  50.3 us (14%)
  matrix products  49.1 us (13%)
  starting transfers between devices  25.8 us (7%)
  other arithmetic  20.8 us (6%)
  between operations  13.9 us (4%)
  blocking collectives  10.5 us (3%)
    reduce_scatter x1, waiting for transfers between devices, local(): lax.psum_scatter(wo_grad, 'dp', scatter_dimension=1, tiled=True)  164 us
    unnamed x25, local copies, waits for them, and re-layouts  14.8 us
    all_to_all x1, waiting for transfers between devices, local(): lax.all_to_all(q_tok, 'seq', split_axis=1, concat_axis=0, tiled=True)  13.1 us
    dot_general x4, matrix products, weigh(): jnp.einsum('kgqs,skd->qkgd', half_probability, v_tile, preferred_element_...  12.9 us
    all_to_all x1, blocking collectives, local(): lax.all_to_all(dk_acc.astype(jnp.bfloat16), 'seq', split_axis=0, concat_a...  10.5 us
    dot_general x8, matrix products, score_tile(): jnp.einsum('qkgd,skd->kgqs', q_blk, k_tile, preferred_element_type=jnp.fl...  8.71 us
    while x60, local copies, waits for them, and re-layouts  8.15 us
  transfers between devices with their start and end apart: 8, of which 6 were waited for; matrix products, arithmetic and copies ran while one was open for 29% of the time, Pallas kernels for 0%

commit v1 on v0

--- a/solution.py
+++ b/solution.py
@@ -1,11 +1,12 @@
 import jax
 import jax.numpy as jnp
 from jax import lax
-from jax.sharding import PartitionSpec as P
+from jax.sharding import Mesh, PartitionSpec as P
 
 QUERY_HEADS = 32
 KEY_VALUE_HEADS = 8
 HEAD_SIZE = 128
+DP = ("dpy", "dpz")
 
 
 def row_starts(lengths, pack_order, win_rows):
@@ -108,14 +109,10 @@
     grad_rows = out_grad.reshape(row_total_count, out_grad.shape[2])
     a_rows = a_head
     product = jnp.dot(a_rows, out_weight, preferred_element_type=jnp.float32)
-    y_out = lax.psum_scatter(
-        lax.optimization_barrier(product.astype(jnp.bfloat16))
-        .astype(jnp.float32)
-        .astype(jnp.bfloat16),
-        "seq",
-        scatter_dimension=0,
-        tiled=True,
-    )
+    seq_count = lax.psum(1, "seq")
+    pieces = product.astype(jnp.bfloat16).reshape(seq_count, win_rows // seq_count, product.shape[1])
+    pieces = lax.all_to_all(pieces, "seq", split_axis=0, concat_axis=0, tiled=True)
+    y_out = jnp.sum(pieces.astype(jnp.float32), axis=0).astype(jnp.bfloat16)
     incoming = lax.all_gather(grad_rows, "seq", axis=0, tiled=True)
     a_rows = a_head
     wo_grad = lax.dot_general(
@@ -203,7 +200,16 @@
         lax.all_to_all(dk_acc.astype(jnp.bfloat16), "seq", split_axis=0, concat_axis=1, tiled=True),
         lax.all_to_all(dv_acc.astype(jnp.bfloat16), "seq", split_axis=0, concat_axis=1, tiled=True),
     )
-    weight_grad = lax.psum_scatter(wo_grad, "dp", scatter_dimension=1, tiled=True)
+    y_count = lax.psum(1, "dpy")
+    z_count = lax.psum(1, "dpz")
+    cols = wo_grad.shape[1]
+    wo_perm = (
+        wo_grad.reshape(wo_grad.shape[0], y_count, z_count, cols // (y_count * z_count))
+        .transpose(0, 2, 1, 3)
+        .reshape(wo_grad.shape[0], cols)
+    )
+    wo_perm = lax.psum_scatter(wo_perm, "dpz", scatter_dimension=1, tiled=True)
+    weight_grad = lax.psum_scatter(wo_perm, "dpy", scatter_dimension=1, tiled=True)
     return (
         y_out.reshape(1, row_total_count, y_out.shape[1]),
         d_q.reshape(1, row_total_count, QUERY_HEADS * HEAD_SIZE),
@@ -214,20 +220,25 @@
 
 
 def solution(mesh):
+    dp_count = mesh.shape["dp"]
+    y_count = 4 if dp_count % 4 == 0 else 1
+    mesh = Mesh(
+        mesh.devices.reshape(mesh.shape["seq"], y_count, dp_count // y_count), ("seq", "dpy", "dpz")
+    )
     in_specs = (
-        P("dp", "seq", None),
-        P("dp", "seq", None),
-        P("dp", "seq", None),
+        P(DP, "seq", None),
+        P(DP, "seq", None),
+        P(DP, "seq", None),
         P("seq", None),
-        P("dp", "seq", None),
-        P("dp", None),
-        P("dp", None),
+        P(DP, "seq", None),
+        P(DP, None),
+        P(DP, None),
     )
     out_specs = (
-        P("dp", "seq", None),
-        P("dp", "seq", None),
-        P("dp", "seq", None),
-        P("dp", "seq", None),
-        P("seq", "dp"),
+        P(DP, "seq", None),
+        P(DP, "seq", None),
+        P(DP, "seq", None),
+        P(DP, "seq", None),
+        P("seq", DP),
     )
     return jax.shard_map(local, mesh=mesh, in_specs=in_specs, out_specs=out_specs, check_vma=False)

time: 371 us -> 210 us (0.57)
  waiting for transfers between devices: 196 us -> 35 us
  blocking collectives: 10.5 us -> 0 us
  starting transfers between devices: 25.8 us -> 36.3 us
    reduce_scatter x2, waiting for transfers between devices: 164 us -> 4.14 us  [the longest x1 3.98 us: local(): wo_perm = lax.psum_scatter(wo_perm, 'dpz', scatter_dimension=1, tiled=True)]
    all_to_all x0 -> x2, starting transfers between devices: none -> 10.6 us  [the longest x1 5.86 us: local(): lax.all_to_all(pieces, 'seq', split_axis=0, concat_axis=0, tiled=True)]
    all_to_all x1 -> x0, blocking collectives: 10.5 us -> none  [local(): lax.all_to_all(dk_acc.astype(jnp.bfloat16), 'seq', split_axis=0, concat_a...]
    while x60 -> x12, local copies, waits for them, and re-layouts: 8.15 us -> 0.86 us
    dot_general x0 -> x1, local copies, waits for them, and re-layouts: none -> 6.49 us  [local(): lax.dot_general(a_rows, incoming, (((0,), (0,)), ((), ())), preferred_ele...]
    reduce_sum x0 -> x1, other arithmetic: none -> 3.85 us  [local(): y_out = jnp.sum(pieces.astype(jnp.float32), axis=0).astype(jnp.bfloat16)]
    all_to_all x1, waiting for transfers between devices: 4.18 us -> 0.39 us  [local(): lax.all_to_all(d_q, 'seq', split_axis=0, concat_axis=1, tiled=True)]
    unnamed x25 -> x27, local copies, waits for them, and re-layouts: 14.8 us -> 14.3 us
  transfers between devices with their start and end apart: 8 -> 10, of which waited for: 6 -> 8; matrix products, arithmetic and copies ran while one was open for 29% -> 56% of each run, Pallas kernels for 0% -> 0%
where the time goes in v1:
time: 210 us; the launch traced here: 207 us
  local copies, waits for them, and re-layouts  52.2 us (25%)
  matrix products  46.8 us (22%)
  starting transfers between devices  36.3 us (17%)
  waiting for transfers between devices  35 us (17%)
  other arithmetic  20.1 us (10%)
  between operations  13.9 us (7%)
  loops' own time  2.23 us (1%)
    unnamed x27, local copies, waits for them, and re-layouts  14.3 us
    all_to_all x1, waiting for transfers between devices, local(): lax.all_to_all(q_tok, 'seq', split_axis=1, concat_axis=0, tiled=True)  13.1 us
    dot_general x4, matrix products, weigh(): jnp.einsum('kgqs,skd->qkgd', half_probability, v_tile, preferred_element_...  12.9 us
    dot_general x8, matrix products, score_tile(): jnp.einsum('qkgd,skd->kgqs', q_blk, k_tile, preferred_element_type=jnp.fl...  8.71 us
    dot_general x1, local copies, waits for them, and re-layouts, local(): lax.dot_general(a_rows, incoming, (((0,), (0,)), ((), ())), preferred_ele...  6.49 us
    all_to_all x1, waiting for transfers between devices, local(): lax.all_to_all(key_token_rows, 'seq', split_axis=1, concat_axis=0, tiled=...  6.37 us
    all_to_all x1, starting transfers between devices, local(): lax.all_to_all(pieces, 'seq', split_axis=0, concat_axis=0, tiled=True)  5.86 us
    all_to_all x1, starting transfers between devices, local(): lax.all_to_all(value_token_rows, 'seq', split_axis=1, concat_axis=0, tile...  5.56 us
  transfers between devices with their start and end apart: 10, of which 8 were waited for; matrix products, arithmetic and copies ran while one was open for 56% of the time, Pallas kernels for 0%

profile of v1, /device:TPU:2, one launch (start us, length us, event | category | flops | bytes accessed | tf_op | source)
XLA Modules:
  0.0 206.6 jit_solution(18307915032052229890)
XLA Ops:
  9.1 5.6 %all-to-all-start.2 = ((bf16[128,8,128]{2,0,1:T(8,128)(2,1)}), bf16[128,8,128]{2,0,1:T(8,128)(2,1)S(1)}, u32[]{:S(2)}, u32[]{:S(2)}) async-start(bf16[128,8,128]{2,0,1:T(8,128)(2,1)} %copy.129), calls=%async_computation.2 | async-start | bytes 524288 | tf_op jit(solution)/shard_map/all_to_all | solution.py:39
  14.7 2.3 %copy.124 = bf16[1,128,4096]{1,2,0:T(8,128)(2,1)} copy(bf16[1,128,4096]{2,1,0:T(8,128)(2,1)} %param.17) | data formatting | bytes 2097152 | tf_op args[0]
  16.9 3.8 %all-to-all-done.2 = bf16[128,8,128]{2,0,1:T(8,128)(2,1)S(1)} async-done(((bf16[128,8,128]{2,0,1:T(8,128)(2,1)}), bf16[128,8,128]{2,0,1:T(8,128)(2,1)S(1)}, u32[]{:S(2)}, u32[]{:S(2)}) %all-to-all-start.2) | async-done | bytes 262176 | tf_op jit(solution)/shard_map/all_to_all | solution.py:39
  20.8 5.6 %all-to-all-start = ((bf16[128,32,128]{0,2,1:T(8,128)(2,1)}), bf16[128,32,128]{0,2,1:T(8,128)(2,1)}, u32[]{:S(2)}, u32[]{:S(2)}) async-start(bf16[128,32,128]{0,2,1:T(8,128)(2,1)} %bitcast.348), calls=%async_computation | async-start | bytes 2097152 | tf_op jit(solution)/shard_map/all_to_all | solution.py:37
  27.9 13.1 %all-to-all-done = bf16[128,32,128]{0,2,1:T(8,128)(2,1)} async-done(((bf16[128,32,128]{0,2,1:T(8,128)(2,1)}), bf16[128,32,128]{0,2,1:T(8,128)(2,1)}, u32[]{:S(2)}, u32[]{:S(2)}) %all-to-all-start) | async-done | bytes 1048608 | tf_op jit(solution)/shard_map/all_to_all | solution.py:37
  40.9 4.8 %all-to-all-start.1 = ((bf16[128,8,128]{2,0,1:T(8,128)(2,1)}), bf16[128,8,128]{2,0,1:T(8,128)(2,1)S(1)}, u32[]{:S(2)}, u32[]{:S(2)}) async-start(bf16[128,8,128]{2,0,1:T(8,128)(2,1)} %copy.128), calls=%async_computation.1 | async-start | bytes 524288 | tf_op jit(solution)/shard_map/all_to_all | solution.py:38
  46.4 2.3 %copy.126 = bf16[8,128,4,128]{3,1,0,2:T(8,128)(2,1)} copy(bf16[8,128,4,128]{1,3,2,0:T(8,128)(2,1)} %bitcast.12) | data formatting | bytes 2097152 | tf_op jit(solution)/shard_map/all_to_all | solution.py:37
  48.7 6.4 %all-to-all-done.1 = bf16[128,8,128]{2,0,1:T(8,128)(2,1)S(1)} async-done(((bf16[128,8,128]{2,0,1:T(8,128)(2,1)}), bf16[128,8,128]{2,0,1:T(8,128)(2,1)S(1)}, u32[]{:S(2)}, u32[]{:S(2)}) %all-to-all-start.1) | async-done | bytes 262176 | tf_op jit(solution)/shard_map/all_to_all | solution.py:38
  55.0 32.0 %while.94 = (s32[]{:T(128)}, bf16[2,512,1,4,128]{1,4,3,2,0:T(8,128)(2,1)}, f32[2,1,4,512,1]{3,2,4,1,0:T(4,128)S(1)}, f32[2,1,4,512,1]{3,2,4,1,0:T(4,128)S(1)}, s...) while((s32[]{:T(128)}, ...), condition=%wide.region_10.11_spmd, body=%wide.region_3.10_spmd.sunk | while | flops 820260864 | bytes 16042333 | solution.py:106
  57.6 4.3 %while.97 = (s32[]{:T(128)}, f32[1,4,512,1]{2,1,3,0:T(4,128)S(1)}, f32[1,4,512,1]{2,1,3,0:T(4,128)S(1)}, s32[512]{0:T(512)S(1)}, s32[]{:T(128)}, /*index=5*/bf16...) while((s32[]{:T(128)}, f32[1,4,512,1]{2,1,3,0:T(4,128)S(1)}, ...), condition=%wide.region_7.7_spmd.clone, body=%wide.region_4.6_spmd.clone.sunk | while | flops 276573184 | bytes 9947322 | solution.py:80
  61.9 7.1 %while.98 = (s32[]{:T(128)}, f32[512,1,4,128]{0,3,2,1:T(8,128)}, bf16[1024,1,128]{0,2,1:T(8,128)(2,1)S(1)}, s32[512]{0:T(512)S(1)}, s32[]{:T(128)}, /*index=5*/b...) while((s32[]{:T(128)}, f32[512,1,4,128]{0,3,2,1:T(8,128)}, ...), condition=%wide.region_9.9_spmd.clone, body=%wide.region_8.8_spmd.clone.sunk | while | flops 543425536 | bytes 3436228 | solution.py:98
  62.2 2.6 %fusion.137 = f32[512,1,4,128]{0,3,2,1:T(8,128)} fusion(f32[4,512]{1,0:T(4,128)S(1)} %bitcast.343, f32[4,512]{1,0:T(4,128)S(1)} %bitcast.338, pred[512,512]{0,1:T(8,128)(4,1)S(1)} %compare_and_fusion.8, f32[512,1,4,128]{0,3,2,1:T(8,128)} %get-tuple-element.1481, bf16[512,1,4,128]{3,0,2,1:T(8,128)(2,1)S(1)} %get-tuple-element.1499, ...), kind=kOutput, calls=%fused_computation.25.clone.1 | convolution fusion | flops 542638080 | bytes 3163648 | tf_op jit(solution)/shard_map/while/body/eval_jaxpr/while/body/kgqs,skd->qkgd/dot_general | solution.py:94
  65.1 3.9 %fusion.137 = f32[512,1,4,128]{0,3,2,1:T(8,128)} fusion(f32[4,512]{1,0:T(4,128)S(1)} %bitcast.343, f32[4,512]{1,0:T(4,128)S(1)} %bitcast.338, pred[512,512]{0,1:T(8,128)(4,1)S(1)} %compare_and_fusion.8, f32[512,1,4,128]{0,3,2,1:T(8,128)} %get-tuple-element.1481, bf16[512,1,4,128]{3,0,2,1:T(8,128)(2,1)S(1)} %get-tuple-element.1499, ...), kind=kOutput, calls=%fused_computation.25.clone.1 | convolution fusion | flops 542638080 | bytes 3163648 | tf_op jit(solution)/shard_map/while/body/eval_jaxpr/while/body/kgqs,skd->qkgd/dot_general | solution.py:94
  69.0 2.1 %bitcast_dynamic-update-slice_fusion.5 = bf16[2,512,1,4,128]{1,4,3,2,0:T(8,128)(2,1)} fusion(bf16[2,512,1,4,128]{1,4,3,2,0:T(8,128)(2,1)} %get-tuple-element.1528, s32[]{:T(128)S(6)} %copy.206, f32[512,1,4,128]{0,3,2,1:T(8,128)} %get-tuple-element.1324), kind=kLoop, calls=%fused_computation.37.clone.1 | loop fusion | flops 262144 | bytes 1572868 | tf_op jit(solution)/shard_map/while/body/jit(dynamic_update_index_in_dim)/dynamic_update_slice | solution.py:106
  73.6 4.3 %while.97 = (s32[]{:T(128)}, f32[1,4,512,1]{2,1,3,0:T(4,128)S(1)}, f32[1,4,512,1]{2,1,3,0:T(4,128)S(1)}, s32[512]{0:T(512)S(1)}, s32[]{:T(128)}, /*index=5*/bf16...) while((s32[]{:T(128)}, f32[1,4,512,1]{2,1,3,0:T(4,128)S(1)}, ...), condition=%wide.region_7.7_spmd.clone, body=%wide.region_4.6_spmd.clone.sunk | while | flops 276573184 | bytes 9947322 | solution.py:80
  77.9 7.0 %while.98 = (s32[]{:T(128)}, f32[512,1,4,128]{0,3,2,1:T(8,128)}, bf16[1024,1,128]{0,2,1:T(8,128)(2,1)S(1)}, s32[512]{0:T(512)S(1)}, s32[]{:T(128)}, /*index=5*/b...) while((s32[]{:T(128)}, f32[512,1,4,128]{0,3,2,1:T(8,128)}, ...), condition=%wide.region_9.9_spmd.clone, body=%wide.region_8.8_spmd.clone.sunk | while | flops 543425536 | bytes 3436228 | solution.py:98
  78.2 2.6 %fusion.137 = f32[512,1,4,128]{0,3,2,1:T(8,128)} fusion(f32[4,512]{1,0:T(4,128)S(1)} %bitcast.343, f32[4,512]{1,0:T(4,128)S(1)} %bitcast.338, pred[512,512]{0,1:T(8,128)(4,1)S(1)} %compare_and_fusion.8, f32[512,1,4,128]{0,3,2,1:T(8,128)} %get-tuple-element.1481, bf16[512,1,4,128]{3,0,2,1:T(8,128)(2,1)S(1)} %get-tuple-element.1499, ...), kind=kOutput, calls=%fused_computation.25.clone.1 | convolution fusion | flops 542638080 | bytes 3163648 | tf_op jit(solution)/shard_map/while/body/eval_jaxpr/while/body/kgqs,skd->qkgd/dot_general | solution.py:94
  81.1 3.8 %fusion.137 = f32[512,1,4,128]{0,3,2,1:T(8,128)} fusion(f32[4,512]{1,0:T(4,128)S(1)} %bitcast.343, f32[4,512]{1,0:T(4,128)S(1)} %bitcast.338, pred[512,512]{0,1:T(8,128)(4,1)S(1)} %compare_and_fusion.8, f32[512,1,4,128]{0,3,2,1:T(8,128)} %get-tuple-element.1481, bf16[512,1,4,128]{3,0,2,1:T(8,128)(2,1)S(1)} %get-tuple-element.1499, ...), kind=kOutput, calls=%fused_computation.25.clone.1 | convolution fusion | flops 542638080 | bytes 3163648 | tf_op jit(solution)/shard_map/while/body/eval_jaxpr/while/body/kgqs,skd->qkgd/dot_general | solution.py:94
  84.9 2.1 %bitcast_dynamic-update-slice_fusion.5 = bf16[2,512,1,4,128]{1,4,3,2,0:T(8,128)(2,1)} fusion(bf16[2,512,1,4,128]{1,4,3,2,0:T(8,128)(2,1)} %get-tuple-element.1528, s32[]{:T(128)S(6)} %copy.206, f32[512,1,4,128]{0,3,2,1:T(8,128)} %get-tuple-element.1324), kind=kLoop, calls=%fused_computation.37.clone.1 | loop fusion | flops 262144 | bytes 1572868 | tf_op jit(solution)/shard_map/while/body/jit(dynamic_update_index_in_dim)/dynamic_update_slice | solution.py:106
  87.0 1.7 copy.131
  88.7 2.3 %copy.132 = bf16[2,512,1,4,128]{4,1,0,3,2:T(8,128)(2,1)} copy(bf16[2,512,1,4,128]{1,4,3,2,0:T(8,128)(2,1)} %get-tuple-element.611) | data formatting | bytes 2097152 | tf_op jit(solution)/shard_map/while | solution.py:106
  92.2 4.3 %convolution_convert_fusion = bf16[1024,2048]{1,0:T(8,128)(2,1)} fusion(bf16[512,2048]{1,0:T(8,128)(2,1)S(1)} %copy-done, bf16[128,8,4,128]{3,2,1,0:T(4,128)(2,1)S(1)} %bitcast.349), kind=kOutput, calls=%fused_computation.88 | convolution fusion | flops 2149580800 | bytes 7340032 | tf_op jit(solution)/shard_map/dot_general | solution.py:111
  96.5 5.9 %all-to-all-start.3 = ((bf16[8,128,2048]{2,1,0:T(8,128)(2,1)}), bf16[8,128,2048]{2,1,0:T(8,128)(2,1)}, u32[]{:S(2)}, u32[]{:S(2)}) async-start(bf16[8,128,2048]{2,1,0:T(8,128)(2,1)} %bitcast.345), calls=%async_computation.3 | async-start | bytes 8388608 | tf_op jit(solution)/shard_map/all_to_all | solution.py:114
  102.4 6.5 %copy.140 = bf16[2048,1024]{1,0:T(8,128)(2,1)} copy(bf16[2048,1024]{0,1:T(8,128)(2,1)} %bitcast.344) | data formatting | bytes 8388608 | tf_op jit(solution)/shard_map/dot_general | solution.py:118
  108.9 4.5 %convolution_bitcast_fusion = f32[512,8,4,64]{0,3,1,2:T(8,128)S(1)} fusion(bf16[4,8,64,1024]{3,2,1,0:T(8,128)(2,1)} %bitcast.346, bf16[1024,512,1,1]{1,0,2,3:T(8,128)(2,1)S(1)} %copy-done.5), kind=kOutput, calls=%fused_computation.89 | convolution fusion | flops 2147483648 | bytes 9437184 | tf_op jit(solution)/shard_map/dot_general | solution.py:118
  113.4 2.7 %copy.141 = f32[512,8,4,64]{0,3,2,1:T(8,128)} copy(f32[512,8,4,64]{0,3,1,2:T(8,128)S(1)} %convolution_bitcast_fusion) | data formatting | bytes 8388608 | tf_op jit(solution)/shard_map/transpose | solution.py:208
  116.1 5.5 %fusion.85 = bf16[1024,512]{0,1:T(8,128)(2,1)} fusion(bf16[512,2048]{1,0:T(8,128)(2,1)S(1)} %copy-done, bf16[1,1024,2048]{2,1,0:T(8,128)(2,1)} %all-gather.3.cloned.1.call-done), kind=kOutput, calls=%fused_computation.90 | convolution fusion | flops 2148007936 | bytes 7340032 | tf_op jit(solution)/shard_map/dot_general | solution.py:121
  123.0 29.0 %while.96 = (s32[]{:T(128)}, bf16[1024,1,4,128]{3,2,0,1:T(4,128)(2,1)}, f32[1024,1,128]{2,0,1:T(8,128)S(1)}, f32[1024,1,128]{2,0,1:T(8,128)S(1)}, bf16[1024,1,4,...) while((s32[]{:T(128)}, ...), condition=%wide.region_16.17_spmd, body=%wide.region_12.16_spmd.sunk | while | flops 1354365952 | bytes 34028200 | solution.py:187
  124.4 1.4 multiply_reduce_fusion.2
  126.9 9.2 %while.99 = (s32[]{:T(128)}, f32[512,1,4,128]{0,3,2,1:T(8,128)S(1)}, f32[1024,1,128]{2,0,1:T(8,128)S(1)}, f32[1024,1,128]{2,0,1:T(8,128)S(1)}, bf16[1024,1,128]{...) while((s32[]{:T(128)}, ...), condition=%wide.region_15.15_spmd.clone, body=%wide.region_14.14_spmd.clone.sunk | while | flops 1353057280 | bytes 26118420 | solution.py:174
  127.2 1.3 fusion.126
  131.8 1.3 fusion.126
  138.9 1.4 multiply_reduce_fusion.2
  141.4 9.2 %while.99 = (s32[]{:T(128)}, f32[512,1,4,128]{0,3,2,1:T(8,128)S(1)}, f32[1024,1,128]{2,0,1:T(8,128)S(1)}, f32[1024,1,128]{2,0,1:T(8,128)S(1)}, bf16[1024,1,128]{...) while((s32[]{:T(128)}, ...), condition=%wide.region_15.15_spmd.clone, body=%wide.region_14.14_spmd.clone.sunk | while | flops 1353057280 | bytes 26118420 | solution.py:174
  141.7 1.3 fusion.126
  146.3 1.3 fusion.126
  154.1 4.8 %all-to-all-start.6 = ((bf16[8,2,8192]{2,1,0:T(2,128)(2,1)}), bf16[8,2,8192]{2,1,0:T(2,128)(2,1)S(1)}, u32[]{:S(2)}, u32[]{:S(2)}) async-start(bf16[8,2,8192]{2,1,0:T(2,128)(2,1)} %reshape.284), calls=%async_computation.6 | async-start | bytes 524288 | tf_op jit(solution)/shard_map/all_to_all | solution.py:201
  160.5 4.4 %all-to-all-done.6 = bf16[8,2,8192]{2,1,0:T(2,128)(2,1)S(1)} async-done(((bf16[8,2,8192]{2,1,0:T(2,128)(2,1)}), bf16[8,2,8192]{2,1,0:T(2,128)(2,1)S(1)}, u32[]{:S(2)}, u32[]{:S(2)}) %all-to-all-start.6) | async-done | bytes 262176 | tf_op jit(solution)/shard_map/all_to_all | solution.py:201
  165.0 4.8 %all-to-all-start.5 = ((bf16[8,2,8192]{2,1,0:T(2,128)(2,1)}), bf16[8,2,8192]{2,1,0:T(2,128)(2,1)S(1)}, u32[]{:S(2)}, u32[]{:S(2)}) async-start(bf16[8,2,8192]{2,1,0:T(2,128)(2,1)} %reshape.282), calls=%async_computation.5 | async-start | bytes 524288 | tf_op jit(solution)/shard_map/all_to_all | solution.py:200
  169.8 4.0 %reduce-scatter.3.cloned.1.call-done = f32[512,256]{0,1:T(8,128)} async-done(((f32[512,2048]{0,1:T(8,128)}), f32[512,256]{0,1:T(8,128)}) %reduce-scatter.3.cloned.1.call-update) | async-done | bytes 524304 | tf_op jit(solution)/shard_map/reduce_scatter | solution.py:211
  173.8 2.1 %all-to-all-done.5 = bf16[8,2,8192]{2,1,0:T(2,128)(2,1)S(1)} async-done(((bf16[8,2,8192]{2,1,0:T(2,128)(2,1)}), bf16[8,2,8192]{2,1,0:T(2,128)(2,1)S(1)}, u32[]{:S(2)}, u32[]{:S(2)}) %all-to-all-start.5) | async-done | bytes 262176 | tf_op jit(solution)/shard_map/all_to_all | solution.py:200
  176.5 4.9 %all-to-all-start.4 = ((bf16[1024,4,128]{2,1,0:T(4,128)(2,1)}), bf16[1024,4,128]{2,1,0:T(4,128)(2,1)S(1)}, u32[]{:S(2)}, u32[]{:S(2)}) async-start(bf16[1024,4,128]{2,1,0:T(4,128)(2,1)} %bitcast.32), calls=%async_computation.4 | async-start | bytes 2097152 | tf_op jit(solution)/shard_map/all_to_all | solution.py:199
  181.5 3.8 %reduce_sum.54 = bf16[128,2048]{1,0:T(8,128)(2,1)} reduce(bf16[8,128,2048]{2,1,0:T(8,128)(2,1)} %all-to-all-done.3, bf16[]{:T(256)} %constant.174.clone.1), dimensions={0}, to_apply=%region_11.12 | reduce | flops 1835008 | bytes 4718594 | tf_op jit(solution)/shard_map/reduce_sum | solution.py:115
  188.2 1.8 copy.143
  190.0 1.9 reshape.283
  193.8 1.8 copy.142
  196.0 1.3 copy.135
  197.3 2.6 %reshape.254 = bf16[1,128,4096]{2,1,0:T(8,128)(2,1)} reshape(bf16[128,8,4,128]{3,2,1,0:T(4,128)(2,1)} %copy.135) | data formatting | bytes 2097152 | tf_op jit(solution)/shard_map/reshape | solution.py:215
  (156 shorter events, 50.1 us)
Async XLA Ops:
  7.2 85.0 %copy-start = (bf16[512,2048]{1,0:T(8,128)(2,1)S(1)}, bf16[512,2048]{1,0:T(8,128)(2,1)}, u32[]{:S(2)}) copy-start(bf16[512,2048]{1,0:T(8,128)(2,1)} %param.20) | copy-start | bytes 6291460
  7.2 19.9 %copy-start.6 = (bf16[1,128,1024]{2,1,0:T(8,128)(2,1)S(1)}, bf16[1,128,1024]{2,1,0:T(8,128)(2,1)}, u32[]{:S(2)}) copy-start(bf16[1,128,1024]{2,1,0:T(8,128)(2,1)} %param.18) | copy-start | bytes 786436
  7.2 38.5 %copy-start.8 = (s32[1,16]{1,0:T(1,128)S(1)}, s32[1,16]{1,0:T(1,128)}, u32[]{:S(2)}) copy-start(s32[1,16]{1,0:T(1,128)} %param.23) | copy-start | bytes 196
  7.2 38.5 %copy-start.7 = (s32[1,16]{1,0:T(1,128)S(1)}, s32[1,16]{1,0:T(1,128)}, u32[]{:S(2)}) copy-start(s32[1,16]{1,0:T(1,128)} %param.22) | copy-start | bytes 196
  9.1 11.6 %all-to-all-start.2 = ((bf16[128,8,128]{2,0,1:T(8,128)(2,1)}), bf16[128,8,128]{2,0,1:T(8,128)(2,1)S(1)}, u32[]{:S(2)}, u32[]{:S(2)}) async-start(bf16[128,8,128]{2,0,1:T(8,128)(2,1)} %copy.129), calls=%async_computation.2 | async-start | bytes 524288 | tf_op jit(solution)/shard_map/all_to_all | solution.py:39
  20.8 34.3 %copy-start.2 = (bf16[128,8,128]{2,0,1:T(8,128)(2,1)}, bf16[128,8,128]{2,0,1:T(8,128)(2,1)S(1)}, u32[]{:S(2)}) copy-start(bf16[128,8,128]{2,0,1:T(8,128)(2,1)S(1)} %all-to-all-done.2) | copy-start | bytes 786436
  20.8 20.2 %all-to-all-start = ((bf16[128,32,128]{0,2,1:T(8,128)(2,1)}), bf16[128,32,128]{0,2,1:T(8,128)(2,1)}, u32[]{:S(2)}, u32[]{:S(2)}) async-start(bf16[128,32,128]{0,2,1:T(8,128)(2,1)} %bitcast.348), calls=%async_computation | async-start | bytes 2097152 | tf_op jit(solution)/shard_map/all_to_all | solution.py:37
  26.3 76.1 %all-gather.3.cloned.1.call-start = ((), (), s32[]{:S(2)}) async-start(), calls=%async_computation.11 | async-start | bytes 4718592 | tf_op jit(solution)/shard_map/all_gather | solution.py:116
  40.9 14.1 %all-to-all-start.1 = ((bf16[128,8,128]{2,0,1:T(8,128)(2,1)}), bf16[128,8,128]{2,0,1:T(8,128)(2,1)S(1)}, u32[]{:S(2)}, u32[]{:S(2)}) async-start(bf16[128,8,128]{2,0,1:T(8,128)(2,1)} %copy.128), calls=%async_computation.1 | async-start | bytes 524288 | tf_op jit(solution)/shard_map/all_to_all | solution.py:38
  96.5 57.6 %all-to-all-start.3 = ((bf16[8,128,2048]{2,1,0:T(8,128)(2,1)}), bf16[8,128,2048]{2,1,0:T(8,128)(2,1)}, u32[]{:S(2)}, u32[]{:S(2)}) async-start(bf16[8,128,2048]{2,1,0:T(8,128)(2,1)} %bitcast.345), calls=%async_computation.3 | async-start | bytes 8388608 | tf_op jit(solution)/shard_map/all_to_all | solution.py:114
  102.4 71.4 %reduce-scatter.3.cloned.1.call-start = ((), (), s32[]{:S(2)}) async-start(), calls=%async_computation.9 | async-start | bytes 4718592 | tf_op jit(solution)/shard_map/reduce_scatter | solution.py:211
  102.4 6.5 %copy-start.5 = (bf16[1024,512,1,1]{1,0,2,3:T(8,128)(2,1)S(1)}, bf16[1024,512,1,1]{1,0,2,3:T(8,128)(2,1)}, u32[]{:S(2)}) copy-start(bf16[1024,512,1,1]{1,0,2,3:T(8,128)(2,1)} %reshape.279) | copy-start | bytes 3145732
  128.5 1.0 copy-start.3
  133.1 1.0 copy-start.3
  143.0 1.0 copy-start.3
  147.6 1.0 copy-start.3
  154.1 10.9 %all-to-all-start.6 = ((bf16[8,2,8192]{2,1,0:T(2,128)(2,1)}), bf16[8,2,8192]{2,1,0:T(2,128)(2,1)S(1)}, u32[]{:S(2)}, u32[]{:S(2)}) async-start(bf16[8,2,8192]{2,1,0:T(2,128)(2,1)} %reshape.284), calls=%async_computation.6 | async-start | bytes 524288 | tf_op jit(solution)/shard_map/all_to_all | solution.py:201
  165.0 10.9 %all-to-all-start.5 = ((bf16[8,2,8192]{2,1,0:T(2,128)(2,1)}), bf16[8,2,8192]{2,1,0:T(2,128)(2,1)S(1)}, u32[]{:S(2)}, u32[]{:S(2)}) async-start(bf16[8,2,8192]{2,1,0:T(2,128)(2,1)} %reshape.282), calls=%async_computation.5 | async-start | bytes 524288 | tf_op jit(solution)/shard_map/all_to_all | solution.py:200
  169.7 30.3 %reduce-scatter.5.cloned.1.call-start = ((), (), s32[]{:S(2)}) async-start(), calls=%async_computation.10 | async-start | bytes 655360 | tf_op jit(solution)/shard_map/reduce_scatter | solution.py:212
  175.8 0.7 copy-start.4
  176.5 19.4 %all-to-all-start.4 = ((bf16[1024,4,128]{2,1,0:T(4,128)(2,1)}), bf16[1024,4,128]{2,1,0:T(4,128)(2,1)S(1)}, u32[]{:S(2)}, u32[]{:S(2)}) async-start(bf16[1024,4,128]{2,1,0:T(4,128)(2,1)} %bitcast.32), calls=%async_computation.4 | async-start | bytes 2097152 | tf_op jit(solution)/shard_map/all_to_all | solution.py:199
  185.3 14.8 %copy-start.1 = (bf16[512,2048]{1,0:T(8,128)(2,1)S(1)}, bf16[512,2048]{1,0:T(8,128)(2,1)}, u32[]{:S(2)}) copy-start(bf16[512,2048]{1,0:T(8,128)(2,1)} %param.20) | copy-start | bytes 6291460
Sparse Core Ops, SparseCore 0:
  29.0 38.5 all-gather.2
  116.2 57.4 reduce-scatter.2
  176.8 23.1 reduce-scatter.4

commit v2 on v1

v2 whole, which is shorter than its diff:
```python
import jax
import jax.numpy as jnp
from jax import lax
from jax.sharding import Mesh, PartitionSpec as P

QUERY_HEADS = 32
KEY_VALUE_HEADS = 8
HEAD_SIZE = 128
DP = ("dpy", "dpz")
BLOCK = 256
MOST = 256


def row_starts(lengths, pack_order, win_rows):
    samples = lengths.shape[0]
    picked = jnp.sum(
        jnp.where(
            pack_order[:, None] == jnp.arange(samples, dtype=jnp.int32)[None, :],
            lengths[None, :],
            0,
        ),
        axis=1,
        dtype=jnp.int32,
    )
    seg_ends = jnp.cumsum(picked, dtype=jnp.int32)
    places = jnp.arange(win_rows, dtype=jnp.int32)
    return jnp.sum(
        jnp.where(seg_ends[None, :] <= places[:, None], picked[None, :], 0), axis=1, dtype=jnp.int32
    )


def local(queries, rotated_key_matrix, value_matrix, out_weight, out_grad, lengths, pack_order):
    seq_count = lax.psum(1, "seq")
    tok = queries.shape[1]
    head_scale = HEAD_SIZE ** (-0.5)
    hq = QUERY_HEADS // seq_count
    hk = KEY_VALUE_HEADS // seq_count
    group_width = hq // hk
    packed = jnp.concatenate(
        [
            queries.reshape(tok, seq_count, hq, HEAD_SIZE),
            rotated_key_matrix.reshape(tok, seq_count, hk, HEAD_SIZE),
            value_matrix.reshape(tok, seq_count, hk, HEAD_SIZE),
        ],
        axis=2,
    ).transpose(1, 0, 2, 3)
    got = lax.all_to_all(packed, "seq", split_axis=0, concat_axis=0, tiled=True)
    win_rows = seq_count * tok
    got = got.reshape(win_rows, hq + 2 * hk, HEAD_SIZE)
    query_head_rows = got[:, :hq].reshape(win_rows, hk, group_width, HEAD_SIZE)
    k_loc = got[:, hq : hq + hk]
    v_loc = got[:, hq + hk :]
    starts = row_starts(lengths[0], pack_order[0], win_rows)
    blk = min(BLOCK, win_rows)
    blk_count = win_rows // blk
    reach = -(-(MOST - 1) // blk)

    def band(i):
        q_start = i * blk
        k_start = max(0, q_start - reach * blk)
        return q_start, k_start, q_start + blk

    def probs(i, q_blk, m=None, l=None):
        q_start, k_start, k_end = band(i)
        k_band = k_loc[k_start:k_end]
        scores = (
            jnp.einsum("qkgd,skd->kgqs", q_blk, k_band, preferred_element_type=jnp.float32)
            * head_scale
        )
        rows_at = q_start + jnp.arange(blk, dtype=jnp.int32)
        cols_at = k_start + jnp.arange(k_end - k_start, dtype=jnp.int32)
        first_at = starts[q_start : q_start + blk]
        visible = (cols_at[None, :] >= first_at[:, None]) & (cols_at[None, :] <= rows_at[:, None])
        if m is None:
            m = jnp.max(jnp.where(visible, scores, -1e30), axis=-1, keepdims=True)
        expd = jnp.where(visible, jnp.exp(scores - m), 0.0)
        if l is None:
            l = jnp.sum(expd, axis=-1, keepdims=True)
        return expd / l, m, l

    out_blocks, stats = [], []
    for i in range(blk_count):
        q_start, k_start, k_end = band(i)
        q_blk = query_head_rows[q_start : q_start + blk]
        attn_prob, m, l = probs(i, q_blk)
        stats.append((m, l))
        out_blocks.append(
            jnp.einsum(
                "kgqs,skd->qkgd",
                attn_prob.astype(jnp.bfloat16),
                v_loc[k_start:k_end],
                preferred_element_type=jnp.float32,
            ).astype(jnp.bfloat16)
        )
    attn_out = jnp.concatenate(out_blocks, axis=0)
    a_head = attn_out.reshape(win_rows, hq * HEAD_SIZE)
    product = jnp.dot(a_head, out_weight, preferred_element_type=jnp.float32)
    pieces = product.astype(jnp.bfloat16).reshape(seq_count, tok, product.shape[1])
    pieces = lax.all_to_all(pieces, "seq", split_axis=0, concat_axis=0, tiled=True)
    y_out = jnp.sum(pieces.astype(jnp.float32), axis=0).astype(jnp.bfloat16)
    incoming = lax.all_gather(out_grad.reshape(tok, out_grad.shape[2]), "seq", axis=0, tiled=True)
    wo_grad = lax.dot_general(
        a_head, incoming, (((0,), (0,)), ((), ())), preferred_element_type=jnp.float32
    )
    d_rows = lax.dot_general(
        incoming, out_weight, (((1,), (1,)), ((), ())), preferred_element_type=jnp.float32
    )
    attention_grad = d_rows.astype(jnp.bfloat16).reshape(win_rows, hk, group_width, HEAD_SIZE)

    dq_blocks = []
    dk_blocks = [None] * blk_count
    dv_blocks = [None] * blk_count
    for i in range(blk_count):
        q_start, k_start, k_end = band(i)
        q_blk = query_head_rows[q_start : q_start + blk]
        g_blk = attention_grad[q_start : q_start + blk]
        o_blk = attn_out[q_start : q_start + blk]
        row_dot = jnp.sum(g_blk.astype(jnp.float32) * o_blk.astype(jnp.float32), axis=-1)
        row_dot = jnp.transpose(row_dot, (1, 2, 0))[..., None]
        attn_prob, _, _ = probs(i, q_blk, *stats[i])
        k_band = k_loc[k_start:k_end]
        v_band = v_loc[k_start:k_end]
        d_prob = jnp.einsum("qkgd,skd->kgqs", g_blk, v_band, preferred_element_type=jnp.float32)
        score_gradient = (attn_prob * (d_prob - row_dot) * head_scale).astype(jnp.bfloat16)
        dq_blocks.append(
            jnp.einsum(
                "kgqs,skd->qkgd", score_gradient, k_band, preferred_element_type=jnp.float32
            ).astype(jnp.bfloat16)
        )
        dk_part = jnp.einsum(
            "kgqs,qkgd->skd", score_gradient, q_blk, preferred_element_type=jnp.float32
        )
        dv_part = jnp.einsum(
            "kgqs,qkgd->skd",
            attn_prob.astype(jnp.bfloat16),
            g_blk,
            preferred_element_type=jnp.float32,
        )
        for j in range(k_start // blk, k_end // blk):
            lo = j * blk - k_start
            for acc, part in ((dk_blocks, dk_part), (dv_blocks, dv_part)):
                piece = part[lo : lo + blk]
                acc[j] = piece if acc[j] is None else acc[j] + piece
    dq_all = jnp.concatenate(dq_blocks, axis=0).reshape(win_rows, hq, HEAD_SIZE)
    dk_all = jnp.concatenate(dk_blocks, axis=0).astype(jnp.bfloat16)
    dv_all = jnp.concatenate(dv_blocks, axis=0).astype(jnp.bfloat16)
    packed_out = jnp.concatenate([dq_all, dk_all, dv_all], axis=1).reshape(
        seq_count, tok, hq + 2 * hk, HEAD_SIZE
    )
    back = lax.all_to_all(packed_out, "seq", split_axis=0, concat_axis=0, tiled=True)
    back = back.transpose(1, 0, 2, 3)
    d_q = back[:, :, :hq].reshape(1, tok, QUERY_HEADS * HEAD_SIZE)
    key_gradient = back[:, :, hq : hq + hk].reshape(1, tok, KEY_VALUE_HEADS * HEAD_SIZE)
    value_gradient = back[:, :, hq + hk :].reshape(1, tok, KEY_VALUE_HEADS * HEAD_SIZE)
    y_count = lax.psum(1, "dpy")
    z_count = lax.psum(1, "dpz")
    cols = wo_grad.shape[1]
    wo_perm = (
        wo_grad.reshape(wo_grad.shape[0], y_count, z_count, cols // (y_count * z_count))
        .transpose(0, 2, 1, 3)
        .reshape(wo_grad.shape[0], cols)
    )
    wo_perm = lax.psum_scatter(wo_perm, "dpz", scatter_dimension=1, tiled=True)
    weight_grad = lax.psum_scatter(wo_perm, "dpy", scatter_dimension=1, tiled=True)
    return (
        y_out.reshape(1, tok, y_out.shape[1]),
        d_q,
        key_gradient,
        value_gradient,
        weight_grad,
    )


def solution(mesh):
    dp_count = mesh.shape["dp"]
    y_count = 4 if dp_count % 4 == 0 else 1
    mesh = Mesh(
        mesh.devices.reshape(mesh.shape["seq"], y_count, dp_count // y_count), ("seq", "dpy", "dpz")
    )
    in_specs = (
        P(DP, "seq", None),
        P(DP, "seq", None),
        P(DP, "seq", None),
        P("seq", None),
        P(DP, "seq", None),
        P(DP, None),
        P(DP, None),
    )
    out_specs = (
        P(DP, "seq", None),
        P(DP, "seq", None),
        P(DP, "seq", None),
        P(DP, "seq", None),
        P("seq", DP),
    )
    return jax.shard_map(local, mesh=mesh, in_specs=in_specs, out_specs=out_specs, check_vma=False)
```

time: 210 us -> 205 us (0.976)
  waiting for transfers between devices: 35 us -> 94 us
  local copies, waits for them, and re-layouts: 52.2 us -> 31.8 us
  starting transfers between devices: 36.3 us -> 18.6 us
  matrix products: 46.8 us -> 33 us
  other arithmetic: 20.1 us -> 11.1 us
  loops' own time: 2.23 us -> 0 us
    all_to_all x1, waiting for transfers between devices: 0.01 us -> 31 us  [local(): lax.all_to_all(pieces, 'seq', split_axis=0, concat_axis=0, tiled=True)]
    all_to_all x6 -> x2, waiting for transfers between devices: 30.1 us -> 50.4 us  [the longest x1 34.5 us: local(): got = lax.all_to_all(packed, 'seq', split_axis=0, concat_axis=0, tiled=True)]
    all_to_all x6 -> x2, starting transfers between devices: 30.4 us -> 12.6 us  [the longest x1 6.56 us: local(): got = lax.all_to_all(packed, 'seq', split_axis=0, concat_axis=0, tiled=True)]
    dot_general x30 -> x26, matrix products: 41.3 us -> 28.4 us  [the longest x4 7.52 us: local(): jnp.einsum('kgqs,skd->qkgd', attn_prob.astype(jnp.bfloat16), v_loc[k_star...]
    dynamic_slice x14 -> x0, local copies, waits for them, and re-layouts: 8.68 us -> none  [the longest x4 2.7 us: back_block(): g_blk = lax.dynamic_slice_in_dim(attention_grad, q_start, block_rows, 0)]
    reduce_scatter x1, waiting for transfers between devices: 3.98 us -> 11.9 us  [local(): wo_perm = lax.psum_scatter(wo_perm, 'dpz', scatter_dimension=1, tiled=True)]
    while x15 -> x0, local copies, waits for them, and re-layouts: 4.99 us -> none  [the longest x3 4.13 us: local(): lax.map(forward_block, jnp.arange(blk_count, dtype=jnp.int32))]
    reduce_sum x6 -> x4, other arithmetic: 6.43 us -> 1.6 us  [probs(): l = jnp.sum(expd, axis=-1, keepdims=True)]
  transfers between devices with their start and end apart: 10 -> 6, of which waited for: 8 -> 4; matrix products, arithmetic and copies ran while one was open for 56% -> 19% of each run, Pallas kernels for 0% -> 0%
where the time goes in v2:
time: 205 us; the launch traced here: 203 us
  waiting for transfers between devices  94 us (46%)
  matrix products  33 us (16%)
  local copies, waits for them, and re-layouts  31.8 us (16%)
  starting transfers between devices  18.6 us (9%)
  between operations  14.3 us (7%)
  other arithmetic  11.1 us (5%)
    all_to_all x1, waiting for transfers between devices, local(): got = lax.all_to_all(packed, 'seq', split_axis=0, concat_axis=0, tiled=True)  34.5 us
    all_to_all x1, waiting for transfers between devices, local(): lax.all_to_all(pieces, 'seq', split_axis=0, concat_axis=0, tiled=True)  31 us
    all_to_all x1, waiting for transfers between devices, local(): lax.all_to_all(packed_out, 'seq', split_axis=0, concat_axis=0, tiled=True)  15.9 us
    unnamed x73, local copies, waits for them, and re-layouts  14.9 us
    reduce_scatter x1, waiting for transfers between devices, local(): wo_perm = lax.psum_scatter(wo_perm, 'dpz', scatter_dimension=1, tiled=True)  11.9 us
    dot_general x4, matrix products, local(): jnp.einsum('kgqs,skd->qkgd', attn_prob.astype(jnp.bfloat16), v_loc[k_star...  7.52 us
    dot_general x1, local copies, waits for them, and re-layouts, local(): lax.dot_general(a_head, incoming, (((0,), (0,)), ((), ())), preferred_ele...  6.64 us
    all_to_all x1, starting transfers between devices, local(): got = lax.all_to_all(packed, 'seq', split_axis=0, concat_axis=0, tiled=True)  6.56 us
  transfers between devices with their start and end apart: 6, of which 4 were waited for; matrix products, arithmetic and copies ran while one was open for 19% of the time, Pallas kernels for 0%

profile of v2, /device:TPU:2, one launch (start us, length us, event | category | flops | bytes accessed | tf_op | source)
XLA Modules:
  0.0 202.8 jit_solution(8232879235119966142)
XLA Ops:
  7.2 0.7 all-gather.3.cloned.1.call-update
  7.9 1.1 copy.188
  9.0 1.8 copy.189
  10.8 1.6 copy.187
  12.5 2.3 %maximum_bitcast_fusion = bf16[8,128,6,128]{1,3,2,0:T(8,128)(2,1)} fusion(bf16[128,8,1,128]{0,3,2,1:T(8,128)(2,1)} %bitcast.455, bf16[128,8,1,128]{0,3,2,1:T(8,128)(2,1)S(1)} %bitcast.454, bf16[128,8,4,128]{0,3,2,1:T(8,128)(2,1)S(1)} %bitcast.447), kind=kLoop, calls=%fused_computation.37 | loop fusion | flops 1572864 | bytes 3145728 | tf_op jit(solution)/shard_map/transpose | solution.py:46
  14.8 2.6 %copy.192 = bf16[8,128,6,128]{3,1,2,0:T(8,128)(2,1)} copy(bf16[8,128,6,128]{1,3,2,0:T(8,128)(2,1)} %maximum_bitcast_fusion) | data formatting | bytes 3145728 | tf_op jit(solution)/shard_map/transpose | solution.py:46
  17.4 6.6 %all-to-all-start = ((bf16[8,128,6,128]{3,1,2,0:T(8,128)(2,1)}), bf16[8,128,6,128]{3,1,2,0:T(8,128)(2,1)}, u32[]{:S(2)}, u32[]{:S(2)}) async-start(bf16[8,128,6,128]{3,1,2,0:T(8,128)(2,1)} %copy.192), calls=%async_computation | async-start | bytes 3145728 | tf_op jit(solution)/shard_map/all_to_all | solution.py:47
  24.8 0.8 fusion.67
  25.6 34.5 %all-to-all-done = bf16[8,128,6,128]{3,1,2,0:T(8,128)(2,1)} async-done(((bf16[8,128,6,128]{3,1,2,0:T(8,128)(2,1)}), bf16[8,128,6,128]{3,1,2,0:T(8,128)(2,1)}, u32[]{:S(2)}, u32[]{:S(2)}) %all-to-all-start) | async-done | bytes 1572896 | tf_op jit(solution)/shard_map/all_to_all | solution.py:47
  60.1 1.5 copy.193
  62.2 0.5 fusion.11
  62.7 1.3 copy-done.12
  65.5 0.5 fusion.17
  66.3 1.4 copy-done.9
  68.2 4.6 %fusion.26 = bf16[1024,512]{0,1:T(8,128)(2,1)S(1)} fusion(bf16[512,2048]{1,0:T(8,128)(2,1)S(1)} %copy-done, bf16[1,1024,2048]{2,1,0:T(8,128)(2,1)} %all-gather.3.cloned.1.call-done), kind=kOutput, calls=%fused_computation.39 | convolution fusion | flops 2148007936 | bytes 7340032 | tf_op jit(solution)/shard_map/dot_general | solution.py:105
  72.8 0.9 fusion.95
  73.7 1.0 copy-done.13
  74.7 1.5 convolution_bitcast_fusion.2
  76.1 2.4 %fusion.61 = (f32[256,4]{0,1:T(4,128)S(1)}, bf16[256,1,4,128]{0,3,2,1:T(8,128)(2,1)}) fusion(bf16[256,1,4,128]{0,3,2,1:T(8,128)(2,1)S(1)} %bitcast.471, f32[4,256]{1,0:T(4,128)S(1)} %fusion.25, f32[4,256]{1,0:T(4,128)S(1)} %get-tuple-element.34, f32[512,256,4]{1,0,2:T(8,128)S(1)} %copy-done.13, pred[256,512]{0,1:T(8,128)(4,1)S(1)} %copy-done.23, ...), kind=kOutput, calls=%fused_computation.95 | convolution fusion | flops 137493504 | bytes 2895872 | tf_op jit(solution)/shard_map/kgqs,skd->qkgd/dot_general | solution.py:88
  78.5 1.7 fusion.31
  80.2 1.0 copy-done.4
  81.2 1.4 convolution_bitcast_fusion.5
  82.7 6.6 %copy.230 = bf16[2048,1024]{1,0:T(8,128)(2,1)} copy(bf16[2048,1024]{0,1:T(8,128)(2,1)} %bitcast.448) | data formatting | bytes 8388608 | tf_op jit(solution)/shard_map/dot_general | solution.py:102
  89.3 1.6 fusion.64
  91.0 1.8 fusion.62
  92.9 1.8 fusion.63
  95.2 2.4 %convolution_bitcast_fusion = f32[512,8,4,64]{0,3,1,2:T(8,128)S(1)} fusion(bf16[1024,512,1,1]{0,1,3,2:T(8,128)(2,1)S(1)} %bitcast.456, bf16[4,8,64,1024]{3,2,1,0:T(8,128)(2,1)S(1)} %bitcast.450), kind=kOutput, calls=%fused_computation.3 | convolution fusion | flops 2147483648 | bytes 9437184 | tf_op jit(solution)/shard_map/dot_general | solution.py:102
  97.6 2.5 %copy.232 = f32[512,8,4,64]{0,3,2,1:T(8,128)} copy(f32[512,8,4,64]{0,3,1,2:T(8,128)S(1)} %convolution_bitcast_fusion) | data formatting | bytes 8388608 | tf_op jit(solution)/shard_map/transpose | solution.py:160
  100.2 1.6 fusion.37
  102.5 1.0 copy-done.8
  103.5 0.8 fusion.30
  105.1 0.8 fusion.29
  106.9 0.8 convolution_bitcast_fusion.3
  107.7 0.8 convolution_bitcast_fusion.4
  109.1 0.5 convolution_bitcast_fusion.6
  110.5 1.4 pad_maximum_fusion
  111.9 6.1 %all-to-all-start.2 = ((bf16[8,128,6,128]{1,3,2,0:T(8,128)(2,1)}), bf16[8,128,6,128]{1,3,2,0:T(8,128)(2,1)}, u32[]{:S(2)}, u32[]{:S(2)}) async-start(bf16[8,128,6,128]{1,3,2,0:T(8,128)(2,1)} %pad_maximum_fusion), calls=%async_computation.2 | async-start | bytes 3145728 | tf_op jit(solution)/shard_map/all_to_all | solution.py:150
  118.0 4.4 %convolution_convert_fusion = bf16[1024,2048]{1,0:T(8,128)(2,1)} fusion(bf16[1024,512]{0,1:T(8,128)(2,1)S(1)} %bitcast.457, bf16[512,2048]{1,0:T(8,128)(2,1)S(1)} %copy-done), kind=kOutput, calls=%fused_computation.2 | convolution fusion | flops 2149580800 | bytes 7340032 | tf_op jit(solution)/shard_map/dot_general | solution.py:97
  122.4 15.9 %all-to-all-done.2 = bf16[8,128,6,128]{1,3,2,0:T(8,128)(2,1)} async-done(((bf16[8,128,6,128]{1,3,2,0:T(8,128)(2,1)}), bf16[8,128,6,128]{1,3,2,0:T(8,128)(2,1)}, u32[]{:S(2)}, u32[]{:S(2)}) %all-to-all-start.2) | async-done | bytes 1572896 | tf_op jit(solution)/shard_map/all_to_all | solution.py:150
  138.2 5.9 %all-to-all-start.1 = ((bf16[8,128,2048]{2,1,0:T(8,128)(2,1)}), bf16[8,128,2048]{2,1,0:T(8,128)(2,1)}, u32[]{:S(2)}, u32[]{:S(2)}) async-start(bf16[8,128,2048]{2,1,0:T(8,128)(2,1)} %bitcast.449), calls=%async_computation.1 | async-start | bytes 8388608 | tf_op jit(solution)/shard_map/all_to_all | solution.py:99
  144.1 11.9 %reduce-scatter.3.cloned.1.call-done = f32[512,256]{0,1:T(8,128)} async-done(((f32[512,2048]{0,1:T(8,128)}), f32[512,256]{0,1:T(8,128)}) %reduce-scatter.3.cloned.1.call-update) | async-done | bytes 524304 | tf_op jit(solution)/shard_map/reduce_scatter | solution.py:163
  156.1 1.3 slice.213
  157.4 1.3 copy.233
  158.7 1.1 fusion.94
  159.8 0.9 copy.235
  160.6 0.8 copy.234
  161.5 31.0 %all-to-all-done.1 = bf16[8,128,2048]{2,1,0:T(8,128)(2,1)} async-done(((bf16[8,128,2048]{2,1,0:T(8,128)(2,1)}), bf16[8,128,2048]{2,1,0:T(8,128)(2,1)}, u32[]{:S(2)}, u32[]{:S(2)}) %all-to-all-start.1) | async-done | bytes 4194336 | tf_op jit(solution)/shard_map/all_to_all | solution.py:99
  192.5 3.8 %reduce_sum.116 = bf16[128,2048]{1,0:T(8,128)(2,1)} reduce(bf16[8,128,2048]{2,1,0:T(8,128)(2,1)} %all-to-all-done.1, bf16[]{:T(256)} %constant.8.clone.1), dimensions={0}, to_apply=%region_11.12 | reduce | flops 1835008 | bytes 4718594 | tf_op jit(solution)/shard_map/reduce_sum | solution.py:100
  (104 shorter events, 8.2 us)
Async XLA Ops:
  7.2 61.0 %copy-start = (bf16[512,2048]{1,0:T(8,128)(2,1)S(1)}, bf16[512,2048]{1,0:T(8,128)(2,1)}, u32[]{:S(2)}) copy-start(bf16[512,2048]{1,0:T(8,128)(2,1)} %param.10) | copy-start | bytes 6291460
  7.2 61.0 %all-gather.3.cloned.1.call-start = ((), (), s32[]{:S(2)}) async-start(), calls=%async_computation.7 | async-start | bytes 4718592 | tf_op jit(solution)/shard_map/all_gather | solution.py:101
  17.4 6.6 %copy-start.31 = (s32[1,16]{1,0:T(1,128)S(1)}, s32[1,16]{1,0:T(1,128)}, u32[]{:S(2)}) copy-start(s32[1,16]{1,0:T(1,128)} %param.12) | copy-start | bytes 196
  17.4 6.6 %copy-start.32 = (s32[1,16]{1,0:T(1,128)S(1)}, s32[1,16]{1,0:T(1,128)}, u32[]{:S(2)}) copy-start(s32[1,16]{1,0:T(1,128)} %param.13) | copy-start | bytes 196
  17.4 42.8 %all-to-all-start = ((bf16[8,128,6,128]{3,1,2,0:T(8,128)(2,1)}), bf16[8,128,6,128]{3,1,2,0:T(8,128)(2,1)}, u32[]{:S(2)}, u32[]{:S(2)}) async-start(bf16[8,128,6,128]{3,1,2,0:T(8,128)(2,1)} %copy.192), calls=%async_computation | async-start | bytes 3145728 | tf_op jit(solution)/shard_map/all_to_all | solution.py:47
  23.9 132.1 %reduce-scatter.3.cloned.1.call-start = ((), (), s32[]{:S(2)}) async-start(), calls=%async_computation.5 | async-start | bytes 4718592 | tf_op jit(solution)/shard_map/reduce_scatter | solution.py:163
  24.7 40.3 %copy-start.16 = (pred[256,512]{0,1:T(8,128)(4,1)}, pred[256,512]{0,1:T(8,128)(4,1)S(1)}, u32[]{:S(2)}) copy-start(pred[256,512]{0,1:T(8,128)(4,1)S(1)} %compare_and_fusion.1) | copy-start | bytes 393220
  25.6 40.7 %copy-start.19 = (pred[256,512]{0,1:T(8,128)(4,1)}, pred[256,512]{0,1:T(8,128)(4,1)S(1)}, u32[]{:S(2)}) copy-start(pred[256,512]{0,1:T(8,128)(4,1)S(1)} %get-tuple-element.50) | copy-start | bytes 393220
  60.1 2.1 %copy-start.22 = (pred[256,512]{0,1:T(8,128)(4,1)S(1)}, pred[256,512]{0,1:T(8,128)(4,1)}, u32[]{:S(2)}) copy-start(pred[256,512]{0,1:T(8,128)(4,1)} %get-tuple-element.51) | copy-start | bytes 393220
  61.7 3.8 %copy-start.1 = (bf16[8,128,6,128]{3,1,0,2:T(8,128)(2,1)}, bf16[8,128,6,128]{3,1,0,2:T(8,128)(2,1)S(1)}, u32[]{:S(2)}) copy-start(bf16[8,128,6,128]{3,1,0,2:T(8,128)(2,1)S(1)} %copy.193) | copy-start | bytes 4718596
  62.7 1.3 copy-start.12
  65.0 1.3 copy-start.6
  66.3 1.4 copy-start.9
  68.2 5.5 %copy-start.23 = (pred[256,512]{0,1:T(8,128)(4,1)S(1)}, pred[256,512]{0,1:T(8,128)(4,1)}, u32[]{:S(2)}) copy-start(pred[256,512]{0,1:T(8,128)(4,1)} %get-tuple-element.51) | copy-start | bytes 393220
  72.8 1.9 copy-start.13
  80.2 1.0 copy-start.4
  89.3 1.7 copy-start.7
  89.3 1.7 copy-start.17
  89.3 1.7 copy-start.27
  91.0 1.8 copy-start.10
  91.0 1.8 copy-start.20
  91.0 1.8 copy-start.25
  92.9 1.8 copy-start.29
  92.9 2.3 %copy-start.3 = (bf16[2048,1024]{1,0:T(8,128)(2,1)S(1)}, bf16[2048,1024]{1,0:T(8,128)(2,1)}, u32[]{:S(2)}) copy-start(bf16[2048,1024]{1,0:T(8,128)(2,1)} %copy.230) | copy-start | bytes 12582916
  94.8 2.8 %copy-start.14 = (bf16[1024,1,4,128]{0,3,2,1:T(8,128)(2,1)}, bf16[1024,1,4,128]{0,3,2,1:T(8,128)(2,1)S(1)}, u32[]{:S(2)}) copy-start(bf16[1024,1,4,128]{0,3,2,1:T(8,128)(2,1)S(1)} %pad_maximum_fusion.1) | copy-start | bytes 3145732
  100.2 1.6 copy-start.2
  100.2 1.9 copy-start.30
  100.2 1.9 copy-start.5
  101.8 1.7 copy-start.8
  101.8 1.7 copy-start.18
  101.8 1.7 copy-start.28
  103.5 1.6 copy-start.11
  103.5 1.6 copy-start.21
  103.5 1.6 copy-start.26
  107.7 1.0 copy-start.24
  111.9 6.1 %copy-start.15 = (bf16[1024,1,4,128]{0,3,2,1:T(8,128)(2,1)S(1)}, bf16[1024,1,4,128]{0,3,2,1:T(8,128)(2,1)}, u32[]{:S(2)}) copy-start(bf16[1024,1,4,128]{0,3,2,1:T(8,128)(2,1)} %copy-done.14) | copy-start | bytes 3145732
  111.9 26.3 %all-to-all-start.2 = ((bf16[8,128,6,128]{1,3,2,0:T(8,128)(2,1)}), bf16[8,128,6,128]{1,3,2,0:T(8,128)(2,1)}, u32[]{:S(2)}, u32[]{:S(2)}) async-start(bf16[8,128,6,128]{1,3,2,0:T(8,128)(2,1)} %pad_maximum_fusion), calls=%async_computation.2 | async-start | bytes 3145728 | tf_op jit(solution)/shard_map/all_to_all | solution.py:150
  138.2 54.2 %all-to-all-start.1 = ((bf16[8,128,2048]{2,1,0:T(8,128)(2,1)}), bf16[8,128,2048]{2,1,0:T(8,128)(2,1)}, u32[]{:S(2)}, u32[]{:S(2)}) async-start(bf16[8,128,2048]{2,1,0:T(8,128)(2,1)} %bitcast.449), calls=%async_computation.1 | async-start | bytes 8388608 | tf_op jit(solution)/shard_map/all_to_all | solution.py:99
  144.1 52.2 %reduce-scatter.5.cloned.1.call-start = ((), (), s32[]{:S(2)}) async-start(), calls=%async_computation.6 | async-start | bytes 655360 | tf_op jit(solution)/shard_map/reduce_scatter | solution.py:164
Sparse Core Ops, SparseCore 0:
  9.8 51.9 all-gather.2
  100.3 55.7 reduce-scatter.2
  159.2 22.8 reduce-scatter.4

commit v3 on v2

--- a/solution.py
+++ b/solution.py
@@ -7,6 +7,7 @@
 KEY_VALUE_HEADS = 8
 HEAD_SIZE = 128
 DP = ("dpy", "dpz")
+SEQ = ("x", "core")
 BLOCK = 256
 MOST = 256
 
@@ -30,7 +31,9 @@
 
 
 def local(queries, rotated_key_matrix, value_matrix, out_weight, out_grad, lengths, pack_order):
-    seq_count = lax.psum(1, "seq")
+    seq_count = lax.psum(1, SEQ)
+    x_count = lax.psum(1, "x")
+    core_count = lax.psum(1, "core")
     tok = queries.shape[1]
     head_scale = HEAD_SIZE ** (-0.5)
     hq = QUERY_HEADS // seq_count
@@ -44,7 +47,8 @@
         ],
         axis=2,
     ).transpose(1, 0, 2, 3)
-    got = lax.all_to_all(packed, "seq", split_axis=0, concat_axis=0, tiled=True)
+    got = lax.all_to_all(packed, SEQ, split_axis=0, concat_axis=0, tiled=True)
+    got, out_grad = lax.optimization_barrier((got, out_grad))
     win_rows = seq_count * tok
     got = got.reshape(win_rows, hq + 2 * hk, HEAD_SIZE)
     query_head_rows = got[:, :hq].reshape(win_rows, hk, group_width, HEAD_SIZE)
@@ -95,10 +99,19 @@
     attn_out = jnp.concatenate(out_blocks, axis=0)
     a_head = attn_out.reshape(win_rows, hq * HEAD_SIZE)
     product = jnp.dot(a_head, out_weight, preferred_element_type=jnp.float32)
-    pieces = product.astype(jnp.bfloat16).reshape(seq_count, tok, product.shape[1])
-    pieces = lax.all_to_all(pieces, "seq", split_axis=0, concat_axis=0, tiled=True)
-    y_out = jnp.sum(pieces.astype(jnp.float32), axis=0).astype(jnp.bfloat16)
-    incoming = lax.all_gather(out_grad.reshape(tok, out_grad.shape[2]), "seq", axis=0, tiled=True)
+    width = product.shape[1]
+    pieces = (
+        product.astype(jnp.bfloat16)
+        .reshape(x_count, core_count, tok, width)
+        .transpose(1, 0, 2, 3)
+    )
+    pieces = lax.all_to_all(pieces, "core", split_axis=0, concat_axis=0, tiled=True)
+    pair_sum = jnp.sum(pieces.astype(jnp.float32), axis=0).astype(jnp.bfloat16)
+    pair_sum = lax.all_to_all(pair_sum, "x", split_axis=0, concat_axis=0, tiled=True)
+    y_out = jnp.sum(pair_sum.astype(jnp.float32), axis=0).astype(jnp.bfloat16)
+    g_rows = lax.all_gather(out_grad.reshape(tok, out_grad.shape[2]), "x", axis=0, tiled=False)
+    g_rows = lax.all_gather(g_rows, "core", axis=0, tiled=False)
+    incoming = g_rows.transpose(1, 0, 2, 3).reshape(win_rows, g_rows.shape[3])
     wo_grad = lax.dot_general(
         a_head, incoming, (((0,), (0,)), ((), ())), preferred_element_type=jnp.float32
     )
@@ -147,7 +160,7 @@
     packed_out = jnp.concatenate([dq_all, dk_all, dv_all], axis=1).reshape(
         seq_count, tok, hq + 2 * hk, HEAD_SIZE
     )
-    back = lax.all_to_all(packed_out, "seq", split_axis=0, concat_axis=0, tiled=True)
+    back = lax.all_to_all(packed_out, SEQ, split_axis=0, concat_axis=0, tiled=True)
     back = back.transpose(1, 0, 2, 3)
     d_q = back[:, :, :hq].reshape(1, tok, QUERY_HEADS * HEAD_SIZE)
     key_gradient = back[:, :, hq : hq + hk].reshape(1, tok, KEY_VALUE_HEADS * HEAD_SIZE)
@@ -174,23 +187,28 @@
 def solution(mesh):
     dp_count = mesh.shape["dp"]
     y_count = 4 if dp_count % 4 == 0 else 1
+    seq_count = mesh.shape["seq"]
+    core_count = 2 if seq_count % 2 == 0 else 1
     mesh = Mesh(
-        mesh.devices.reshape(mesh.shape["seq"], y_count, dp_count // y_count), ("seq", "dpy", "dpz")
+        mesh.devices.reshape(
+            seq_count // core_count, core_count, y_count, dp_count // y_count
+        ),
+        ("x", "core", "dpy", "dpz"),
     )
     in_specs = (
-        P(DP, "seq", None),
-        P(DP, "seq", None),
-        P(DP, "seq", None),
-        P("seq", None),
-        P(DP, "seq", None),
+        P(DP, SEQ, None),
+        P(DP, SEQ, None),
+        P(DP, SEQ, None),
+        P(SEQ, None),
+        P(DP, SEQ, None),
         P(DP, None),
         P(DP, None),
     )
     out_specs = (
-        P(DP, "seq", None),
-        P(DP, "seq", None),
-        P(DP, "seq", None),
-        P(DP, "seq", None),
-        P("seq", DP),
+        P(DP, SEQ, None),
+        P(DP, SEQ, None),
+        P(DP, SEQ, None),
+        P(DP, SEQ, None),
+        P(SEQ, DP),
     )
     return jax.shard_map(local, mesh=mesh, in_specs=in_specs, out_specs=out_specs, check_vma=False)

time: 205 us -> 235 us (1.15)
  blocking collectives: 0 us -> 26.8 us
  local copies, waits for them, and re-layouts: 31.8 us -> 47.5 us
  waiting for transfers between devices: 94 us -> 80.9 us
  other arithmetic: 11.1 us -> 14.7 us
    all_to_all x3, waiting for transfers between devices: 81.4 us -> 34 us  [the longest x1 19 us: local(): lax.all_to_all(pair_sum, 'x', split_axis=0, concat_axis=0, tiled=True)]
    all_gather x1 -> x2, waiting for transfers between devices: 0.02 us -> 45.2 us  [the longest x1 32.7 us: local(): lax.all_gather(out_grad.reshape(tok, out_grad.shape[2]), 'x', axis=0, til...]
    all_to_all x0 -> x1, blocking collectives: none -> 26.8 us  [local(): got = lax.all_to_all(packed, SEQ, split_axis=0, concat_axis=0, tiled=True)]
    reduce_scatter x1, waiting for transfers between devices: 11.9 us -> 0.01 us  [local(): wo_perm = lax.psum_scatter(wo_perm, 'dpz', scatter_dimension=1, tiled=True)]
    transpose x0 -> x1, local copies, waits for them, and re-layouts: none -> 11.2 us  [local(): incoming = g_rows.transpose(1, 0, 2, 3).reshape(win_rows, g_rows.shape[3])]
    reshape x0 -> x2, local copies, waits for them, and re-layouts: none -> 10 us  [the longest x1 7.71 us: local(): incoming = g_rows.transpose(1, 0, 2, 3).reshape(win_rows, g_rows.shape[3])]
    dot_general x1 -> x0, local copies, waits for them, and re-layouts: 6.64 us -> none  [local(): lax.dot_general(a_head, incoming, (((0,), (0,)), ((), ())), preferred_ele...]
    reduce_sum x1 -> x2, other arithmetic: 3.85 us -> 8.12 us  [the longest x1 5.21 us: local(): pair_sum = jnp.sum(pieces.astype(jnp.float32), axis=0).astype(jnp.bfloat16)]
  transfers between devices with their start and end apart: 6 -> 7, of which waited for: 4 -> 5; matrix products, arithmetic and copies ran while one was open for 19% -> 17% of each run, Pallas kernels for 0% -> 0%
where the time goes in v3:
time: 235 us; the launch traced here: 233 us
  waiting for transfers between devices  80.9 us (34%)
  local copies, waits for them, and re-layouts  47.5 us (20%)
  matrix products  32 us (14%)
  blocking collectives  26.8 us (11%)
  starting transfers between devices  16.7 us (7%)
  other arithmetic  14.7 us (6%)
  between operations  14.6 us (6%)
    all_gather x1, waiting for transfers between devices, local(): lax.all_gather(out_grad.reshape(tok, out_grad.shape[2]), 'x', axis=0, til...  32.7 us
    all_to_all x1, blocking collectives, local(): got = lax.all_to_all(packed, SEQ, split_axis=0, concat_axis=0, tiled=True)  26.8 us
    all_to_all x1, waiting for transfers between devices, local(): lax.all_to_all(pair_sum, 'x', split_axis=0, concat_axis=0, tiled=True)  19 us
    unnamed x119, local copies, waits for them, and re-layouts  16.1 us
    all_to_all x1, waiting for transfers between devices, local(): lax.all_to_all(packed_out, SEQ, split_axis=0, concat_axis=0, tiled=True)  15 us
    all_gather x1, waiting for transfers between devices, local(): g_rows = lax.all_gather(g_rows, 'core', axis=0, tiled=False)  12.5 us
    transpose x1, local copies, waits for them, and re-layouts, local(): incoming = g_rows.transpose(1, 0, 2, 3).reshape(win_rows, g_rows.shape[3])  11.2 us
    dot_general x4, matrix products, local(): jnp.einsum('kgqs,skd->qkgd', attn_prob.astype(jnp.bfloat16), v_loc[k_star...  8.7 us
  transfers between devices with their start and end apart: 7, of which 5 were waited for; matrix products, arithmetic and copies ran while one was open for 17% of the time, Pallas kernels for 0%

profile of v3, /device:TPU:2, one launch (start us, length us, event | category | flops | bytes accessed | tf_op | source)
XLA Modules:
  0.0 233.3 jit_solution(10886765528669761368)
XLA Ops:
  7.2 1.3 copy.190
  8.5 1.8 copy.191
  10.3 1.6 copy.189
  11.9 2.3 maximum_bitcast_fusion
  14.2 2.6 %copy.194 = bf16[8,128,6,128]{3,1,2,0:T(8,128)(2,1)} copy(bf16[8,128,6,128]{1,3,2,0:T(8,128)(2,1)} %maximum_bitcast_fusion) | data formatting | bytes 3145728 | tf_op jit(solution)/shard_map/transpose | solution.py:49
  16.8 26.8 %all_to_all.20 = bf16[8,128,6,128]{3,1,2,0:T(8,128)(2,1)} all-to-all(bf16[8,128,6,128]{3,1,2,0:T(8,128)(2,1)} %copy.194), channel_id=1, replica_groups=mesh['x'=4,'core'=2,'dpy'=4,'dpz'=8] {'x','core'}, dimensions={0} | all-to-all | bytes 3145728 | tf_op jit(solution)/shard_map/all_to_all | solution.py:50
  43.7 32.7 %all-gather.4.cloned.1.call-done = bf16[4,128,2048]{2,1,0:T(8,128)(2,1)} async-done(((bf16[1,128,2048]{2,1,0:T(8,128)(2,1)}), bf16[4,128,2048]{2,1,0:T(8,128)(2,1)}) %all-gather.4.cloned.1.call-update) | async-done | bytes 2097168 | tf_op jit(solution)/shard_map/all_gather | solution.py:112
  77.7 1.6 copy.195
  80.3 1.4 copy-done.18
  84.0 1.3 copy-done.14
  85.7 12.5 %all-gather.6.cloned.1.call-done = bf16[8,128,2048]{2,1,0:T(8,128)(2,1)} async-done(((bf16[4,128,2048]{2,1,0:T(8,128)(2,1)}), bf16[8,128,2048]{2,1,0:T(8,128)(2,1)}) %all-gather.6.cloned.1.call-update) | async-done | bytes 4194320 | tf_op jit(solution)/shard_map/all_gather | solution.py:113
  98.3 11.2 %copy.206 = bf16[4,2,128,2048]{2,1,0,3:T(2,128)(2,1)} copy(bf16[4,2,128,2048]{3,2,0,1:T(8,128)(2,1)} %bitcast.453) | data formatting | bytes 8388608 | tf_op jit(solution)/shard_map/transpose | solution.py:114
  109.5 7.7 %reshape.439 = bf16[1024,2048]{0,1:T(8,128)(2,1)} reshape(bf16[4,2,128,2048]{2,1,0,3:T(2,128)(2,1)} %copy.206) | data formatting | bytes 8388608 | tf_op jit(solution)/shard_map/reshape | solution.py:114
  117.2 4.5 %convolution_convert_fusion.1 = bf16[1024,512]{0,1:T(8,128)(2,1)S(1)} fusion(bf16[512,2048]{1,0:T(8,128)(2,1)S(1)} %copy-done, bf16[1024,2048]{0,1:T(8,128)(2,1)} %reshape.439), kind=kOutput, calls=%fused_computation.38 | convolution fusion | flops 2148007936 | bytes 7340032 | tf_op jit(solution)/shard_map/dot_general | solution.py:118
  121.8 2.1 fusion.59
  123.9 1.8 fusion.56
  125.8 2.4 %fusion.57 = (f32[256,4]{0,1:T(4,128)}, bf16[256,1,4,128]{0,3,2,1:T(8,128)(2,1)S(1)}) fusion(bf16[256,1,4,128]{0,3,2,1:T(8,128)(2,1)S(1)} %bitcast.472, f32[4,256]{1,0:T(4,128)S(1)} %fusion.21, f32[4,256]{1,0:T(4,128)S(1)} %get-tuple-element.40, f32[512,256,4]{1,0,2:T(8,128)S(1)} %copy-done.12, pred[256,512]{0,1:T(8,128)(4,1)S(1)} %compare_and_fusion.1, ...), kind=kOutput, calls=%fused_computation.96 | convolution fusion | flops 137493504 | bytes 2895872 | tf_op jit(solution)/shard_map/kgqs,skd->qkgd/dot_general | solution.py:92
  128.2 2.4 %fusion.58 = (f32[256,4]{0,1:T(4,128)}, bf16[256,1,4,128]{0,3,2,1:T(8,128)(2,1)S(1)}) fusion(bf16[256,1,4,128]{0,3,2,1:T(8,128)(2,1)S(1)} %bitcast.469, f32[4,256]{1,0:T(4,128)S(1)} %fusion.19, f32[4,256]{1,0:T(4,128)S(1)} %get-tuple-element.42, f32[512,256,4]{1,0,2:T(8,128)S(1)} %copy-done.15, pred[256,512]{0,1:T(8,128)(4,1)S(1)} %get-tuple-element.54, ...), kind=kOutput, calls=%fused_computation.98 | convolution fusion | flops 137493504 | bytes 2895872 | tf_op jit(solution)/shard_map/kgqs,skd->qkgd/dot_general | solution.py:92
  130.8 2.4 %convolution_bitcast_fusion = f32[512,8,4,64]{0,3,1,2:T(8,128)S(1)} fusion(bf16[1024,512,1,1]{0,1,3,2:T(8,128)(2,1)S(1)} %bitcast.461, bf16[4,8,64,1024]{3,2,1,0:T(8,128)(2,1)S(1)} %bitcast.454), kind=kOutput, calls=%fused_computation.2 | convolution fusion | flops 2147483648 | bytes 9437184 | tf_op jit(solution)/shard_map/dot_general | solution.py:115
  133.2 2.5 %copy.235 = f32[512,8,4,64]{0,3,2,1:T(8,128)} copy(f32[512,8,4,64]{0,3,1,2:T(8,128)S(1)} %convolution_bitcast_fusion) | data formatting | bytes 8388608 | tf_op jit(solution)/shard_map/transpose | solution.py:173
  135.8 0.9 copy-done.32
  136.6 2.6 %convolution_bitcast_fusion.2 = f32[512,1,128]{0,2,1:T(8,128)S(1)} fusion(bf16[256,4,128]{0,2,1:T(8,128)(2,1)} %bitcast.476, f32[4,256]{1,0:T(4,128)S(1)} %fusion.23, f32[4,256]{1,0:T(4,128)S(1)} %get-tuple-element.38, f32[512,256,4]{1,0,2:T(8,128)} %copy-done.18, pred[256,512]{0,1:T(8,128)(4,1)S(1)} %copy-done.32), kind=kOutput, calls=%fused_computation.66 | convolution fusion | flops 136839168 | bytes 2760704 | tf_op jit(solution)/shard_map/kgqs,qkgd->skd/dot_general | solution.py:146
  139.2 0.7 slice.276
  140.0 0.8 fusion.26
  142.6 1.0 copy-done.13
  143.6 0.8 fusion.25
  145.2 0.8 fusion.24
  147.3 0.5 copy-done.24
  147.8 2.4 %convolution_convert_fusion = bf16[1024,2048]{1,0:T(8,128)(2,1)S(1)} fusion(bf16[1024,512]{0,1:T(8,128)(2,1)S(1)} %bitcast.462, bf16[512,2048]{1,0:T(8,128)(2,1)S(1)} %copy-done), kind=kOutput, calls=%fused_computation.1 | convolution fusion | flops 2149580800 | bytes 7340032 | tf_op jit(solution)/shard_map/dot_general | solution.py:101
  150.2 2.3 copy.287
  152.5 5.7 %all-to-all-start.1 = ((bf16[2,4,128,2048]{3,2,1,0:T(8,128)(2,1)}), bf16[2,4,128,2048]{3,2,1,0:T(8,128)(2,1)}, u32[]{:S(2)}, u32[]{:S(2)}) async-start(bf16[2,4,128,2048]{3,2,1,0:T(8,128)(2,1)} %bitcast.431), calls=%async_computation.1 | async-start | bytes 8388608 | tf_op jit(solution)/shard_map/all_to_all | solution.py:108
  158.2 2.6 %convolution_bitcast_fusion.3 = f32[512,1,128]{0,2,1:T(8,128)S(1)} fusion(bf16[256,4,128]{0,2,1:T(8,128)(2,1)} %bitcast.473, f32[4,256]{1,0:T(4,128)} %copy-done.46, f32[4,256]{1,0:T(4,128)S(1)} %get-tuple-element.40, f32[512,256,4]{1,0,2:T(8,128)} %copy-done.11, pred[256,512]{0,1:T(8,128)(4,1)} %copy-done.25), kind=kOutput, calls=%fused_computation.67 | convolution fusion | flops 136839168 | bytes 2760704 | tf_op jit(solution)/shard_map/kgqs,qkgd->skd/dot_general | solution.py:146
  160.9 0.8 convolution_bitcast_fusion.4
  163.1 0.6 copy-done.3
  165.4 1.4 pad_maximum_fusion
  166.7 5.0 %all-to-all-start.3 = ((bf16[8,128,6,128]{1,3,2,0:T(8,128)(2,1)}), bf16[8,128,6,128]{1,3,2,0:T(8,128)(2,1)}, u32[]{:S(2)}, u32[]{:S(2)}) async-start(bf16[8,128,6,128]{1,3,2,0:T(8,128)(2,1)} %pad_maximum_fusion), calls=%async_computation.3 | async-start | bytes 3145728 | tf_op jit(solution)/shard_map/all_to_all | solution.py:163
  171.8 5.2 %reduce_sum.128 = bf16[4,128,2048]{2,1,0:T(8,128)(2,1)} reduce(bf16[2,4,128,2048]{3,2,1,0:T(8,128)(2,1)} %all-to-all-done.1, bf16[]{:T(256)} %constant.24.clone.1), dimensions={0}, to_apply=%region_11.12 | reduce | flops 1048576 | bytes 6291458 | tf_op jit(solution)/shard_map/reduce_sum | solution.py:109
  177.0 15.0 %all-to-all-done.3 = bf16[8,128,6,128]{1,3,2,0:T(8,128)(2,1)} async-done(((bf16[8,128,6,128]{1,3,2,0:T(8,128)(2,1)}), bf16[8,128,6,128]{1,3,2,0:T(8,128)(2,1)}, u32[]{:S(2)}, u32[]{:S(2)}) %all-to-all-start.3) | async-done | bytes 1572896 | tf_op jit(solution)/shard_map/all_to_all | solution.py:163
  192.0 5.9 %all-to-all-start.2 = ((bf16[4,128,2048]{2,1,0:T(8,128)(2,1)}), bf16[4,128,2048]{2,1,0:T(8,128)(2,1)}, u32[]{:S(2)}, u32[]{:S(2)}) async-start(bf16[4,128,2048]{2,1,0:T(8,128)(2,1)} %reduce_sum.128), calls=%async_computation.2 | async-start | bytes 4194304 | tf_op jit(solution)/shard_map/all_to_all | solution.py:110
  197.9 0.6 reduce-scatter.5.cloned.1.call-update
  198.4 1.3 slice.213
  199.7 1.3 copy.236
  201.0 1.1 fusion.89
  202.1 0.9 copy.238
  203.0 0.8 copy.237
  203.8 19.0 %all-to-all-done.2 = bf16[4,128,2048]{2,1,0:T(8,128)(2,1)} async-done(((bf16[4,128,2048]{2,1,0:T(8,128)(2,1)}), bf16[4,128,2048]{2,1,0:T(8,128)(2,1)}, u32[]{:S(2)}, u32[]{:S(2)}) %all-to-all-start.2) | async-done | bytes 2097184 | tf_op jit(solution)/shard_map/all_to_all | solution.py:110
  222.8 2.9 %reduce_sum.129 = bf16[128,2048]{1,0:T(8,128)(2,1)} reduce(bf16[4,128,2048]{2,1,0:T(8,128)(2,1)} %all-to-all-done.2, bf16[]{:T(256)} %constant.24.clone.1), dimensions={0}, to_apply=%region_12.13 | reduce | flops 786432 | bytes 2621442 | tf_op jit(solution)/shard_map/reduce_sum | solution.py:111
  225.7 1.1 reduce-scatter.5.cloned.1.call-done
  (157 shorter events, 11.9 us)
Async XLA Ops:
  7.2 110.0 %copy-start = (bf16[512,2048]{1,0:T(8,128)(2,1)S(1)}, bf16[512,2048]{1,0:T(8,128)(2,1)}, u32[]{:S(2)}) copy-start(bf16[512,2048]{1,0:T(8,128)(2,1)} %param.10) | copy-start | bytes 6291460
  7.2 69.3 %all-gather.4.cloned.1.call-start = ((), (), s32[]{:S(2)}) async-start(), calls=%async_computation.6 | async-start | bytes 2621440 | tf_op jit(solution)/shard_map/all_gather | solution.py:112
  43.6 32.9 %copy-start.51 = (s32[1,16]{1,0:T(1,128)S(1)}, s32[1,16]{1,0:T(1,128)}, u32[]{:S(2)}) copy-start(s32[1,16]{1,0:T(1,128)} %param.12) | copy-start | bytes 196
  43.7 32.9 %copy-start.52 = (s32[1,16]{1,0:T(1,128)S(1)}, s32[1,16]{1,0:T(1,128)}, u32[]{:S(2)}) copy-start(s32[1,16]{1,0:T(1,128)} %param.13) | copy-start | bytes 196
  43.7 54.6 %all-gather.6.cloned.1.call-start = ((), (), s32[]{:S(2)}) async-start(), calls=%async_computation.9 | async-start | bytes 6291456 | tf_op jit(solution)/shard_map/all_gather | solution.py:113
  76.5 121.4 %reduce-scatter.3.cloned.1.call-start = ((), (), s32[]{:S(2)}) async-start(), calls=%async_computation.7 | async-start | bytes 4718592 | tf_op jit(solution)/shard_map/reduce_scatter | solution.py:176
  77.3 48.4 %copy-start.25 = (pred[256,512]{0,1:T(8,128)(4,1)}, pred[256,512]{0,1:T(8,128)(4,1)S(1)}, u32[]{:S(2)}) copy-start(pred[256,512]{0,1:T(8,128)(4,1)S(1)} %compare_and_fusion.1) | copy-start | bytes 393220
  77.6 2.7 %copy-start.30 = (pred[256,512]{0,1:T(8,128)(4,1)}, pred[256,512]{0,1:T(8,128)(4,1)S(1)}, u32[]{:S(2)}) copy-start(pred[256,512]{0,1:T(8,128)(4,1)S(1)} %get-tuple-element.55) | copy-start | bytes 393220
  77.7 50.6 %copy-start.27 = (pred[256,512]{0,1:T(8,128)(4,1)}, pred[256,512]{0,1:T(8,128)(4,1)S(1)}, u32[]{:S(2)}) copy-start(pred[256,512]{0,1:T(8,128)(4,1)S(1)} %get-tuple-element.54) | copy-start | bytes 393220
  79.3 3.9 %copy-start.1 = (bf16[8,128,6,128]{3,1,0,2:T(8,128)(2,1)}, bf16[8,128,6,128]{3,1,0,2:T(8,128)(2,1)S(1)}, u32[]{:S(2)}) copy-start(bf16[8,128,6,128]{3,1,0,2:T(8,128)(2,1)S(1)} %copy.195) | copy-start | bytes 4718596
  79.6 61.7 %copy-start.5 = (f32[1,4,256,256]{2,3,1,0:T(8,128)}, f32[1,4,256,256]{2,3,1,0:T(8,128)S(1)}, u32[]{:S(2)}) copy-start(f32[1,4,256,256]{2,3,1,0:T(8,128)S(1)} %get-tuple-element.45) | copy-start | bytes 3145732
  83.1 42.6 %copy-start.46 = (f32[4,256]{1,0:T(4,128)}, f32[4,256]{1,0:T(4,128)S(1)}, u32[]{:S(2)}) copy-start(f32[4,256]{1,0:T(4,128)S(1)} %fusion.21) | copy-start | bytes 12292
  85.7 42.5 %copy-start.48 = (f32[4,256]{1,0:T(4,128)}, f32[4,256]{1,0:T(4,128)S(1)}, u32[]{:S(2)}) copy-start(f32[4,256]{1,0:T(4,128)S(1)} %fusion.19) | copy-start | bytes 12292
  121.8 2.2 copy-start.34
  121.8 2.2 copy-start.42
  121.8 4.0 %copy-start.40 = (bf16[256,512]{0,1:T(8,128)(2,1)}, bf16[256,512]{0,1:T(8,128)(2,1)S(1)}, u32[]{:S(2)}) copy-start(bf16[256,512]{0,1:T(8,128)(2,1)S(1)} %get-tuple-element.28) | copy-start | bytes 786436
  121.8 6.4 %copy-start.37 = (bf16[256,512]{0,1:T(8,128)(2,1)}, bf16[256,512]{0,1:T(8,128)(2,1)S(1)}, u32[]{:S(2)}) copy-start(bf16[256,512]{0,1:T(8,128)(2,1)S(1)} %get-tuple-element.29) | copy-start | bytes 786436
  121.8 2.1 copy-start.19
  121.8 2.1 copy-start.31
  123.9 1.9 copy-start.12
  125.8 2.4 %copy-start.15 = (f32[512,256,4]{1,0,2:T(8,128)S(1)}, f32[512,256,4]{1,0,2:T(8,128)}, u32[]{:S(2)}) copy-start(f32[512,256,4]{1,0,2:T(8,128)} %copy-done.14) | copy-start | bytes 6291460
  128.2 2.6 %copy-start.4 = (bf16[1024,2048]{0,1:T(8,128)(2,1)S(1)}, bf16[1024,2048]{0,1:T(8,128)(2,1)}, u32[]{:S(2)}) copy-start(bf16[1024,2048]{0,1:T(8,128)(2,1)} %reshape.439) | copy-start | bytes 12582916
  130.8 2.4 %copy-start.23 = (bf16[1024,1,4,128]{0,3,2,1:T(8,128)(2,1)}, bf16[1024,1,4,128]{0,3,2,1:T(8,128)(2,1)S(1)}, u32[]{:S(2)}) copy-start(bf16[1024,1,4,128]{0,3,2,1:T(8,128)(2,1)S(1)} %pad_maximum_fusion.1) | copy-start | bytes 3145732
  136.6 3.3 %copy-start.2 = (bf16[8,128,6,128]{3,1,0,2:T(8,128)(2,1)S(1)}, bf16[8,128,6,128]{3,1,0,2:T(8,128)(2,1)}, u32[]{:S(2)}) copy-start(bf16[8,128,6,128]{3,1,0,2:T(8,128)(2,1)} %copy-done.1) | copy-start | bytes 4718596
  136.6 3.3 %copy-start.20 = (f32[512,256,4]{1,0,2:T(8,128)S(1)}, f32[512,256,4]{1,0,2:T(8,128)}, u32[]{:S(2)}) copy-start(f32[512,256,4]{1,0,2:T(8,128)} %copy-done.18) | copy-start | bytes 6291460
  136.6 3.3 %copy-start.43 = (bf16[256,512]{0,1:T(8,128)(2,1)S(1)}, bf16[256,512]{0,1:T(8,128)(2,1)}, u32[]{:S(2)}) copy-start(bf16[256,512]{0,1:T(8,128)(2,1)} %copy-done.42) | copy-start | bytes 786436
  141.8 1.8 copy-start.13
  141.8 1.8 copy-start.26
  141.8 1.8 copy-start.47
  141.8 1.8 copy-start.54
  143.6 1.6 copy-start.16
  143.6 1.6 copy-start.28
  143.6 1.6 copy-start.38
  143.6 1.6 copy-start.49
  143.6 1.6 copy-start.55
  144.5 1.6 copy-start.7
  152.5 14.3 %all-to-all-start.1 = ((bf16[2,4,128,2048]{3,2,1,0:T(8,128)(2,1)}), bf16[2,4,128,2048]{3,2,1,0:T(8,128)(2,1)}, u32[]{:S(2)}, u32[]{:S(2)}) async-start(bf16[2,4,128,2048]{3,2,1,0:T(8,128)(2,1)} %bitcast.431), calls=%async_computation.1 | async-start | bytes 8388608 | tf_op jit(solution)/shard_map/all_to_all | solution.py:108
  158.1 2.7 %copy-start.17 = (f32[512,256,4]{1,0,2:T(8,128)S(1)}, f32[512,256,4]{1,0,2:T(8,128)}, u32[]{:S(2)}) copy-start(f32[512,256,4]{1,0,2:T(8,128)} %copy-done.14) | copy-start | bytes 6291460
  158.1 2.7 %copy-start.29 = (pred[256,512]{0,1:T(8,128)(4,1)S(1)}, pred[256,512]{0,1:T(8,128)(4,1)}, u32[]{:S(2)}) copy-start(pred[256,512]{0,1:T(8,128)(4,1)} %copy-done.27) | copy-start | bytes 393220
  158.1 2.7 %copy-start.39 = (bf16[256,512]{0,1:T(8,128)(2,1)S(1)}, bf16[256,512]{0,1:T(8,128)(2,1)}, u32[]{:S(2)}) copy-start(bf16[256,512]{0,1:T(8,128)(2,1)} %copy-done.37) | copy-start | bytes 786436
  158.2 2.7 %copy-start.50 = (f32[4,256]{1,0:T(4,128)S(1)}, f32[4,256]{1,0:T(4,128)}, u32[]{:S(2)}) copy-start(f32[4,256]{1,0:T(4,128)} %copy-done.48) | copy-start | bytes 12292
  162.2 1.5 copy-start.3
  162.2 1.8 copy-start.8
  162.6 1.8 copy-start.10
  163.0 1.9 copy-start.22
  166.7 25.3 %all-to-all-start.3 = ((bf16[8,128,6,128]{1,3,2,0:T(8,128)(2,1)}), bf16[8,128,6,128]{1,3,2,0:T(8,128)(2,1)}, u32[]{:S(2)}, u32[]{:S(2)}) async-start(bf16[8,128,6,128]{1,3,2,0:T(8,128)(2,1)} %pad_maximum_fusion), calls=%async_computation.3 | async-start | bytes 3145728 | tf_op jit(solution)/shard_map/all_to_all | solution.py:163
  192.0 30.8 %all-to-all-start.2 = ((bf16[4,128,2048]{2,1,0:T(8,128)(2,1)}), bf16[4,128,2048]{2,1,0:T(8,128)(2,1)}, u32[]{:S(2)}, u32[]{:S(2)}) async-start(bf16[4,128,2048]{2,1,0:T(8,128)(2,1)} %reduce_sum.128), calls=%async_computation.2 | async-start | bytes 4194304 | tf_op jit(solution)/shard_map/all_to_all | solution.py:110
  197.9 28.9 %reduce-scatter.5.cloned.1.call-start = ((), (), s32[]{:S(2)}) async-start(), calls=%async_computation.8 | async-start | bytes 655360 | tf_op jit(solution)/shard_map/reduce_scatter | solution.py:177
  (15 other events, 17.1 us)
Sparse Core Ops, SparseCore 0:
  43.8 32.5 all-gather.3
  78.2 19.9 all-gather.5
  135.9 56.6 reduce-scatter.2
  201.4 25.3 reduce-scatter.4

commit v4 on v2

--- a/solution.py
+++ b/solution.py
@@ -36,20 +36,26 @@
     hq = QUERY_HEADS // seq_count
     hk = KEY_VALUE_HEADS // seq_count
     group_width = hq // hk
-    packed = jnp.concatenate(
-        [
-            queries.reshape(tok, seq_count, hq, HEAD_SIZE),
-            rotated_key_matrix.reshape(tok, seq_count, hk, HEAD_SIZE),
-            value_matrix.reshape(tok, seq_count, hk, HEAD_SIZE),
-        ],
-        axis=2,
-    ).transpose(1, 0, 2, 3)
-    got = lax.all_to_all(packed, "seq", split_axis=0, concat_axis=0, tiled=True)
     win_rows = seq_count * tok
-    got = got.reshape(win_rows, hq + 2 * hk, HEAD_SIZE)
-    query_head_rows = got[:, :hq].reshape(win_rows, hk, group_width, HEAD_SIZE)
-    k_loc = got[:, hq : hq + hk]
-    v_loc = got[:, hq + hk :]
+    query_head_rows, k_loc, v_loc = (
+        lax.all_to_all(
+            queries.reshape(tok, QUERY_HEADS, HEAD_SIZE), "seq", split_axis=1, concat_axis=0, tiled=True
+        ).reshape(win_rows, hk, group_width, HEAD_SIZE),
+        lax.all_to_all(
+            rotated_key_matrix.reshape(tok, KEY_VALUE_HEADS, HEAD_SIZE),
+            "seq",
+            split_axis=1,
+            concat_axis=0,
+            tiled=True,
+        ),
+        lax.all_to_all(
+            value_matrix.reshape(tok, KEY_VALUE_HEADS, HEAD_SIZE),
+            "seq",
+            split_axis=1,
+            concat_axis=0,
+            tiled=True,
+        ),
+    )
     starts = row_starts(lengths[0], pack_order[0], win_rows)
     blk = min(BLOCK, win_rows)
     blk_count = win_rows // blk
@@ -144,14 +150,14 @@
     dq_all = jnp.concatenate(dq_blocks, axis=0).reshape(win_rows, hq, HEAD_SIZE)
     dk_all = jnp.concatenate(dk_blocks, axis=0).astype(jnp.bfloat16)
     dv_all = jnp.concatenate(dv_blocks, axis=0).astype(jnp.bfloat16)
-    packed_out = jnp.concatenate([dq_all, dk_all, dv_all], axis=1).reshape(
-        seq_count, tok, hq + 2 * hk, HEAD_SIZE
-    )
-    back = lax.all_to_all(packed_out, "seq", split_axis=0, concat_axis=0, tiled=True)
-    back = back.transpose(1, 0, 2, 3)
-    d_q = back[:, :, :hq].reshape(1, tok, QUERY_HEADS * HEAD_SIZE)
-    key_gradient = back[:, :, hq : hq + hk].reshape(1, tok, KEY_VALUE_HEADS * HEAD_SIZE)
-    value_gradient = back[:, :, hq + hk :].reshape(1, tok, KEY_VALUE_HEADS * HEAD_SIZE)
+    d_q, key_gradient, value_gradient = (
+        lax.all_to_all(dq_all, "seq", split_axis=0, concat_axis=1, tiled=True),
+        lax.all_to_all(dk_all, "seq", split_axis=0, concat_axis=1, tiled=True),
+        lax.all_to_all(dv_all, "seq", split_axis=0, concat_axis=1, tiled=True),
+    )
+    d_q = d_q.reshape(1, tok, QUERY_HEADS * HEAD_SIZE)
+    key_gradient = key_gradient.reshape(1, tok, KEY_VALUE_HEADS * HEAD_SIZE)
+    value_gradient = value_gradient.reshape(1, tok, KEY_VALUE_HEADS * HEAD_SIZE)
     y_count = lax.psum(1, "dpy")
     z_count = lax.psum(1, "dpz")
     cols = wo_grad.shape[1]

time: 205 us -> 243 us (1.19)
  local copies, waits for them, and re-layouts: 31.8 us -> 60.7 us
  waiting for transfers between devices: 94 us -> 67.2 us
  starting transfers between devices: 18.6 us -> 36.1 us
  matrix products: 33 us -> 42.1 us
  other arithmetic: 11.1 us -> 19.2 us
    all_to_all x2 -> x6, waiting for transfers between devices: 50.4 us -> 32.4 us  [the longest x1 11.6 us: local(): lax.all_to_all(queries.reshape(tok, QUERY_HEADS, HEAD_SIZE), 'seq', split...]
    all_to_all x2 -> x6, starting transfers between devices: 12.6 us -> 30.2 us  [the longest x1 5.56 us: local(): lax.all_to_all(rotated_key_matrix.reshape(tok, KEY_VALUE_HEADS, HEAD_SIZE...]
    reduce_scatter x1, waiting for transfers between devices: 11.9 us -> 0.01 us  [local(): wo_perm = lax.psum_scatter(wo_perm, 'dpz', scatter_dimension=1, tiled=True)]
    convert_element_type x0 -> x4, local copies, waits for them, and re-layouts: none -> 7.57 us  [local(): g_blk.astype(jnp.float32) * o_blk.astype(jnp.float32)]
    unnamed x73 -> x144, local copies, waits for them, and re-layouts: 14.9 us -> 22.5 us
    reshape x0 -> x4, local copies, waits for them, and re-layouts: none -> 5.89 us  [the longest x1 2.61 us: local(): d_q = d_q.reshape(1, tok, QUERY_HEADS * HEAD_SIZE)]
    dot_general x4, matrix products: 1.23 us -> 4.96 us  [local(): jnp.einsum('kgqs,skd->qkgd', score_gradient, k_band, preferred_element_ty...]
    slice x2 -> x9, local copies, waits for them, and re-layouts: 2.36 us -> 6.05 us  [the longest x2 3.25 us: local(): v_loc[k_start:k_end]]
  transfers between devices with their start and end apart: 6 -> 10, of which waited for: 4 -> 6; matrix products, arithmetic and copies ran while one was open for 19% -> 32% of each run, Pallas kernels for 0% -> 0%
where the time goes in v4:
time: 243 us; the launch traced here: 240 us
  waiting for transfers between devices  67.2 us (28%)
  local copies, waits for them, and re-layouts  60.7 us (25%)
  matrix products  42.1 us (17%)
  starting transfers between devices  36.1 us (15%)
  other arithmetic  19.2 us (8%)
  between operations  14.5 us (6%)
    all_to_all x1, waiting for transfers between devices, local(): lax.all_to_all(pieces, 'seq', split_axis=0, concat_axis=0, tiled=True)  33.4 us
    unnamed x144, local copies, waits for them, and re-layouts  22.5 us
    all_to_all x1, waiting for transfers between devices, local(): lax.all_to_all(queries.reshape(tok, QUERY_HEADS, HEAD_SIZE), 'seq', split...  11.6 us
    all_to_all x1, waiting for transfers between devices, local(): lax.all_to_all(dq_all, 'seq', split_axis=0, concat_axis=1, tiled=True)  8.85 us
    convert_element_type x4, local copies, waits for them, and re-layouts, local(): g_blk.astype(jnp.float32) * o_blk.astype(jnp.float32)  7.57 us
    dot_general x1, local copies, waits for them, and re-layouts, local(): lax.dot_general(a_head, incoming, (((0,), (0,)), ((), ())), preferred_ele...  6.49 us
    dot_general x4, matrix products, local(): jnp.einsum('kgqs,qkgd->skd', attn_prob.astype(jnp.bfloat16), g_blk, prefe...  6.26 us
    all_to_all x1, waiting for transfers between devices, local(): lax.all_to_all(value_matrix.reshape(tok, KEY_VALUE_HEADS, HEAD_SIZE), 'se...  6.16 us
  transfers between devices with their start and end apart: 10, of which 6 were waited for; matrix products, arithmetic and copies ran while one was open for 32% of the time, Pallas kernels for 0%

profile of v4, /device:TPU:2, one launch (start us, length us, event | category | flops | bytes accessed | tf_op | source)
XLA Modules:
  0.0 239.7 jit_solution(17634503356803067582)
XLA Ops:
  9.7 5.6 %all-to-all-start = ((bf16[128,8,128]{2,0,1:T(8,128)(2,1)}), bf16[128,8,128]{2,0,1:T(8,128)(2,1)S(1)}, u32[]{:S(2)}, u32[]{:S(2)}) async-start(bf16[128,8,128]{2,0,1:T(8,128)(2,1)} %copy.247), calls=%async_computation | async-start | bytes 524288 | tf_op jit(solution)/shard_map/all_to_all | solution.py:44
  17.2 4.2 %all-to-all-done = bf16[128,8,128]{2,0,1:T(8,128)(2,1)S(1)} async-done(((bf16[128,8,128]{2,0,1:T(8,128)(2,1)}), bf16[128,8,128]{2,0,1:T(8,128)(2,1)S(1)}, u32[]{:S(2)}, u32[]{:S(2)}) %all-to-all-start) | async-done | bytes 262176 | tf_op jit(solution)/shard_map/all_to_all | solution.py:44
  21.3 4.8 %all-to-all-start.2 = ((bf16[128,8,128]{2,0,1:T(8,128)(2,1)}), bf16[128,8,128]{2,0,1:T(8,128)(2,1)S(1)}, u32[]{:S(2)}, u32[]{:S(2)}) async-start(bf16[128,8,128]{2,0,1:T(8,128)(2,1)} %copy.251), calls=%async_computation.2 | async-start | bytes 524288 | tf_op jit(solution)/shard_map/all_to_all | solution.py:51
  26.7 2.3 copy.248
  29.1 6.2 %all-to-all-done.2 = bf16[128,8,128]{2,0,1:T(8,128)(2,1)S(1)} async-done(((bf16[128,8,128]{2,0,1:T(8,128)(2,1)}), bf16[128,8,128]{2,0,1:T(8,128)(2,1)S(1)}, u32[]{:S(2)}, u32[]{:S(2)}) %all-to-all-start.2) | async-done | bytes 262176 | tf_op jit(solution)/shard_map/all_to_all | solution.py:51
  36.0 5.0 %all-to-all-start.1 = ((bf16[128,32,128]{0,2,1:T(8,128)(2,1)}), bf16[128,32,128]{0,2,1:T(8,128)(2,1)S(1)}, u32[]{:S(2)}, u32[]{:S(2)}) async-start(bf16[128,32,128]{0,2,1:T(8,128)(2,1)} %bitcast.7), calls=%async_computation.1 | async-start | bytes 2097152 | tf_op jit(solution)/shard_map/all_to_all | solution.py:41
  41.6 1.6 fusion.63
  43.9 1.5 slice.168
  46.2 1.8 fusion.82
  47.9 11.6 %all-to-all-done.1 = bf16[128,32,128]{0,2,1:T(8,128)(2,1)S(1)} async-done(((bf16[128,32,128]{0,2,1:T(8,128)(2,1)}), bf16[128,32,128]{0,2,1:T(8,128)(2,1)S(1)}, u32[]{:S(2)}, u32[]{:S(2)}) %all-to-all-start.1) | async-done | bytes 1048608 | tf_op jit(solution)/shard_map/all_to_all | solution.py:41
  68.2 1.4 copy-done.7
  70.7 4.5 %fusion.26 = bf16[1024,512]{0,1:T(8,128)(2,1)S(1)} fusion(bf16[512,2048]{1,0:T(8,128)(2,1)S(1)} %copy-done, bf16[1,1024,2048]{2,1,0:T(8,128)(2,1)} %all-gather.3.cloned.1.call-done), kind=kOutput, calls=%fused_computation.37 | convolution fusion | flops 2148007936 | bytes 7340032 | tf_op jit(solution)/shard_map/dot_general | solution.py:111
  76.2 1.9 copy.266
  78.1 1.9 copy.270
  80.0 1.9 copy.274
  81.9 1.9 copy.262
  83.8 2.6 %convolution_bitcast_fusion.2 = f32[512,1,128]{0,2,1:T(8,128)S(1)} fusion(bf16[256,4,128]{0,2,1:T(8,128)(2,1)} %bitcast.482, f32[4,256]{1,0:T(4,128)} %fusion.25, f32[4,256]{1,0:T(4,128)S(1)} %get-tuple-element.37, f32[512,256,4]{1,0,2:T(8,128)} %copy-done.7, pred[256,512]{0,1:T(8,128)(4,1)} %get-tuple-element.54), kind=kOutput, calls=%fused_computation.65 | convolution fusion | flops 136839168 | bytes 2760704 | tf_op jit(solution)/shard_map/kgqs,qkgd->skd/dot_general | solution.py:139
  87.5 1.8 fusion.31
  91.8 1.6 multiply_reduce_fusion.2
  93.5 1.6 multiply_reduce_fusion.1
  96.1 2.3 copy.259
  98.4 6.5 %copy.286 = bf16[2048,1024]{1,0:T(8,128)(2,1)} copy(bf16[2048,1024]{0,1:T(8,128)(2,1)} %bitcast.441) | data formatting | bytes 8388608 | tf_op jit(solution)/shard_map/dot_general | solution.py:108
  104.8 4.9 %convolution_bitcast_fusion = f32[512,8,4,64]{0,3,1,2:T(8,128)S(1)} fusion(bf16[1024,512,1,1]{0,1,3,2:T(8,128)(2,1)} %bitcast.466, bf16[4,8,64,1024]{3,2,1,0:T(8,128)(2,1)} %bitcast.443), kind=kOutput, calls=%fused_computation.3 | convolution fusion | flops 2147483648 | bytes 9437184 | tf_op jit(solution)/shard_map/dot_general | solution.py:108
  109.7 2.6 %copy.288 = f32[512,8,4,64]{0,3,2,1:T(8,128)} copy(f32[512,8,4,64]{0,3,1,2:T(8,128)S(1)} %convolution_bitcast_fusion) | data formatting | bytes 8388608 | tf_op jit(solution)/shard_map/transpose | solution.py:166
  112.3 1.7 convolution_bitcast_fusion.5
  114.8 2.5 %convolution_bitcast_fusion.4 = f32[512,1,128]{0,2,1:T(8,128)S(1)} fusion(bf16[256,4,128]{0,2,1:T(8,128)(2,1)} %bitcast.479, f32[4,256]{1,0:T(4,128)S(1)} %copy-done.60, f32[4,256]{1,0:T(4,128)S(1)} %get-tuple-element.41, f32[512,256,4]{1,0,2:T(8,128)} %copy-done.5, pred[256,512]{0,1:T(8,128)(4,1)} %get-tuple-element.53), kind=kOutput, calls=%fused_computation.67 | convolution fusion | flops 136839168 | bytes 2760704 | tf_op jit(solution)/shard_map/kgqs,qkgd->skd/dot_general | solution.py:139
  120.5 2.4 reduce.15
  122.9 1.8 copy.318
  124.7 1.7 reshape.567
  126.4 5.1 %all-to-all-start.6 = ((bf16[8,2,8192]{2,1,0:T(2,128)(2,1)}), bf16[8,2,8192]{2,1,0:T(2,128)(2,1)}, u32[]{:S(2)}, u32[]{:S(2)}) async-start(bf16[8,2,8192]{2,1,0:T(2,128)(2,1)} %reshape.567), calls=%async_computation.6 | async-start | bytes 524288 | tf_op jit(solution)/shard_map/all_to_all | solution.py:156
  131.6 2.8 %fusion.29 = bf16[4,256,512]{1,2,0:T(8,128)(2,1)S(1)} fusion(bf16[512,128,1]{1,0,2:T(8,128)(2,1)} %bitcast.491, bf16[256,4,128]{0,2,1:T(8,128)(2,1)} %bitcast.480, f32[4,256]{1,0:T(4,128)} %bitcast.502, f32[4,256]{1,0:T(4,128)} %fusion.21, f32[4,256]{1,0:T(4,128)S(1)} %get-tuple-element.41, f32[512,256,4]{1,0,2:T(8,128)} %copy-done.5, ...), kind=kOutput, calls=%fused_computation.38 | convolution fusion | flops 138412032 | bytes 3682304 | tf_op jit(solution)/shard_map/qkgd,skd->kgqs/dot_general | solution.py:129
  140.4 1.5 reduce.14
  141.9 1.8 reshape.565
  144.8 4.8 %all-to-all-start.5 = ((bf16[8,2,8192]{2,1,0:T(2,128)(2,1)}), bf16[8,2,8192]{2,1,0:T(2,128)(2,1)S(1)}, u32[]{:S(2)}, u32[]{:S(2)}) async-start(bf16[8,2,8192]{2,1,0:T(2,128)(2,1)} %reshape.565), calls=%async_computation.5 | async-start | bytes 524288 | tf_op jit(solution)/shard_map/all_to_all | solution.py:155
  149.6 1.4 fusion.39
  152.2 1.8 copy.276
  154.0 1.7 all-to-all-done.5
  155.7 4.9 %all-to-all-start.4 = ((bf16[1024,4,128]{2,1,0:T(4,128)(2,1)}), bf16[1024,4,128]{2,1,0:T(4,128)(2,1)S(1)}, u32[]{:S(2)}, u32[]{:S(2)}) async-start(bf16[1024,4,128]{2,1,0:T(4,128)(2,1)} %copy.276), calls=%async_computation.4 | async-start | bytes 2097152 | tf_op jit(solution)/shard_map/all_to_all | solution.py:154
  160.6 5.7 %convolution_convert_fusion = bf16[1024,2048]{1,0:T(8,128)(2,1)} fusion(bf16[1024,512]{0,1:T(8,128)(2,1)} %bitcast.467, bf16[512,2048]{1,0:T(8,128)(2,1)S(1)} %copy-done), kind=kOutput, calls=%fused_computation.2 | convolution fusion | flops 2149580800 | bytes 7340032 | tf_op jit(solution)/shard_map/dot_general | solution.py:103
  166.3 8.8 %all-to-all-done.4 = bf16[1024,4,128]{2,1,0:T(4,128)(2,1)S(1)} async-done(((bf16[1024,4,128]{2,1,0:T(4,128)(2,1)}), bf16[1024,4,128]{2,1,0:T(4,128)(2,1)S(1)}, u32[]{:S(2)}, u32[]{:S(2)}) %all-to-all-start.4) | async-done | bytes 1048608 | tf_op jit(solution)/shard_map/all_to_all | solution.py:154
  175.1 5.9 %all-to-all-start.3 = ((bf16[8,128,2048]{2,1,0:T(8,128)(2,1)}), bf16[8,128,2048]{2,1,0:T(8,128)(2,1)}, u32[]{:S(2)}, u32[]{:S(2)}) async-start(bf16[8,128,2048]{2,1,0:T(8,128)(2,1)} %bitcast.442), calls=%async_computation.3 | async-start | bytes 8388608 | tf_op jit(solution)/shard_map/all_to_all | solution.py:105
  184.7 1.8 copy.289
  186.5 1.9 reshape.568
  190.3 1.8 copy.290
  192.1 1.4 copy.277
  193.4 2.6 %reshape.538 = bf16[1,128,4096]{2,1,0:T(8,128)(2,1)} reshape(bf16[128,8,4,128]{3,2,1,0:T(4,128)(2,1)} %copy.277) | data formatting | bytes 2097152 | tf_op jit(solution)/shard_map/reshape | solution.py:158
  196.0 33.4 %all-to-all-done.3 = bf16[8,128,2048]{2,1,0:T(8,128)(2,1)} async-done(((bf16[8,128,2048]{2,1,0:T(8,128)(2,1)}), bf16[8,128,2048]{2,1,0:T(8,128)(2,1)}, u32[]{:S(2)}, u32[]{:S(2)}) %all-to-all-start.3) | async-done | bytes 4194336 | tf_op jit(solution)/shard_map/all_to_all | solution.py:105
  229.4 3.8 %reduce_sum.116 = bf16[128,2048]{1,0:T(8,128)(2,1)} reduce(bf16[8,128,2048]{2,1,0:T(8,128)(2,1)} %all-to-all-done.3, bf16[]{:T(256)} %constant.8.clone.1), dimensions={0}, to_apply=%region_11.12 | reduce | flops 1835008 | bytes 4718594 | tf_op jit(solution)/shard_map/reduce_sum | solution.py:106
  (201 shorter events, 40.8 us)
Async XLA Ops:
  7.2 63.5 %copy-start = (bf16[512,2048]{1,0:T(8,128)(2,1)S(1)}, bf16[512,2048]{1,0:T(8,128)(2,1)}, u32[]{:S(2)}) copy-start(bf16[512,2048]{1,0:T(8,128)(2,1)} %param.10) | copy-start | bytes 6291460
  7.2 8.1 %copy-start.63 = (s32[1,16]{1,0:T(1,128)S(1)}, s32[1,16]{1,0:T(1,128)}, u32[]{:S(2)}) copy-start(s32[1,16]{1,0:T(1,128)} %param.13) | copy-start | bytes 196
  7.2 8.1 %copy-start.62 = (s32[1,16]{1,0:T(1,128)S(1)}, s32[1,16]{1,0:T(1,128)}, u32[]{:S(2)}) copy-start(s32[1,16]{1,0:T(1,128)} %param.12) | copy-start | bytes 196
  7.2 9.2 %copy-start.44 = (bf16[1,128,1024]{2,1,0:T(8,128)(2,1)S(1)}, bf16[1,128,1024]{2,1,0:T(8,128)(2,1)}, u32[]{:S(2)}) copy-start(bf16[1,128,1024]{2,1,0:T(8,128)(2,1)} %param.9) | copy-start | bytes 786436
  7.2 63.4 %all-gather.3.cloned.1.call-start = ((), (), s32[]{:S(2)}) async-start(), calls=%async_computation.11 | async-start | bytes 4718592 | tf_op jit(solution)/shard_map/all_gather | solution.py:107
  9.7 11.6 %all-to-all-start = ((bf16[128,8,128]{2,0,1:T(8,128)(2,1)}), bf16[128,8,128]{2,0,1:T(8,128)(2,1)S(1)}, u32[]{:S(2)}, u32[]{:S(2)}) async-start(bf16[128,8,128]{2,0,1:T(8,128)(2,1)} %copy.247), calls=%async_computation | async-start | bytes 524288 | tf_op jit(solution)/shard_map/all_to_all | solution.py:44
  21.3 13.9 %all-to-all-start.2 = ((bf16[128,8,128]{2,0,1:T(8,128)(2,1)}), bf16[128,8,128]{2,0,1:T(8,128)(2,1)S(1)}, u32[]{:S(2)}, u32[]{:S(2)}) async-start(bf16[128,8,128]{2,0,1:T(8,128)(2,1)} %copy.251), calls=%async_computation.2 | async-start | bytes 524288 | tf_op jit(solution)/shard_map/all_to_all | solution.py:51
  36.0 23.6 %all-to-all-start.1 = ((bf16[128,32,128]{0,2,1:T(8,128)(2,1)}), bf16[128,32,128]{0,2,1:T(8,128)(2,1)S(1)}, u32[]{:S(2)}, u32[]{:S(2)}) async-start(bf16[128,32,128]{0,2,1:T(8,128)(2,1)} %bitcast.7), calls=%async_computation.1 | async-start | bytes 2097152 | tf_op jit(solution)/shard_map/all_to_all | solution.py:41
  41.0 140.1 %reduce-scatter.3.cloned.1.call-start = ((), (), s32[]{:S(2)}) async-start(), calls=%async_computation.9 | async-start | bytes 4718592 | tf_op jit(solution)/shard_map/reduce_scatter | solution.py:169
  60.8 2.1 copy-start.34
  60.9 2.1 copy-start.38
  62.2 1.8 copy-start.17
  62.2 1.8 copy-start.25
  62.3 5.5 %copy-start.12 = (bf16[2,128,4,128]{3,1,0,2:T(8,128)(2,1)}, bf16[2,128,4,128]{3,1,0,2:T(8,128)(2,1)S(1)}, u32[]{:S(2)}) copy-start(bf16[2,128,4,128]{3,1,0,2:T(8,128)(2,1)S(1)} %copy.257) | copy-start | bytes 786436
  62.3 2.2 copy-start.10
  64.1 1.9 copy-start.23
  66.0 1.8 copy-start.19
  66.0 1.8 copy-start.21
  66.5 1.8 copy-start.1
  83.8 2.6 %copy-start.8 = (f32[512,256,4]{1,0,2:T(8,128)S(1)}, f32[512,256,4]{1,0,2:T(8,128)}, u32[]{:S(2)}) copy-start(f32[512,256,4]{1,0,2:T(8,128)} %copy-done.7) | copy-start | bytes 6291460
  83.8 2.6 %copy-start.20 = (pred[256,512]{0,1:T(8,128)(4,1)S(1)}, pred[256,512]{0,1:T(8,128)(4,1)}, u32[]{:S(2)}) copy-start(pred[256,512]{0,1:T(8,128)(4,1)} %get-tuple-element.54) | copy-start | bytes 393220
  83.8 2.6 %copy-start.43 = (f32[256,1,4,128]{3,0,2,1:T(8,128)S(1)}, f32[256,1,4,128]{3,0,2,1:T(8,128)}, u32[]{:S(2)}) copy-start(f32[256,1,4,128]{3,0,2,1:T(8,128)} %copy.274) | copy-start | bytes 1572868
  83.8 2.6 %copy-start.52 = (bf16[4,128,1,128]{3,1,0,2:T(8,128)(2,1)S(1)}, bf16[4,128,1,128]{3,1,0,2:T(8,128)(2,1)}, u32[]{:S(2)}) copy-start(bf16[4,128,1,128]{3,1,0,2:T(8,128)(2,1)} %get-tuple-element.31) | copy-start | bytes 393220
  83.8 2.6 %copy-start.61 = (f32[4,256]{1,0:T(4,128)S(1)}, f32[4,256]{1,0:T(4,128)}, u32[]{:S(2)}) copy-start(f32[4,256]{1,0:T(4,128)} %fusion.25) | copy-start | bytes 12292
  86.4 2.9 %copy-start.47 = (f32[512,1,128]{0,2,1:T(8,128)}, f32[512,1,128]{0,2,1:T(8,128)S(1)}, u32[]{:S(2)}) copy-start(f32[512,1,128]{0,2,1:T(8,128)S(1)} %convolution_bitcast_fusion.2) | copy-start | bytes 786436
  87.5 2.5 %copy-start.35 = (pred[256,256]{0,1:T(8,128)(4,1)S(1)}, pred[256,256]{0,1:T(8,128)(4,1)}, u32[]{:S(2)}) copy-start(pred[256,256]{0,1:T(8,128)(4,1)} %fusion.66) | copy-start | bytes 196612
  87.5 2.5 %copy-start.42 = (f32[256,1,4,128]{3,0,2,1:T(8,128)S(1)}, f32[256,1,4,128]{3,0,2,1:T(8,128)}, u32[]{:S(2)}) copy-start(f32[256,1,4,128]{3,0,2,1:T(8,128)} %copy.262) | copy-start | bytes 1572868
  87.5 2.5 %copy-start.53 = (bf16[2,128,1,128]{3,1,0,2:T(8,128)(2,1)S(1)}, bf16[2,128,1,128]{3,1,0,2:T(8,128)(2,1)}, u32[]{:S(2)}) copy-start(bf16[2,128,1,128]{3,1,0,2:T(8,128)(2,1)} %slice.168) | copy-start | bytes 196612
  87.5 2.5 %copy-start.55 = (f32[4,256]{1,0:T(4,128)S(1)}, f32[4,256]{1,0:T(4,128)}, u32[]{:S(2)}) copy-start(f32[4,256]{1,0:T(4,128)} %fusion.60) | copy-start | bytes 12292
  114.8 2.5 %copy-start.3 = (f32[512,256,4]{1,0,2:T(8,128)S(1)}, f32[512,256,4]{1,0,2:T(8,128)}, u32[]{:S(2)}) copy-start(f32[512,256,4]{1,0,2:T(8,128)} %copy-done.1) | copy-start | bytes 6291460
  114.8 2.5 %copy-start.29 = (bf16[256,512]{0,1:T(8,128)(2,1)S(1)}, bf16[256,512]{0,1:T(8,128)(2,1)}, u32[]{:S(2)}) copy-start(bf16[256,512]{0,1:T(8,128)(2,1)} %get-tuple-element.17) | copy-start | bytes 786436
  114.8 2.5 %copy-start.58 = (f32[4,256]{1,0:T(4,128)S(1)}, f32[4,256]{1,0:T(4,128)}, u32[]{:S(2)}) copy-start(f32[4,256]{1,0:T(4,128)} %fusion.23) | copy-start | bytes 12292
  126.4 18.4 %all-to-all-start.6 = ((bf16[8,2,8192]{2,1,0:T(2,128)(2,1)}), bf16[8,2,8192]{2,1,0:T(2,128)(2,1)}, u32[]{:S(2)}, u32[]{:S(2)}) async-start(bf16[8,2,8192]{2,1,0:T(2,128)(2,1)} %reshape.567), calls=%async_computation.6 | async-start | bytes 524288 | tf_op jit(solution)/shard_map/all_to_all | solution.py:156
  131.5 2.8 %copy-start.26 = (bf16[4,128,1,128]{3,1,0,2:T(8,128)(2,1)S(1)}, bf16[4,128,1,128]{3,1,0,2:T(8,128)(2,1)}, u32[]{:S(2)}) copy-start(bf16[4,128,1,128]{3,1,0,2:T(8,128)(2,1)} %get-tuple-element.27) | copy-start | bytes 393220
  131.5 4.0 %copy-start.4 = (f32[512,256,4]{1,0,2:T(8,128)S(1)}, f32[512,256,4]{1,0,2:T(8,128)}, u32[]{:S(2)}) copy-start(f32[512,256,4]{1,0,2:T(8,128)} %copy-done.1) | copy-start | bytes 6291460
  131.5 4.0 %copy-start.30 = (bf16[256,512]{0,1:T(8,128)(2,1)S(1)}, bf16[256,512]{0,1:T(8,128)(2,1)}, u32[]{:S(2)}) copy-start(bf16[256,512]{0,1:T(8,128)(2,1)} %get-tuple-element.17) | copy-start | bytes 786436
  131.5 4.0 %copy-start.50 = (bf16[4,128,1,128]{3,1,0,2:T(8,128)(2,1)S(1)}, bf16[4,128,1,128]{3,1,0,2:T(8,128)(2,1)}, u32[]{:S(2)}) copy-start(bf16[4,128,1,128]{3,1,0,2:T(8,128)(2,1)} %get-tuple-element.32) | copy-start | bytes 393220
  131.5 4.0 %copy-start.59 = (f32[4,256]{1,0:T(4,128)S(1)}, f32[4,256]{1,0:T(4,128)}, u32[]{:S(2)}) copy-start(f32[4,256]{1,0:T(4,128)} %fusion.23) | copy-start | bytes 12292
  131.5 4.0 %copy-start.65 = (f32[256,4]{0,1:T(4,128)S(1)}, f32[256,4]{0,1:T(4,128)}, u32[]{:S(2)}) copy-start(f32[256,4]{0,1:T(4,128)} %get-tuple-element.47) | copy-start | bytes 12292
  135.5 2.1 copy-start.11
  136.4 2.1 copy-start.33
  139.6 4.0 %copy-start.9 = (bf16[4,256,512]{1,2,0:T(8,128)(2,1)S(1)}, bf16[4,256,512]{1,2,0:T(8,128)(2,1)}, u32[]{:S(2)}) copy-start(bf16[4,256,512]{1,2,0:T(8,128)(2,1)} %fusion.31) | copy-start | bytes 3145732
  139.6 4.0 %copy-start.22 = (bf16[4,128,1,128]{3,1,0,2:T(8,128)(2,1)S(1)}, bf16[4,128,1,128]{3,1,0,2:T(8,128)(2,1)}, u32[]{:S(2)}) copy-start(bf16[4,128,1,128]{3,1,0,2:T(8,128)(2,1)} %get-tuple-element.28) | copy-start | bytes 393220
  141.9 7.8 %copy-start.39 = (bf16[2,128,1,128]{3,1,0,2:T(8,128)(2,1)S(1)}, bf16[2,128,1,128]{3,1,0,2:T(8,128)(2,1)}, u32[]{:S(2)}) copy-start(bf16[2,128,1,128]{3,1,0,2:T(8,128)(2,1)} %slice.166) | copy-start | bytes 196612
  144.8 10.8 %all-to-all-start.5 = ((bf16[8,2,8192]{2,1,0:T(2,128)(2,1)}), bf16[8,2,8192]{2,1,0:T(2,128)(2,1)S(1)}, u32[]{:S(2)}, u32[]{:S(2)}) async-start(bf16[8,2,8192]{2,1,0:T(2,128)(2,1)} %reshape.565), calls=%async_computation.5 | async-start | bytes 524288 | tf_op jit(solution)/shard_map/all_to_all | solution.py:155
  155.7 19.4 %all-to-all-start.4 = ((bf16[1024,4,128]{2,1,0:T(4,128)(2,1)}), bf16[1024,4,128]{2,1,0:T(4,128)(2,1)S(1)}, u32[]{:S(2)}, u32[]{:S(2)}) async-start(bf16[1024,4,128]{2,1,0:T(4,128)(2,1)} %copy.276), calls=%async_computation.4 | async-start | bytes 2097152 | tf_op jit(solution)/shard_map/all_to_all | solution.py:154
  175.1 54.3 %all-to-all-start.3 = ((bf16[8,128,2048]{2,1,0:T(8,128)(2,1)}), bf16[8,128,2048]{2,1,0:T(8,128)(2,1)}, u32[]{:S(2)}, u32[]{:S(2)}) async-start(bf16[8,128,2048]{2,1,0:T(8,128)(2,1)} %bitcast.442), calls=%async_computation.3 | async-start | bytes 8388608 | tf_op jit(solution)/shard_map/all_to_all | solution.py:105
  181.0 52.2 %reduce-scatter.5.cloned.1.call-start = ((), (), s32[]{:S(2)}) async-start(), calls=%async_computation.10 | async-start | bytes 655360 | tf_op jit(solution)/shard_map/reduce_scatter | solution.py:170
  (28 other events, 34.0 us)
Sparse Core Ops, SparseCore 0:
  9.9 44.8 all-gather.2
  112.5 55.6 reduce-scatter.2
  184.9 25.5 reduce-scatter.4

commit v5 on v2

--- a/solution.py
+++ b/solution.py
@@ -96,8 +96,6 @@
     a_head = attn_out.reshape(win_rows, hq * HEAD_SIZE)
     product = jnp.dot(a_head, out_weight, preferred_element_type=jnp.float32)
     pieces = product.astype(jnp.bfloat16).reshape(seq_count, tok, product.shape[1])
-    pieces = lax.all_to_all(pieces, "seq", split_axis=0, concat_axis=0, tiled=True)
-    y_out = jnp.sum(pieces.astype(jnp.float32), axis=0).astype(jnp.bfloat16)
     incoming = lax.all_gather(out_grad.reshape(tok, out_grad.shape[2]), "seq", axis=0, tiled=True)
     wo_grad = lax.dot_general(
         a_head, incoming, (((0,), (0,)), ((), ())), preferred_element_type=jnp.float32
@@ -106,11 +104,15 @@
         incoming, out_weight, (((1,), (1,)), ((), ())), preferred_element_type=jnp.float32
     )
     attention_grad = d_rows.astype(jnp.bfloat16).reshape(win_rows, hk, group_width, HEAD_SIZE)
+    pieces, attention_grad = lax.optimization_barrier((pieces, attention_grad))
+    pieces = lax.all_to_all(pieces, "seq", split_axis=0, concat_axis=0, tiled=True)
 
     dq_blocks = []
     dk_blocks = [None] * blk_count
     dv_blocks = [None] * blk_count
     for i in range(blk_count):
+        if i == blk_count // 2:
+            pieces, attention_grad = lax.optimization_barrier((pieces, attention_grad))
         q_start, k_start, k_end = band(i)
         q_blk = query_head_rows[q_start : q_start + blk]
         g_blk = attention_grad[q_start : q_start + blk]
@@ -141,6 +143,7 @@
             for acc, part in ((dk_blocks, dk_part), (dv_blocks, dv_part)):
                 piece = part[lo : lo + blk]
                 acc[j] = piece if acc[j] is None else acc[j] + piece
+    y_out = jnp.sum(pieces.astype(jnp.float32), axis=0).astype(jnp.bfloat16)
     dq_all = jnp.concatenate(dq_blocks, axis=0).reshape(win_rows, hq, HEAD_SIZE)
     dk_all = jnp.concatenate(dk_blocks, axis=0).astype(jnp.bfloat16)
     dv_all = jnp.concatenate(dv_blocks, axis=0).astype(jnp.bfloat16)

time: 205 us -> 201 us (0.980)
  local copies, waits for them, and re-layouts: 31.8 us -> 28 us
    reduce_scatter x1, waiting for transfers between devices: 11.9 us -> 0.01 us  [local(): wo_perm = lax.psum_scatter(wo_perm, 'dpz', scatter_dimension=1, tiled=True)]
    all_to_all x1, waiting for transfers between devices: 31 us -> 38.6 us  [local(): lax.all_to_all(pieces, 'seq', split_axis=0, concat_axis=0, tiled=True)]
    dot_general x4, matrix products: 7.52 us -> 2.63 us  [local(): jnp.einsum('kgqs,skd->qkgd', attn_prob.astype(jnp.bfloat16), v_loc[k_star...]
    reduce_scatter x1, waiting for transfers between devices: 0.01 us -> 3.92 us  [local(): lax.psum_scatter(wo_perm, 'dpy', scatter_dimension=1, tiled=True)]
    unnamed x73 -> x75, local copies, waits for them, and re-layouts: 14.9 us -> 12.3 us
    dot_general x1, matrix products: 2.41 us -> 4.89 us  [local(): lax.dot_general(a_head, incoming, (((0,), (0,)), ((), ())), preferred_ele...]
  transfers between devices with their start and end apart: 6 -> 6, of which waited for: 4 -> 4; matrix products, arithmetic and copies ran while one was open for 19% -> 28% of each run, Pallas kernels for 0% -> 0%
where the time goes in v5:
time: 201 us
  waiting for transfers between devices  93.9 us (47%)
  matrix products  33.3 us (17%)
  local copies, waits for them, and re-layouts  28 us (14%)
  starting transfers between devices  18.4 us (9%)
  between operations  14.3 us (7%)
  other arithmetic  12.6 us (6%)
    all_to_all x1, waiting for transfers between devices, local(): lax.all_to_all(pieces, 'seq', split_axis=0, concat_axis=0, tiled=True)  38.6 us
    all_to_all x1, waiting for transfers between devices, local(): got = lax.all_to_all(packed, 'seq', split_axis=0, concat_axis=0, tiled=True)  34.4 us
    all_to_all x1, waiting for transfers between devices, local(): lax.all_to_all(packed_out, 'seq', split_axis=0, concat_axis=0, tiled=True)  15.7 us
    unnamed x75, local copies, waits for them, and re-layouts  12.3 us
    all_to_all x1, starting transfers between devices, local(): got = lax.all_to_all(packed, 'seq', split_axis=0, concat_axis=0, tiled=True)  6.55 us
    dot_general x1, local copies, waits for them, and re-layouts, local(): lax.dot_general(a_head, incoming, (((0,), (0,)), ((), ())), preferred_ele...  6.4 us
    all_to_all x1, starting transfers between devices, local(): lax.all_to_all(pieces, 'seq', split_axis=0, concat_axis=0, tiled=True)  6.19 us
    all_to_all x1, starting transfers between devices, local(): lax.all_to_all(packed_out, 'seq', split_axis=0, concat_axis=0, tiled=True)  5.62 us
  transfers between devices with their start and end apart: 6, of which 4 were waited for; matrix products, arithmetic and copies ran while one was open for 28% of the time, Pallas kernels for 0%

profile of v5, /device:TPU:2, one launch (start us, length us, event | category | flops | bytes accessed | tf_op | source)
XLA Modules:
  0.0 200.6 jit_solution(9277468078803794921)
XLA Ops:
  7.2 0.7 all-gather.3.cloned.1.call-update
  7.9 1.1 copy.188
  9.0 1.8 copy.189
  10.8 1.6 copy.187
  12.5 2.3 %maximum_bitcast_fusion = bf16[8,128,6,128]{1,3,2,0:T(8,128)(2,1)} fusion(bf16[128,8,1,128]{0,3,2,1:T(8,128)(2,1)} %bitcast.434, bf16[128,8,1,128]{0,3,2,1:T(8,128)(2,1)S(1)} %bitcast.433, bf16[128,8,4,128]{0,3,2,1:T(8,128)(2,1)S(1)} %bitcast.426), kind=kLoop, calls=%fused_computation.37 | loop fusion | flops 1572864 | bytes 3145728 | tf_op jit(solution)/shard_map/transpose | solution.py:46
  14.8 2.6 %copy.192 = bf16[8,128,6,128]{3,1,2,0:T(8,128)(2,1)} copy(bf16[8,128,6,128]{1,3,2,0:T(8,128)(2,1)} %maximum_bitcast_fusion) | data formatting | bytes 3145728 | tf_op jit(solution)/shard_map/transpose | solution.py:46
  17.3 6.5 %all-to-all-start = ((bf16[8,128,6,128]{3,1,2,0:T(8,128)(2,1)}), bf16[8,128,6,128]{3,1,2,0:T(8,128)(2,1)}, u32[]{:S(2)}, u32[]{:S(2)}) async-start(bf16[8,128,6,128]{3,1,2,0:T(8,128)(2,1)} %copy.192), calls=%async_computation | async-start | bytes 3145728 | tf_op jit(solution)/shard_map/all_to_all | solution.py:47
  24.7 0.9 fusion.63
  25.7 34.4 %all-to-all-done = bf16[8,128,6,128]{3,1,2,0:T(8,128)(2,1)} async-done(((bf16[8,128,6,128]{3,1,2,0:T(8,128)(2,1)}), bf16[8,128,6,128]{3,1,2,0:T(8,128)(2,1)}, u32[]{:S(2)}, u32[]{:S(2)}) %all-to-all-start) | async-done | bytes 1572896 | tf_op jit(solution)/shard_map/all_to_all | solution.py:47
  60.0 1.5 copy.193
  65.5 0.6 copy-done.24
  66.1 0.7 fusion.42
  67.0 0.7 fusion.41
  67.8 0.7 fusion.40
  68.7 0.6 copy-done.19
  69.3 1.0 copy-done.12
  70.3 4.3 %convolution_convert_fusion = bf16[1024,2048]{1,0:T(8,128)(2,1)} fusion(bf16[1024,512]{0,1:T(8,128)(2,1)S(1)} %bitcast.445, bf16[512,2048]{1,0:T(8,128)(2,1)S(1)} %copy-done), kind=kOutput, calls=%fused_computation.2 | convolution fusion | flops 2149580800 | bytes 7340032 | tf_op jit(solution)/shard_map/dot_general | solution.py:97
  74.6 6.4 %copy.230 = bf16[2048,1024]{1,0:T(8,128)(2,1)} copy(bf16[2048,1024]{0,1:T(8,128)(2,1)} %bitcast.427) | data formatting | bytes 8388608 | tf_op jit(solution)/shard_map/dot_general | solution.py:100
  81.0 4.9 %convolution_bitcast_fusion = f32[512,8,4,64]{0,3,1,2:T(8,128)S(1)} fusion(bf16[1024,512,1,1]{0,1,3,2:T(8,128)(2,1)} %bitcast.446, bf16[4,8,64,1024]{3,2,1,0:T(8,128)(2,1)} %bitcast.429), kind=kOutput, calls=%fused_computation.3 | convolution fusion | flops 2147483648 | bytes 9437184 | tf_op jit(solution)/shard_map/dot_general | solution.py:100
  85.9 2.5 %copy.232 = f32[512,8,4,64]{0,3,2,1:T(8,128)} copy(f32[512,8,4,64]{0,3,1,2:T(8,128)S(1)} %convolution_bitcast_fusion) | data formatting | bytes 8388608 | tf_op jit(solution)/shard_map/transpose | solution.py:163
  88.4 5.5 %fusion.26 = bf16[1024,512]{0,1:T(8,128)(2,1)} fusion(bf16[512,2048]{1,0:T(8,128)(2,1)S(1)} %copy-done, bf16[1,1024,2048]{2,1,0:T(8,128)(2,1)} %all-gather.3.cloned.1.call-done), kind=kOutput, calls=%fused_computation.39 | convolution fusion | flops 2148007936 | bytes 7340032 | tf_op jit(solution)/shard_map/dot_general | solution.py:103
  94.0 6.2 %all-to-all-start.1 = ((bf16[8,128,2048]{2,1,0:T(8,128)(2,1)}), bf16[8,128,2048]{2,1,0:T(8,128)(2,1)}, u32[]{:S(2)}, u32[]{:S(2)}) async-start(bf16[8,128,2048]{2,1,0:T(8,128)(2,1)} %bitcast.428), calls=%async_computation.1 | async-start | bytes 8388608 | tf_op jit(solution)/shard_map/all_to_all | solution.py:108
  100.1 1.4 multiply_reduce_fusion.3
  101.5 1.6 fusion.37
  103.1 0.9 fusion.39
  104.1 0.8 fusion.29
  104.9 1.0 fusion.43
  106.4 0.9 fusion.48
  107.4 0.8 convolution_bitcast_fusion.4
  108.2 0.7 copy-done.29
  108.9 1.0 fusion.49
  109.9 38.6 %all-to-all-done.1 = bf16[8,128,2048]{2,1,0:T(8,128)(2,1)} async-done(((bf16[8,128,2048]{2,1,0:T(8,128)(2,1)}), bf16[8,128,2048]{2,1,0:T(8,128)(2,1)}, u32[]{:S(2)}, u32[]{:S(2)}) %all-to-all-start.1) | async-done | bytes 4194336 | tf_op jit(solution)/shard_map/all_to_all | solution.py:108
  148.5 2.5 %convolution_bitcast_fusion.2 = f32[512,1,128]{0,2,1:T(8,128)S(1)} fusion(bf16[1024,1,4,128]{0,3,2,1:T(8,128)(2,1)} %bitcast.437, f32[4,256]{1,0:T(4,128)S(1)} %fusion.25, f32[4,256]{1,0:T(4,128)S(1)} %get-tuple-element.42, f32[512,256,4]{1,0,2:T(8,128)} %copy-done.6, pred[256,512]{0,1:T(8,128)(4,1)} %copy-done.23), kind=kOutput, calls=%fused_computation.67 | convolution fusion | flops 136839168 | bytes 2760704 | tf_op jit(solution)/shard_map/kgqs,qkgd->skd/dot_general | solution.py:135
  151.4 0.8 fusion.31
  153.1 0.7 copy-done.5
  153.9 0.8 fusion.30
  155.8 0.8 convolution_bitcast_fusion.3
  157.6 1.3 pad_maximum_fusion
  158.9 5.6 %all-to-all-start.2 = ((bf16[8,128,6,128]{1,3,2,0:T(8,128)(2,1)}), bf16[8,128,6,128]{1,3,2,0:T(8,128)(2,1)}, u32[]{:S(2)}, u32[]{:S(2)}) async-start(bf16[8,128,6,128]{1,3,2,0:T(8,128)(2,1)} %pad_maximum_fusion), calls=%async_computation.2 | async-start | bytes 3145728 | tf_op jit(solution)/shard_map/all_to_all | solution.py:153
  164.5 0.7 reduce-scatter.5.cloned.1.call-update
  165.2 3.8 %reduce_sum.116 = bf16[128,2048]{1,0:T(8,128)(2,1)} reduce(bf16[8,128,2048]{2,1,0:T(8,128)(2,1)} %all-to-all-done.1, bf16[]{:T(256)} %constant.8.clone.1), dimensions={0}, to_apply=%region_11.12 | reduce | flops 1835008 | bytes 4718594 | tf_op jit(solution)/shard_map/reduce_sum | solution.py:146
  169.1 15.7 %all-to-all-done.2 = bf16[8,128,6,128]{1,3,2,0:T(8,128)(2,1)} async-done(((bf16[8,128,6,128]{1,3,2,0:T(8,128)(2,1)}), bf16[8,128,6,128]{1,3,2,0:T(8,128)(2,1)}, u32[]{:S(2)}, u32[]{:S(2)}) %all-to-all-start.2) | async-done | bytes 1572896 | tf_op jit(solution)/shard_map/all_to_all | solution.py:153
  184.8 1.3 slice.205
  186.1 1.3 copy.233
  187.4 1.1 fusion.106
  188.4 0.9 copy.235
  189.3 0.8 copy.234
  190.1 3.9 %reduce-scatter.5.cloned.1.call-done = f32[512,64]{0,1:T(8,128)} async-done(((f32[512,256]{0,1:T(8,128)}), f32[512,64]{0,1:T(8,128)}) %reduce-scatter.5.cloned.1.call-update) | async-done | bytes 131088 | tf_op jit(solution)/shard_map/reduce_scatter | solution.py:167
  (107 shorter events, 8.7 us)
Async XLA Ops:
  7.2 63.1 %copy-start = (bf16[512,2048]{1,0:T(8,128)(2,1)S(1)}, bf16[512,2048]{1,0:T(8,128)(2,1)}, u32[]{:S(2)}) copy-start(bf16[512,2048]{1,0:T(8,128)(2,1)} %param.10) | copy-start | bytes 6291460
  7.2 67.4 %all-gather.3.cloned.1.call-start = ((), (), s32[]{:S(2)}) async-start(), calls=%async_computation.7 | async-start | bytes 4718592 | tf_op jit(solution)/shard_map/all_gather | solution.py:99
  17.3 6.6 %copy-start.32 = (s32[1,16]{1,0:T(1,128)S(1)}, s32[1,16]{1,0:T(1,128)}, u32[]{:S(2)}) copy-start(s32[1,16]{1,0:T(1,128)} %param.12) | copy-start | bytes 196
  17.3 6.6 %copy-start.33 = (s32[1,16]{1,0:T(1,128)S(1)}, s32[1,16]{1,0:T(1,128)}, u32[]{:S(2)}) copy-start(s32[1,16]{1,0:T(1,128)} %param.13) | copy-start | bytes 196
  17.3 42.7 %all-to-all-start = ((bf16[8,128,6,128]{3,1,2,0:T(8,128)(2,1)}), bf16[8,128,6,128]{3,1,2,0:T(8,128)(2,1)}, u32[]{:S(2)}, u32[]{:S(2)}) async-start(bf16[8,128,6,128]{3,1,2,0:T(8,128)(2,1)} %copy.192), calls=%async_computation | async-start | bytes 3145728 | tf_op jit(solution)/shard_map/all_to_all | solution.py:47
  23.9 140.6 %reduce-scatter.3.cloned.1.call-start = ((), (), s32[]{:S(2)}) async-start(), calls=%async_computation.5 | async-start | bytes 4718592 | tf_op jit(solution)/shard_map/reduce_scatter | solution.py:166
  24.7 38.9 %copy-start.20 = (pred[256,512]{0,1:T(8,128)(4,1)}, pred[256,512]{0,1:T(8,128)(4,1)S(1)}, u32[]{:S(2)}) copy-start(pred[256,512]{0,1:T(8,128)(4,1)S(1)} %compare_and_fusion.1) | copy-start | bytes 393220
  25.7 36.9 %copy-start.23 = (pred[256,512]{0,1:T(8,128)(4,1)}, pred[256,512]{0,1:T(8,128)(4,1)S(1)}, u32[]{:S(2)}) copy-start(pred[256,512]{0,1:T(8,128)(4,1)S(1)} %get-tuple-element.51) | copy-start | bytes 393220
  61.5 6.2 %copy-start.1 = (bf16[8,128,6,128]{3,1,0,2:T(8,128)(2,1)}, bf16[8,128,6,128]{3,1,0,2:T(8,128)(2,1)S(1)}, u32[]{:S(2)}) copy-start(bf16[8,128,6,128]{3,1,0,2:T(8,128)(2,1)S(1)} %copy.193) | copy-start | bytes 4718596
  62.6 2.9 %copy-start.6 = (f32[512,256,4]{1,0,2:T(8,128)}, f32[512,256,4]{1,0,2:T(8,128)S(1)}, u32[]{:S(2)}) copy-start(f32[512,256,4]{1,0,2:T(8,128)S(1)} %get-tuple-element.43) | copy-start | bytes 6291460
  63.1 1.1 copy-start.26
  63.6 3.3 %copy-start.4 = (f32[512,256,4]{1,0,2:T(8,128)}, f32[512,256,4]{1,0,2:T(8,128)S(1)}, u32[]{:S(2)}) copy-start(f32[512,256,4]{1,0,2:T(8,128)S(1)} %get-tuple-element.45) | copy-start | bytes 6291460
  64.6 3.2 %copy-start.8 = (f32[512,256,4]{1,0,2:T(8,128)}, f32[512,256,4]{1,0,2:T(8,128)S(1)}, u32[]{:S(2)}) copy-start(f32[512,256,4]{1,0,2:T(8,128)S(1)} %get-tuple-element.47) | copy-start | bytes 6291460
  65.1 1.0 copy-start.24
  66.1 0.9 copy-start.21
  67.0 1.5 copy-start.14
  67.8 0.8 copy-start.16
  68.6 0.7 copy-start.19
  69.3 1.0 copy-start.12
  94.0 54.5 %all-to-all-start.1 = ((bf16[8,128,2048]{2,1,0:T(8,128)(2,1)}), bf16[8,128,2048]{2,1,0:T(8,128)(2,1)}, u32[]{:S(2)}, u32[]{:S(2)}) async-start(bf16[8,128,2048]{2,1,0:T(8,128)(2,1)} %bitcast.428), calls=%async_computation.1 | async-start | bytes 8388608 | tf_op jit(solution)/shard_map/all_to_all | solution.py:108
  101.5 1.6 copy-start.2
  101.5 2.6 %copy-start.9 = (f32[512,256,4]{1,0,2:T(8,128)S(1)}, f32[512,256,4]{1,0,2:T(8,128)}, u32[]{:S(2)}) copy-start(f32[512,256,4]{1,0,2:T(8,128)} %copy-done.8) | copy-start | bytes 6291460
  101.5 2.6 %copy-start.10 = (bf16[1024,512]{0,1:T(8,128)(2,1)S(1)}, bf16[1024,512]{0,1:T(8,128)(2,1)}, u32[]{:S(2)}) copy-start(bf16[1024,512]{0,1:T(8,128)(2,1)} %fusion.26) | copy-start | bytes 3145732
  101.5 2.5 %copy-start.27 = (pred[256,512]{0,1:T(8,128)(4,1)S(1)}, pred[256,512]{0,1:T(8,128)(4,1)}, u32[]{:S(2)}) copy-start(pred[256,512]{0,1:T(8,128)(4,1)} %get-tuple-element.50) | copy-start | bytes 393220
  108.2 0.7 copy-start.29
  109.9 41.1 %copy-start.11 = (bf16[1024,512]{0,1:T(8,128)(2,1)S(1)}, bf16[1024,512]{0,1:T(8,128)(2,1)}, u32[]{:S(2)}) copy-start(bf16[1024,512]{0,1:T(8,128)(2,1)} %fusion.26) | copy-start | bytes 3145732
  109.9 41.3 %copy-start.25 = (pred[256,512]{0,1:T(8,128)(4,1)S(1)}, pred[256,512]{0,1:T(8,128)(4,1)}, u32[]{:S(2)}) copy-start(pred[256,512]{0,1:T(8,128)(4,1)} %copy-done.23) | copy-start | bytes 393220
  148.5 2.6 %copy-start.15 = (bf16[256,1,4,128]{0,3,2,1:T(8,128)(2,1)S(1)}, bf16[256,1,4,128]{0,3,2,1:T(8,128)(2,1)}, u32[]{:S(2)}) copy-start(bf16[256,1,4,128]{0,3,2,1:T(8,128)(2,1)} %copy-done.14) | copy-start | bytes 786436
  148.5 2.6 %copy-start.17 = (bf16[256,1,4,128]{0,3,2,1:T(8,128)(2,1)S(1)}, bf16[256,1,4,128]{0,3,2,1:T(8,128)(2,1)}, u32[]{:S(2)}) copy-start(bf16[256,1,4,128]{0,3,2,1:T(8,128)(2,1)} %copy-done.16) | copy-start | bytes 786436
  148.5 2.8 %copy-start.3 = (bf16[8,128,6,128]{3,1,0,2:T(8,128)(2,1)S(1)}, bf16[8,128,6,128]{3,1,0,2:T(8,128)(2,1)}, u32[]{:S(2)}) copy-start(bf16[8,128,6,128]{3,1,0,2:T(8,128)(2,1)} %copy-done.1) | copy-start | bytes 4718596
  148.5 3.0 %copy-start.7 = (f32[512,256,4]{1,0,2:T(8,128)S(1)}, f32[512,256,4]{1,0,2:T(8,128)}, u32[]{:S(2)}) copy-start(f32[512,256,4]{1,0,2:T(8,128)} %copy-done.6) | copy-start | bytes 6291460
  152.3 1.6 copy-start.5
  152.3 1.6 copy-start.22
  153.9 1.2 copy-start.13
  153.9 1.2 copy-start.18
  155.7 1.0 copy-start.30
  155.7 1.0 copy-start.31
  156.7 0.8 copy-start.28
  158.9 25.8 %all-to-all-start.2 = ((bf16[8,128,6,128]{1,3,2,0:T(8,128)(2,1)}), bf16[8,128,6,128]{1,3,2,0:T(8,128)(2,1)}, u32[]{:S(2)}, u32[]{:S(2)}) async-start(bf16[8,128,6,128]{1,3,2,0:T(8,128)(2,1)} %pad_maximum_fusion), calls=%async_computation.2 | async-start | bytes 3145728 | tf_op jit(solution)/shard_map/all_to_all | solution.py:153
  164.5 29.5 %reduce-scatter.5.cloned.1.call-start = ((), (), s32[]{:S(2)}) async-start(), calls=%async_computation.6 | async-start | bytes 655360 | tf_op jit(solution)/shard_map/reduce_scatter | solution.py:167
Sparse Core Ops, SparseCore 0:
  9.8 51.8 all-gather.2
  88.6 55.7 reduce-scatter.2
  168.4 25.5 reduce-scatter.4

commit v6 on v3

--- a/solution.py
+++ b/solution.py
@@ -48,7 +48,6 @@
         axis=2,
     ).transpose(1, 0, 2, 3)
     got = lax.all_to_all(packed, SEQ, split_axis=0, concat_axis=0, tiled=True)
-    got, out_grad = lax.optimization_barrier((got, out_grad))
     win_rows = seq_count * tok
     got = got.reshape(win_rows, hq + 2 * hk, HEAD_SIZE)
     query_head_rows = got[:, :hq].reshape(win_rows, hk, group_width, HEAD_SIZE)
@@ -99,19 +98,12 @@
     attn_out = jnp.concatenate(out_blocks, axis=0)
     a_head = attn_out.reshape(win_rows, hq * HEAD_SIZE)
     product = jnp.dot(a_head, out_weight, preferred_element_type=jnp.float32)
-    width = product.shape[1]
     pieces = (
         product.astype(jnp.bfloat16)
-        .reshape(x_count, core_count, tok, width)
+        .reshape(x_count, core_count, tok, product.shape[1])
         .transpose(1, 0, 2, 3)
     )
-    pieces = lax.all_to_all(pieces, "core", split_axis=0, concat_axis=0, tiled=True)
-    pair_sum = jnp.sum(pieces.astype(jnp.float32), axis=0).astype(jnp.bfloat16)
-    pair_sum = lax.all_to_all(pair_sum, "x", split_axis=0, concat_axis=0, tiled=True)
-    y_out = jnp.sum(pair_sum.astype(jnp.float32), axis=0).astype(jnp.bfloat16)
-    g_rows = lax.all_gather(out_grad.reshape(tok, out_grad.shape[2]), "x", axis=0, tiled=False)
-    g_rows = lax.all_gather(g_rows, "core", axis=0, tiled=False)
-    incoming = g_rows.transpose(1, 0, 2, 3).reshape(win_rows, g_rows.shape[3])
+    incoming = lax.all_gather(out_grad.reshape(tok, out_grad.shape[2]), SEQ, axis=0, tiled=True)
     wo_grad = lax.dot_general(
         a_head, incoming, (((0,), (0,)), ((), ())), preferred_element_type=jnp.float32
     )
@@ -119,11 +111,17 @@
         incoming, out_weight, (((1,), (1,)), ((), ())), preferred_element_type=jnp.float32
     )
     attention_grad = d_rows.astype(jnp.bfloat16).reshape(win_rows, hk, group_width, HEAD_SIZE)
+    pieces, attention_grad = lax.optimization_barrier((pieces, attention_grad))
+    pieces = lax.all_to_all(pieces, "core", split_axis=0, concat_axis=0, tiled=True)
+    pieces = jnp.sum(pieces.astype(jnp.float32), axis=0).astype(jnp.bfloat16)
+    pieces = lax.all_to_all(pieces, "x", split_axis=0, concat_axis=0, tiled=True)
 
     dq_blocks = []
     dk_blocks = [None] * blk_count
     dv_blocks = [None] * blk_count
     for i in range(blk_count):
+        if i == blk_count // 2:
+            pieces, attention_grad = lax.optimization_barrier((pieces, attention_grad))
         q_start, k_start, k_end = band(i)
         q_blk = query_head_rows[q_start : q_start + blk]
         g_blk = attention_grad[q_start : q_start + blk]
@@ -154,6 +152,7 @@
             for acc, part in ((dk_blocks, dk_part), (dv_blocks, dv_part)):
                 piece = part[lo : lo + blk]
                 acc[j] = piece if acc[j] is None else acc[j] + piece
+    y_out = jnp.sum(pieces.astype(jnp.float32), axis=0).astype(jnp.bfloat16)
     dq_all = jnp.concatenate(dq_blocks, axis=0).reshape(win_rows, hq, HEAD_SIZE)
     dk_all = jnp.concatenate(dk_blocks, axis=0).astype(jnp.bfloat16)
     dv_all = jnp.concatenate(dv_blocks, axis=0).astype(jnp.bfloat16)

time: 235 us -> 191 us (0.81)
  blocking collectives: 26.8 us -> 8.13 us
  local copies, waits for them, and re-layouts: 47.5 us -> 29.4 us
  waiting for transfers between devices: 80.9 us -> 72.8 us
    all_gather x2 -> x1, waiting for transfers between devices: 45.2 us -> 0.01 us  [local(): lax.all_gather(out_grad.reshape(tok, out_grad.shape[2]), SEQ, axis=0, til...]
    all_to_all x2, waiting for transfers between devices: 19 us -> 49.4 us  [the longest x1 34.4 us: local(): got = lax.all_to_all(packed, SEQ, split_axis=0, concat_axis=0, tiled=True)]
    all_to_all x1, blocking collectives: 26.8 us -> 8.13 us  [local(): lax.all_to_all(pieces, 'core', split_axis=0, concat_axis=0, tiled=True)]
    transpose x1 -> x0, local copies, waits for them, and re-layouts: 11.2 us -> none  [local(): incoming = g_rows.transpose(1, 0, 2, 3).reshape(win_rows, g_rows.shape[3])]
    reshape x2 -> x1, local copies, waits for them, and re-layouts: 10 us -> 0.58 us  [local(): pieces = product.astype(jnp.bfloat16).reshape(x_count, core_count, tok, p...]
    dot_general x0 -> x1, local copies, waits for them, and re-layouts: none -> 6.39 us  [local(): lax.dot_general(a_head, incoming, (((0,), (0,)), ((), ())), preferred_ele...]
    dot_general x4, matrix products: 8.7 us -> 2.64 us  [local(): jnp.einsum('kgqs,skd->qkgd', attn_prob.astype(jnp.bfloat16), v_loc[k_star...]
    all_to_all x1, waiting for transfers between devices: 15 us -> 18.2 us  [local(): lax.all_to_all(packed_out, SEQ, split_axis=0, concat_axis=0, tiled=True)]
  transfers between devices with their start and end apart: 7 -> 6, of which waited for: 5 -> 4; matrix products, arithmetic and copies ran while one was open for 17% -> 30% of each run, Pallas kernels for 0% -> 0%
where the time goes in v6:
time: 191 us; the launch traced here: 190 us
  waiting for transfers between devices  72.8 us (38%)
  matrix products  31.2 us (16%)
  local copies, waits for them, and re-layouts  29.4 us (15%)
  starting transfers between devices  17.6 us (9%)
  other arithmetic  16.2 us (8%)
  between operations  14.4 us (8%)
  blocking collectives  8.13 us (4%)
    all_to_all x1, waiting for transfers between devices, local(): got = lax.all_to_all(packed, SEQ, split_axis=0, concat_axis=0, tiled=True)  34.4 us
    all_to_all x1, waiting for transfers between devices, local(): lax.all_to_all(packed_out, SEQ, split_axis=0, concat_axis=0, tiled=True)  18.2 us
    all_to_all x1, waiting for transfers between devices, local(): lax.all_to_all(pieces, 'x', split_axis=0, concat_axis=0, tiled=True)  15 us
    unnamed x77, local copies, waits for them, and re-layouts  13.1 us
    all_to_all x1, blocking collectives, local(): lax.all_to_all(pieces, 'core', split_axis=0, concat_axis=0, tiled=True)  8.13 us
    all_to_all x1, starting transfers between devices, local(): got = lax.all_to_all(packed, SEQ, split_axis=0, concat_axis=0, tiled=True)  6.55 us
    dot_general x1, local copies, waits for them, and re-layouts, local(): lax.dot_general(a_head, incoming, (((0,), (0,)), ((), ())), preferred_ele...  6.39 us
    all_to_all x1, starting transfers between devices, local(): lax.all_to_all(packed_out, SEQ, split_axis=0, concat_axis=0, tiled=True)  5.64 us
  transfers between devices with their start and end apart: 6, of which 4 were waited for; matrix products, arithmetic and copies ran while one was open for 30% of the time, Pallas kernels for 0%

profile of v6, /device:TPU:2, one launch (start us, length us, event | category | flops | bytes accessed | tf_op | source)
XLA Modules:
  0.0 189.6 jit_solution(14404267682815351885)
XLA Ops:
  7.9 1.1 copy.190
  9.0 1.8 copy.191
  10.8 1.6 copy.189
  12.5 2.3 %maximum_bitcast_fusion = bf16[8,128,6,128]{1,3,2,0:T(8,128)(2,1)} fusion(bf16[128,8,1,128]{0,3,2,1:T(8,128)(2,1)} %bitcast.438, bf16[128,8,1,128]{0,3,2,1:T(8,128)(2,1)S(1)} %bitcast.437, bf16[128,8,4,128]{0,3,2,1:T(8,128)(2,1)S(1)} %bitcast.430), kind=kLoop, calls=%fused_computation.38 | loop fusion | flops 1572864 | bytes 3145728 | tf_op jit(solution)/shard_map/transpose | solution.py:49
  14.7 2.6 %copy.194 = bf16[8,128,6,128]{3,1,2,0:T(8,128)(2,1)} copy(bf16[8,128,6,128]{1,3,2,0:T(8,128)(2,1)} %maximum_bitcast_fusion) | data formatting | bytes 3145728 | tf_op jit(solution)/shard_map/transpose | solution.py:49
  17.3 6.5 %all-to-all-start = ((bf16[8,128,6,128]{3,1,2,0:T(8,128)(2,1)}), bf16[8,128,6,128]{3,1,2,0:T(8,128)(2,1)}, u32[]{:S(2)}, u32[]{:S(2)}) async-start(bf16[8,128,6,128]{3,1,2,0:T(8,128)(2,1)} %copy.194), calls=%async_computation | async-start | bytes 3145728 | tf_op jit(solution)/shard_map/all_to_all | solution.py:50
  24.7 0.9 fusion.63
  25.7 34.4 %all-to-all-done = bf16[8,128,6,128]{3,1,2,0:T(8,128)(2,1)} async-done(((bf16[8,128,6,128]{3,1,2,0:T(8,128)(2,1)}), bf16[8,128,6,128]{3,1,2,0:T(8,128)(2,1)}, u32[]{:S(2)}, u32[]{:S(2)}) %all-to-all-start) | async-done | bytes 1572896 | tf_op jit(solution)/shard_map/all_to_all | solution.py:50
  60.0 1.5 copy.195
  66.1 0.7 fusion.42
  67.0 0.7 fusion.41
  67.8 0.7 fusion.40
  68.6 0.7 copy-done.20
  69.3 1.1 pad_maximum_fusion.1
  70.4 6.4 %copy.233 = bf16[2048,1024]{1,0:T(8,128)(2,1)} copy(bf16[2048,1024]{0,1:T(8,128)(2,1)} %bitcast.431) | data formatting | bytes 8388608 | tf_op jit(solution)/shard_map/dot_general | solution.py:107
  76.8 4.9 %convolution_bitcast_fusion = f32[512,8,4,64]{0,3,1,2:T(8,128)S(1)} fusion(bf16[1024,512,1,1]{0,1,3,2:T(8,128)(2,1)} %bitcast.449, bf16[4,8,64,1024]{3,2,1,0:T(8,128)(2,1)} %bitcast.433), kind=kOutput, calls=%fused_computation.4 | convolution fusion | flops 2147483648 | bytes 9437184 | tf_op jit(solution)/shard_map/dot_general | solution.py:107
  81.7 2.5 %copy.235 = f32[512,8,4,64]{0,3,2,1:T(8,128)} copy(f32[512,8,4,64]{0,3,1,2:T(8,128)S(1)} %convolution_bitcast_fusion) | data formatting | bytes 8388608 | tf_op jit(solution)/shard_map/transpose | solution.py:172
  84.2 3.6 %convolution_convert_fusion = bf16[1024,2048]{1,0:T(8,128)(2,1)S(1)} fusion(bf16[1024,512]{0,1:T(8,128)(2,1)} %bitcast.450, bf16[512,2048]{1,0:T(8,128)(2,1)S(1)} %copy-done), kind=kOutput, calls=%fused_computation.3 | convolution fusion | flops 2149580800 | bytes 7340032 | tf_op jit(solution)/shard_map/dot_general | solution.py:100
  88.4 1.6 copy-done.5
  90.0 3.4 %fusion.26 = bf16[1024,512]{0,1:T(8,128)(2,1)} fusion(bf16[512,2048]{1,0:T(8,128)(2,1)S(1)} %copy-done, bf16[1,1024,2048]{2,1,0:T(8,128)(2,1)S(1)} %copy-done.5), kind=kOutput, calls=%fused_computation.40 | convolution fusion | flops 2148007936 | bytes 7340032 | tf_op jit(solution)/shard_map/dot_general | solution.py:110
  93.4 8.1 %all_to_all.20 = bf16[2,4,128,2048]{3,2,1,0:T(8,128)(2,1)} all-to-all(bf16[2,4,128,2048]{3,2,1,0:T(8,128)(2,1)S(1)} %bitcast.409), channel_id=1, replica_groups=mesh['x'=4,'core'=2,'dpy'=4,'dpz'=8] {'core'}, dimensions={0} | all-to-all | bytes 8388608 | tf_op jit(solution)/shard_map/all_to_all | solution.py:115
  101.5 5.1 %reduce_sum.128 = bf16[4,128,2048]{2,1,0:T(8,128)(2,1)} reduce(bf16[2,4,128,2048]{3,2,1,0:T(8,128)(2,1)} %all_to_all.20, bf16[]{:T(256)} %constant.24.clone.1), dimensions={0}, to_apply=%region_11.12 | reduce | flops 1048576 | bytes 6291458 | tf_op jit(solution)/shard_map/reduce_sum | solution.py:116
  106.7 5.3 %all-to-all-start.2 = ((bf16[4,128,2048]{2,1,0:T(8,128)(2,1)}), bf16[4,128,2048]{2,1,0:T(8,128)(2,1)S(1)}, u32[]{:S(2)}, u32[]{:S(2)}) async-start(bf16[4,128,2048]{2,1,0:T(8,128)(2,1)} %reduce_sum.128), calls=%async_computation.2 | async-start | bytes 4194304 | tf_op jit(solution)/shard_map/all_to_all | solution.py:117
  112.0 1.3 multiply_reduce_fusion.3
  113.3 2.8 %fusion.29 = bf16[4,256,512]{1,2,0:T(8,128)(2,1)S(1)} fusion(f32[4,256]{1,0:T(4,128)S(1)} %bitcast.457, f32[4,256]{1,0:T(4,128)S(1)} %fusion.21, f32[4,256]{1,0:T(4,128)S(1)} %get-tuple-element.46, f32[512,256,4]{1,0,2:T(8,128)} %copy-done.10, pred[256,512]{0,1:T(8,128)(4,1)} %get-tuple-element.50, bf16[1024,1,4,128]{0,3,2,1:T(8,128)(2,1)} %bitcast.440, ...), kind=kOutput, calls=%fused_computation.41 | convolution fusion | flops 138412032 | bytes 3682304 | tf_op jit(solution)/shard_map/qkgd,skd->kgqs/dot_general | solution.py:134
  116.5 1.0 fusion.39
  117.5 1.0 fusion.43
  119.0 0.9 fusion.48
  119.9 0.8 convolution_bitcast_fusion.4
  120.7 0.7 copy-done.30
  121.4 1.0 fusion.49
  122.5 15.0 %all-to-all-done.2 = bf16[4,128,2048]{2,1,0:T(8,128)(2,1)S(1)} async-done(((bf16[4,128,2048]{2,1,0:T(8,128)(2,1)}), bf16[4,128,2048]{2,1,0:T(8,128)(2,1)S(1)}, u32[]{:S(2)}, u32[]{:S(2)}) %all-to-all-start.2) | async-done | bytes 2097184 | tf_op jit(solution)/shard_map/all_to_all | solution.py:117
  137.5 2.5 %convolution_bitcast_fusion.2 = f32[512,1,128]{0,2,1:T(8,128)S(1)} fusion(bf16[1024,1,4,128]{0,3,2,1:T(8,128)(2,1)} %bitcast.441, f32[4,256]{1,0:T(4,128)S(1)} %fusion.25, f32[4,256]{1,0:T(4,128)S(1)} %get-tuple-element.42, f32[512,256,4]{1,0,2:T(8,128)} %copy-done.8, pred[256,512]{0,1:T(8,128)(4,1)} %copy-done.24), kind=kOutput, calls=%fused_computation.68 | convolution fusion | flops 136839168 | bytes 2760704 | tf_op jit(solution)/shard_map/kgqs,qkgd->skd/dot_general | solution.py:144
  140.5 0.8 fusion.31
  142.2 0.7 copy-done.7
  142.9 0.8 fusion.30
  144.8 0.8 convolution_bitcast_fusion.3
  146.6 1.4 pad_maximum_fusion
  148.0 5.6 %all-to-all-start.3 = ((bf16[8,128,6,128]{1,3,2,0:T(8,128)(2,1)}), bf16[8,128,6,128]{1,3,2,0:T(8,128)(2,1)}, u32[]{:S(2)}, u32[]{:S(2)}) async-start(bf16[8,128,6,128]{1,3,2,0:T(8,128)(2,1)} %pad_maximum_fusion), calls=%async_computation.3 | async-start | bytes 3145728 | tf_op jit(solution)/shard_map/all_to_all | solution.py:162
  153.6 0.7 reduce-scatter.5.cloned.1.call-update
  154.4 1.3 reduce_sum.129
  155.7 18.2 %all-to-all-done.3 = bf16[8,128,6,128]{1,3,2,0:T(8,128)(2,1)} async-done(((bf16[8,128,6,128]{1,3,2,0:T(8,128)(2,1)}), bf16[8,128,6,128]{1,3,2,0:T(8,128)(2,1)}, u32[]{:S(2)}, u32[]{:S(2)}) %all-to-all-start.3) | async-done | bytes 1572896 | tf_op jit(solution)/shard_map/all_to_all | solution.py:162
  173.9 1.3 slice.205
  175.2 1.3 copy.236
  176.5 1.1 fusion.106
  177.6 0.9 copy.238
  178.4 0.8 copy.237
  179.3 3.8 %reduce-scatter.5.cloned.1.call-done = f32[512,64]{0,1:T(8,128)} async-done(((f32[512,256]{0,1:T(8,128)}), f32[512,64]{0,1:T(8,128)}) %reduce-scatter.5.cloned.1.call-update) | async-done | bytes 131088 | tf_op jit(solution)/shard_map/reduce_scatter | solution.py:176
  (112 shorter events, 10.9 us)
Async XLA Ops:
  7.2 77.1 %copy-start = (bf16[512,2048]{1,0:T(8,128)(2,1)S(1)}, bf16[512,2048]{1,0:T(8,128)(2,1)}, u32[]{:S(2)}) copy-start(bf16[512,2048]{1,0:T(8,128)(2,1)} %param.10) | copy-start | bytes 6291460
  7.2 63.2 %all-gather.3.cloned.1.call-start = ((), (), s32[]{:S(2)}) async-start(), calls=%async_computation.8 | async-start | bytes 4718592 | tf_op jit(solution)/shard_map/all_gather | solution.py:106
  17.3 6.6 %copy-start.33 = (s32[1,16]{1,0:T(1,128)S(1)}, s32[1,16]{1,0:T(1,128)}, u32[]{:S(2)}) copy-start(s32[1,16]{1,0:T(1,128)} %param.12) | copy-start | bytes 196
  17.3 6.6 %copy-start.34 = (s32[1,16]{1,0:T(1,128)S(1)}, s32[1,16]{1,0:T(1,128)}, u32[]{:S(2)}) copy-start(s32[1,16]{1,0:T(1,128)} %param.13) | copy-start | bytes 196
  17.3 42.7 %all-to-all-start = ((bf16[8,128,6,128]{3,1,2,0:T(8,128)(2,1)}), bf16[8,128,6,128]{3,1,2,0:T(8,128)(2,1)}, u32[]{:S(2)}, u32[]{:S(2)}) async-start(bf16[8,128,6,128]{3,1,2,0:T(8,128)(2,1)} %copy.194), calls=%async_computation | async-start | bytes 3145728 | tf_op jit(solution)/shard_map/all_to_all | solution.py:50
  23.9 129.8 %reduce-scatter.3.cloned.1.call-start = ((), (), s32[]{:S(2)}) async-start(), calls=%async_computation.6 | async-start | bytes 4718592 | tf_op jit(solution)/shard_map/reduce_scatter | solution.py:175
  24.7 38.9 %copy-start.21 = (pred[256,512]{0,1:T(8,128)(4,1)}, pred[256,512]{0,1:T(8,128)(4,1)S(1)}, u32[]{:S(2)}) copy-start(pred[256,512]{0,1:T(8,128)(4,1)S(1)} %compare_and_fusion.1) | copy-start | bytes 393220
  25.7 36.9 %copy-start.24 = (pred[256,512]{0,1:T(8,128)(4,1)}, pred[256,512]{0,1:T(8,128)(4,1)S(1)}, u32[]{:S(2)}) copy-start(pred[256,512]{0,1:T(8,128)(4,1)S(1)} %get-tuple-element.51) | copy-start | bytes 393220
  61.5 6.2 %copy-start.2 = (bf16[8,128,6,128]{3,1,0,2:T(8,128)(2,1)}, bf16[8,128,6,128]{3,1,0,2:T(8,128)(2,1)S(1)}, u32[]{:S(2)}) copy-start(bf16[8,128,6,128]{3,1,0,2:T(8,128)(2,1)S(1)} %copy.195) | copy-start | bytes 4718596
  62.6 2.9 %copy-start.8 = (f32[512,256,4]{1,0,2:T(8,128)}, f32[512,256,4]{1,0,2:T(8,128)S(1)}, u32[]{:S(2)}) copy-start(f32[512,256,4]{1,0,2:T(8,128)S(1)} %get-tuple-element.43) | copy-start | bytes 6291460
  63.1 1.1 copy-start.27
  63.6 3.3 %copy-start.6 = (f32[512,256,4]{1,0,2:T(8,128)}, f32[512,256,4]{1,0,2:T(8,128)S(1)}, u32[]{:S(2)}) copy-start(f32[512,256,4]{1,0,2:T(8,128)S(1)} %get-tuple-element.45) | copy-start | bytes 6291460
  64.6 3.2 %copy-start.10 = (f32[512,256,4]{1,0,2:T(8,128)}, f32[512,256,4]{1,0,2:T(8,128)S(1)}, u32[]{:S(2)}) copy-start(f32[512,256,4]{1,0,2:T(8,128)S(1)} %get-tuple-element.47) | copy-start | bytes 6291460
  65.1 1.0 copy-start.25
  66.1 0.9 copy-start.22
  67.0 1.5 copy-start.15
  67.8 0.8 copy-start.17
  68.6 0.7 copy-start.20
  87.9 2.2 %copy-start.5 = (bf16[1,1024,2048]{2,1,0:T(8,128)(2,1)S(1)}, bf16[1,1024,2048]{2,1,0:T(8,128)(2,1)}, u32[]{:S(2)}) copy-start(bf16[1,1024,2048]{2,1,0:T(8,128)(2,1)} %all-gather.3.cloned.1.call-done) | copy-start | bytes 12582916
  106.7 30.8 %all-to-all-start.2 = ((bf16[4,128,2048]{2,1,0:T(8,128)(2,1)}), bf16[4,128,2048]{2,1,0:T(8,128)(2,1)S(1)}, u32[]{:S(2)}, u32[]{:S(2)}) async-start(bf16[4,128,2048]{2,1,0:T(8,128)(2,1)} %reduce_sum.128), calls=%async_computation.2 | async-start | bytes 4194304 | tf_op jit(solution)/shard_map/all_to_all | solution.py:117
  113.3 2.8 %copy-start.3 = (bf16[8,128,6,128]{3,1,0,2:T(8,128)(2,1)S(1)}, bf16[8,128,6,128]{3,1,0,2:T(8,128)(2,1)}, u32[]{:S(2)}) copy-start(bf16[8,128,6,128]{3,1,0,2:T(8,128)(2,1)} %copy-done.2) | copy-start | bytes 4718596
  113.3 2.8 %copy-start.12 = (bf16[1024,512]{0,1:T(8,128)(2,1)S(1)}, bf16[1024,512]{0,1:T(8,128)(2,1)}, u32[]{:S(2)}) copy-start(bf16[1024,512]{0,1:T(8,128)(2,1)} %fusion.26) | copy-start | bytes 3145732
  117.5 2.5 %copy-start.11 = (f32[512,256,4]{1,0,2:T(8,128)S(1)}, f32[512,256,4]{1,0,2:T(8,128)}, u32[]{:S(2)}) copy-start(f32[512,256,4]{1,0,2:T(8,128)} %copy-done.10) | copy-start | bytes 6291460
  117.5 2.5 %copy-start.28 = (pred[256,512]{0,1:T(8,128)(4,1)S(1)}, pred[256,512]{0,1:T(8,128)(4,1)}, u32[]{:S(2)}) copy-start(pred[256,512]{0,1:T(8,128)(4,1)} %get-tuple-element.50) | copy-start | bytes 393220
  120.7 0.7 copy-start.30
  122.5 17.6 %copy-start.13 = (bf16[1024,512]{0,1:T(8,128)(2,1)S(1)}, bf16[1024,512]{0,1:T(8,128)(2,1)}, u32[]{:S(2)}) copy-start(bf16[1024,512]{0,1:T(8,128)(2,1)} %fusion.26) | copy-start | bytes 3145732
  122.5 17.8 %copy-start.26 = (pred[256,512]{0,1:T(8,128)(4,1)S(1)}, pred[256,512]{0,1:T(8,128)(4,1)}, u32[]{:S(2)}) copy-start(pred[256,512]{0,1:T(8,128)(4,1)} %copy-done.24) | copy-start | bytes 393220
  137.5 2.6 %copy-start.16 = (bf16[256,1,4,128]{0,3,2,1:T(8,128)(2,1)S(1)}, bf16[256,1,4,128]{0,3,2,1:T(8,128)(2,1)}, u32[]{:S(2)}) copy-start(bf16[256,1,4,128]{0,3,2,1:T(8,128)(2,1)} %copy-done.15) | copy-start | bytes 786436
  137.5 2.6 %copy-start.18 = (bf16[256,1,4,128]{0,3,2,1:T(8,128)(2,1)S(1)}, bf16[256,1,4,128]{0,3,2,1:T(8,128)(2,1)}, u32[]{:S(2)}) copy-start(bf16[256,1,4,128]{0,3,2,1:T(8,128)(2,1)} %copy-done.17) | copy-start | bytes 786436
  137.5 2.8 %copy-start.4 = (bf16[8,128,6,128]{3,1,0,2:T(8,128)(2,1)S(1)}, bf16[8,128,6,128]{3,1,0,2:T(8,128)(2,1)}, u32[]{:S(2)}) copy-start(bf16[8,128,6,128]{3,1,0,2:T(8,128)(2,1)} %copy-done.2) | copy-start | bytes 4718596
  137.5 3.0 %copy-start.9 = (f32[512,256,4]{1,0,2:T(8,128)S(1)}, f32[512,256,4]{1,0,2:T(8,128)}, u32[]{:S(2)}) copy-start(f32[512,256,4]{1,0,2:T(8,128)} %copy-done.8) | copy-start | bytes 6291460
  141.3 1.6 copy-start.7
  141.3 1.6 copy-start.23
  142.9 1.2 copy-start.14
  142.9 1.2 copy-start.19
  144.8 1.0 copy-start.31
  144.8 1.0 copy-start.32
  145.7 0.8 copy-start.29
  148.0 25.9 %all-to-all-start.3 = ((bf16[8,128,6,128]{1,3,2,0:T(8,128)(2,1)}), bf16[8,128,6,128]{1,3,2,0:T(8,128)(2,1)}, u32[]{:S(2)}, u32[]{:S(2)}) async-start(bf16[8,128,6,128]{1,3,2,0:T(8,128)(2,1)} %pad_maximum_fusion), calls=%async_computation.3 | async-start | bytes 3145728 | tf_op jit(solution)/shard_map/all_to_all | solution.py:162
  153.6 29.4 %reduce-scatter.5.cloned.1.call-start = ((), (), s32[]{:S(2)}) async-start(), calls=%async_computation.7 | async-start | bytes 655360 | tf_op jit(solution)/shard_map/reduce_scatter | solution.py:176
  175.2 7.9 %copy-start.1 = (bf16[512,2048]{1,0:T(8,128)(2,1)S(1)}, bf16[512,2048]{1,0:T(8,128)(2,1)}, u32[]{:S(2)}) copy-start(bf16[512,2048]{1,0:T(8,128)(2,1)} %param.10) | copy-start | bytes 6291460
Sparse Core Ops, SparseCore 0:
  9.9 51.8 all-gather.2
  84.3 55.7 reduce-scatter.2
  157.5 25.4 reduce-scatter.4

commit v7 on v6

--- a/solution.py
+++ b/solution.py
@@ -103,14 +103,31 @@
         .reshape(x_count, core_count, tok, product.shape[1])
         .transpose(1, 0, 2, 3)
     )
-    incoming = lax.all_gather(out_grad.reshape(tok, out_grad.shape[2]), SEQ, axis=0, tiled=True)
+    g_mine = lax.all_gather(out_grad.reshape(tok, out_grad.shape[2]), "x", axis=0, tiled=False)
+    g_other = lax.ppermute(
+        g_mine, "core", perm=[(c, (c + 1) % core_count) for c in range(core_count)]
+    )
+    core_at = lax.axis_index("core")
+    a_split = a_head.reshape(x_count, core_count, tok, hq * HEAD_SIZE)
+    a_mine = lax.dynamic_index_in_dim(a_split, core_at, axis=1, keepdims=False)
+    a_other = lax.dynamic_index_in_dim(a_split, 1 - core_at, axis=1, keepdims=False)
+    contract_rows = (((0, 1), (0, 1)), ((), ()))
     wo_grad = lax.dot_general(
-        a_head, incoming, (((0,), (0,)), ((), ())), preferred_element_type=jnp.float32
-    )
-    d_rows = lax.dot_general(
-        incoming, out_weight, (((1,), (1,)), ((), ())), preferred_element_type=jnp.float32
-    )
-    attention_grad = d_rows.astype(jnp.bfloat16).reshape(win_rows, hk, group_width, HEAD_SIZE)
+        a_mine, g_mine, contract_rows, preferred_element_type=jnp.float32
+    ) + lax.dot_general(a_other, g_other, contract_rows, preferred_element_type=jnp.float32)
+    contract_cols = (((2,), (1,)), ((), ()))
+    d_mine = lax.dot_general(
+        g_mine, out_weight, contract_cols, preferred_element_type=jnp.float32
+    ).astype(jnp.bfloat16)
+    d_other = lax.dot_general(
+        g_other, out_weight, contract_cols, preferred_element_type=jnp.float32
+    ).astype(jnp.bfloat16)
+    d_rows = jnp.where(
+        core_at == 0,
+        jnp.stack([d_mine, d_other], axis=1),
+        jnp.stack([d_other, d_mine], axis=1),
+    )
+    attention_grad = d_rows.reshape(win_rows, hk, group_width, HEAD_SIZE)
     pieces, attention_grad = lax.optimization_barrier((pieces, attention_grad))
     pieces = lax.all_to_all(pieces, "core", split_axis=0, concat_axis=0, tiled=True)
     pieces = jnp.sum(pieces.astype(jnp.float32), axis=0).astype(jnp.bfloat16)

time: 191 us -> 204 us (1.068)
  local copies, waits for them, and re-layouts: 29.4 us -> 38.2 us
  waiting for transfers between devices: 72.8 us -> 67.3 us
  matrix products: 31.2 us -> 35.6 us
  blocking collectives: 8.13 us -> 12.1 us
  other arithmetic: 16.2 us -> 18.3 us
    all_to_all x1, waiting for transfers between devices: 34.4 us -> 18.9 us  [local(): got = lax.all_to_all(packed, SEQ, split_axis=0, concat_axis=0, tiled=True)]
    all_gather x1, waiting for transfers between devices: 0.01 us -> 8.98 us  [local(): lax.all_gather(out_grad.reshape(tok, out_grad.shape[2]), 'x', axis=0, til...]
    dot_general x1 -> x0, local copies, waits for them, and re-layouts: 6.39 us -> none  [local(): lax.dot_general(a_head, incoming, (((0,), (0,)), ((), ())), preferred_ele...]
    add x0 -> x1, local copies, waits for them, and re-layouts: none -> 5.39 us  [local(): lax.dot_general(a_mine, g_mine, contract_rows, preferred_element_type=jnp...]
    all_to_all x1, blocking collectives: 8.13 us -> 12.1 us  [local(): lax.all_to_all(pieces, 'core', split_axis=0, concat_axis=0, tiled=True)]
    dot_general x4, matrix products: 2.64 us -> 5.74 us  [local(): jnp.einsum('kgqs,skd->qkgd', attn_prob.astype(jnp.bfloat16), v_loc[k_star...]
    transpose x1, local copies, waits for them, and re-layouts: 2.5 us -> 4.85 us  [local(): wo_perm = wo_grad.reshape(wo_grad.shape[0], y_count, z_count, cols // (y_...]
    dynamic_slice x0 -> x1, local copies, waits for them, and re-layouts: none -> 2.17 us  [local(): lax.dynamic_index_in_dim(a_split, 1 - core_at, axis=1, keepdims=False)]
  transfers between devices with their start and end apart: 6 -> 7, of which waited for: 4 -> 5; matrix products, arithmetic and copies ran while one was open for 30% -> 31% of each run, Pallas kernels for 0% -> 0%
where the time goes in v7:
time: 204 us; the launch traced here: 203 us
  waiting for transfers between devices  67.3 us (33%)
  local copies, waits for them, and re-layouts  38.2 us (19%)
  matrix products  35.6 us (17%)
  other arithmetic  18.3 us (9%)
  starting transfers between devices  17.3 us (8%)
  between operations  14.6 us (7%)
  blocking collectives  12.1 us (6%)
    all_to_all x1, waiting for transfers between devices, local(): got = lax.all_to_all(packed, SEQ, split_axis=0, concat_axis=0, tiled=True)  18.9 us
    all_to_all x1, waiting for transfers between devices, local(): lax.all_to_all(packed_out, SEQ, split_axis=0, concat_axis=0, tiled=True)  18.2 us
    all_to_all x1, waiting for transfers between devices, local(): lax.all_to_all(pieces, 'x', split_axis=0, concat_axis=0, tiled=True)  15.9 us
    unnamed x91, local copies, waits for them, and re-layouts  13.1 us
    all_to_all x1, blocking collectives, local(): lax.all_to_all(pieces, 'core', split_axis=0, concat_axis=0, tiled=True)  12.1 us
    all_gather x1, waiting for transfers between devices, local(): lax.all_gather(out_grad.reshape(tok, out_grad.shape[2]), 'x', axis=0, til...  8.98 us
    all_to_all x1, starting transfers between devices, local(): got = lax.all_to_all(packed, SEQ, split_axis=0, concat_axis=0, tiled=True)  6.54 us
    dot_general x4, matrix products, local(): jnp.einsum('qkgd,skd->kgqs', g_blk, v_band, preferred_element_type=jnp.fl...  6.41 us
  transfers between devices with their start and end apart: 7, of which 5 were waited for; matrix products, arithmetic and copies ran while one was open for 31% of the time, Pallas kernels for 0%

profile of v7, /device:TPU:2, one launch (start us, length us, event | category | flops | bytes accessed | tf_op | source)
XLA Modules:
  0.0 203.2 jit_solution(11917535467345258699)
XLA Ops:
  7.2 1.8 copy.240
  9.0 1.1 copy.241
  10.1 1.8 copy.242
  11.9 2.3 %maximum_bitcast_fusion = bf16[8,128,6,128]{1,3,2,0:T(8,128)(2,1)} fusion(bf16[128,8,1,128]{0,3,2,1:T(8,128)(2,1)} %bitcast.462, bf16[128,8,1,128]{0,3,2,1:T(8,128)(2,1)S(1)} %bitcast.461, bf16[128,8,4,128]{0,3,2,1:T(8,128)(2,1)S(1)} %bitcast.455), kind=kLoop, calls=%fused_computation.40 | loop fusion | flops 1572864 | bytes 3145728 | tf_op jit(solution)/shard_map/transpose | solution.py:49
  14.2 2.6 %copy.245 = bf16[8,128,6,128]{3,1,2,0:T(8,128)(2,1)} copy(bf16[8,128,6,128]{1,3,2,0:T(8,128)(2,1)} %maximum_bitcast_fusion) | data formatting | bytes 3145728 | tf_op jit(solution)/shard_map/transpose | solution.py:49
  16.8 6.5 %all-to-all-start = ((bf16[8,128,6,128]{3,1,2,0:T(8,128)(2,1)}), bf16[8,128,6,128]{3,1,2,0:T(8,128)(2,1)}, u32[]{:S(2)}, u32[]{:S(2)}) async-start(bf16[8,128,6,128]{3,1,2,0:T(8,128)(2,1)} %copy.245), calls=%async_computation | async-start | bytes 3145728 | tf_op jit(solution)/shard_map/all_to_all | solution.py:50
  25.2 18.9 %all-to-all-done = bf16[8,128,6,128]{3,1,2,0:T(8,128)(2,1)} async-done(((bf16[8,128,6,128]{3,1,2,0:T(8,128)(2,1)}), bf16[8,128,6,128]{3,1,2,0:T(8,128)(2,1)}, u32[]{:S(2)}, u32[]{:S(2)}) %all-to-all-start) | async-done | bytes 1572896 | tf_op jit(solution)/shard_map/all_to_all | solution.py:50
  44.2 1.5 copy.246
  49.9 1.8 fusion.16
  51.7 9.0 %all-gather.2.cloned.1.call-done = bf16[4,128,2048]{2,1,0:T(8,128)(2,1)} async-done(((bf16[1,128,2048]{2,1,0:T(8,128)(2,1)}), bf16[4,128,2048]{2,1,0:T(8,128)(2,1)}) %all-gather.2.cloned.1.call-update) | async-done | bytes 2097168 | tf_op jit(solution)/shard_map/all_gather | solution.py:106
  60.7 2.2 %fusion.25 = f32[4,256]{1,0:T(4,128)S(1)} fusion(f32[512,256,4]{1,0,2:T(8,128)} %get-tuple-element.47, f32[4,256]{1,0:T(4,128)S(1)} %get-tuple-element.46, pred[256,512]{0,1:T(8,128)(4,1)S(1)} %compare_and_fusion.1), kind=kLoop, calls=%fused_computation.37 | loop fusion | flops 2096128 | bytes 2236416 | tf_op jit(solution)/shard_map/reduce_sum | solution.py:81
  62.9 1.8 fusion.51
  64.7 1.8 fusion.53
  66.6 1.7 fusion.52
  69.0 1.1 pad_maximum_fusion.1
  70.2 1.8 reshape_reshape.3
  72.0 2.2 %constant_dynamic-slice_fusion.1 = (bf16[4,1,128,512]{2,1,0,3:T(2,128)(2,1)S(1)}, bf16[4,1,128,512]{2,1,0,3:T(2,128)(2,1)S(1)}) fusion(bf16[4,2,128,512]{2,1,0,3:T(2,128)(2,1)S(1)} %reshape_reshape.3, s32[]{:T(128)S(6)} %select_n.77, s32[]{:T(128)S(6)} %select_n.76), kind=kLoop, calls=%fused_computation.181 | loop fusion | bytes 2097160 | tf_op jit(solution)/shard_map/jit(dynamic_index_in_dim)/dynamic_slice | solution.py:113
  74.1 1.3 fusion.73
  75.4 4.8 %bitcast_add_fusion = f32[512,2048]{1,0:T(8,128)} fusion(f32[512,2048,1]{1,0,2:T(8,128)S(1)} %fusion.73, bf16[4,128,2048]{2,1,0:T(8,128)(2,1)} %collective-permute-done, bf16[4,1,128,512]{2,1,0,3:T(2,128)(2,1)S(1)} %get-tuple-element.34), kind=kOutput, calls=%fused_computation | convolution fusion | flops 1074790400 | bytes 11010048 | tf_op jit(solution)/shard_map/dot_general | solution.py:117
  80.3 5.4 %copy.287 = f32[512,2048]{0,1:T(8,128)} copy(f32[512,2048]{1,0:T(8,128)} %bitcast_add_fusion) | data formatting | bytes 8388608 | tf_op jit(solution)/shard_map/add | solution.py:115
  85.6 4.8 %copy.288 = f32[512,8,4,64]{0,3,2,1:T(8,128)} copy(f32[512,8,4,64]{0,3,1,2:T(8,128)} %bitcast.434) | data formatting | bytes 8388608 | tf_op jit(solution)/shard_map/transpose | solution.py:189
  90.5 1.2 copy-done.7
  91.7 2.4 %convolution_convert_fusion = bf16[1024,2048]{1,0:T(8,128)(2,1)S(1)} fusion(bf16[1024,512]{0,1:T(8,128)(2,1)S(1)} %bitcast.457, bf16[512,2048]{1,0:T(8,128)(2,1)S(1)} %copy-done), kind=kOutput, calls=%fused_computation.2 | convolution fusion | flops 2149580800 | bytes 7340032 | tf_op jit(solution)/shard_map/dot_general | solution.py:100
  94.1 2.3 %copy.346 = bf16[4,2,128,2048]{3,2,0,1:T(8,128)(2,1)} copy(bf16[4,2,128,2048]{3,2,1,0:T(8,128)(2,1)S(1)} %bitcast.456) | data formatting | bytes 8388608 | tf_op jit(solution)/shard_map/reshape | solution.py:103
  96.4 1.3 fusion.46
  97.7 2.9 %fusion.43 = bf16[4,1,128,512]{3,2,0,1:T(8,128)(2,1)S(1)} fusion(bf16[4,128,2048]{2,1,0:T(8,128)(2,1)} %collective-permute-done, bf16[512,2048]{1,0:T(8,128)(2,1)S(1)} %copy-done), kind=kOutput, calls=%fused_computation.55 | convolution fusion | flops 1074003968 | bytes 4718592 | tf_op jit(solution)/shard_map/dot_general | solution.py:122
  100.8 0.9 copy.257
  102.5 12.1 %all_to_all.20 = bf16[2,4,128,2048]{3,2,1,0:T(8,128)(2,1)} all-to-all(bf16[2,4,128,2048]{3,2,1,0:T(8,128)(2,1)} %bitcast.433), channel_id=1, replica_groups=mesh['x'=4,'core'=2,'dpy'=4,'dpz'=8] {'core'}, dimensions={0} | all-to-all | bytes 8388608 | tf_op jit(solution)/shard_map/all_to_all | solution.py:132
  114.6 5.1 %reduce_sum.128 = bf16[4,128,2048]{2,1,0:T(8,128)(2,1)} reduce(bf16[2,4,128,2048]{3,2,1,0:T(8,128)(2,1)} %all_to_all.20, bf16[]{:T(256)} %constant.38.clone.1), dimensions={0}, to_apply=%region_11.12 | reduce | flops 1048576 | bytes 6291458 | tf_op jit(solution)/shard_map/reduce_sum | solution.py:133
  119.7 5.0 %all-to-all-start.2 = ((bf16[4,128,2048]{2,1,0:T(8,128)(2,1)}), bf16[4,128,2048]{2,1,0:T(8,128)(2,1)S(1)}, u32[]{:S(2)}, u32[]{:S(2)}) async-start(bf16[4,128,2048]{2,1,0:T(8,128)(2,1)} %reduce_sum.128), calls=%async_computation.2 | async-start | bytes 4194304 | tf_op jit(solution)/shard_map/all_to_all | solution.py:134
  124.8 1.1 multiply_reduce_fusion.3
  125.9 2.6 %fusion.28 = bf16[4,256,512]{1,2,0:T(8,128)(2,1)S(1)} fusion(f32[4,256]{1,0:T(4,128)S(1)} %bitcast.468, f32[4,256]{1,0:T(4,128)S(1)} %fusion.23, f32[4,256]{1,0:T(4,128)S(1)} %get-tuple-element.48, f32[512,256,4]{1,0,2:T(8,128)} %copy-done.15, pred[256,512]{0,1:T(8,128)(4,1)} %copy-done.27, bf16[1024,1,4,128]{0,3,2,1:T(8,128)(2,1)S(1)} %select_n.75, ...), kind=kOutput, calls=%fused_computation.42 | convolution fusion | flops 138412032 | bytes 3682304 | tf_op jit(solution)/shard_map/qkgd,skd->kgqs/dot_general | solution.py:151
  129.0 1.0 fusion.50
  129.9 1.0 fusion.54
  133.3 1.0 fusion.60
  134.4 15.9 %all-to-all-done.2 = bf16[4,128,2048]{2,1,0:T(8,128)(2,1)S(1)} async-done(((bf16[4,128,2048]{2,1,0:T(8,128)(2,1)}), bf16[4,128,2048]{2,1,0:T(8,128)(2,1)S(1)}, u32[]{:S(2)}, u32[]{:S(2)}) %all-to-all-start.2) | async-done | bytes 2097184 | tf_op jit(solution)/shard_map/all_to_all | solution.py:134
  150.2 1.2 multiply_reduce_fusion.1
  151.5 2.6 %fusion.29 = bf16[4,256,512]{1,2,0:T(8,128)(2,1)S(1)} fusion(f32[4,256]{1,0:T(4,128)S(1)} %bitcast.469, f32[4,256]{1,0:T(4,128)S(1)} %fusion.25, f32[4,256]{1,0:T(4,128)S(1)} %get-tuple-element.46, f32[512,256,4]{1,0,2:T(8,128)} %get-tuple-element.47, pred[256,512]{0,1:T(8,128)(4,1)} %copy-done.23, bf16[1024,1,4,128]{0,3,2,1:T(8,128)(2,1)S(1)} %select_n.75, ...), kind=kOutput, calls=%fused_computation.43 | convolution fusion | flops 138412032 | bytes 3682304 | tf_op jit(solution)/shard_map/qkgd,skd->kgqs/dot_general | solution.py:151
  158.2 1.0 copy-done.9
  160.2 1.4 pad_maximum_fusion
  161.6 5.6 %all-to-all-start.3 = ((bf16[8,128,6,128]{1,3,2,0:T(8,128)(2,1)}), bf16[8,128,6,128]{1,3,2,0:T(8,128)(2,1)}, u32[]{:S(2)}, u32[]{:S(2)}) async-start(bf16[8,128,6,128]{1,3,2,0:T(8,128)(2,1)} %pad_maximum_fusion), calls=%async_computation.3 | async-start | bytes 3145728 | tf_op jit(solution)/shard_map/all_to_all | solution.py:179
  167.9 1.3 reduce_sum.129
  169.2 18.2 %all-to-all-done.3 = bf16[8,128,6,128]{1,3,2,0:T(8,128)(2,1)} async-done(((bf16[8,128,6,128]{1,3,2,0:T(8,128)(2,1)}), bf16[8,128,6,128]{1,3,2,0:T(8,128)(2,1)}, u32[]{:S(2)}, u32[]{:S(2)}) %all-to-all-start.3) | async-done | bytes 1572896 | tf_op jit(solution)/shard_map/all_to_all | solution.py:179
  187.4 1.3 slice.205
  188.8 1.3 copy.289
  190.1 1.1 fusion.122
  191.1 0.9 copy.290
  192.8 3.9 %reduce-scatter.5.cloned.1.call-done = f32[512,64]{0,1:T(8,128)} async-done(((f32[512,256]{0,1:T(8,128)}), f32[512,64]{0,1:T(8,128)}) %reduce-scatter.5.cloned.1.call-update) | async-done | bytes 131088 | tf_op jit(solution)/shard_map/reduce_scatter | solution.py:193
  (135 shorter events, 17.0 us)
Async XLA Ops:
  7.2 83.4 %copy-start = (bf16[512,2048]{1,0:T(8,128)(2,1)S(1)}, bf16[512,2048]{1,0:T(8,128)(2,1)}, u32[]{:S(2)}) copy-start(bf16[512,2048]{1,0:T(8,128)(2,1)} %param.10) | copy-start | bytes 6291460
  16.8 7.3 %copy-start.40 = (s32[1,16]{1,0:T(1,128)S(1)}, s32[1,16]{1,0:T(1,128)}, u32[]{:S(2)}) copy-start(s32[1,16]{1,0:T(1,128)} %param.12) | copy-start | bytes 196
  16.8 7.4 %copy-start.41 = (s32[1,16]{1,0:T(1,128)S(1)}, s32[1,16]{1,0:T(1,128)}, u32[]{:S(2)}) copy-start(s32[1,16]{1,0:T(1,128)} %param.13) | copy-start | bytes 196
  16.8 27.4 %all-to-all-start = ((bf16[8,128,6,128]{3,1,2,0:T(8,128)(2,1)}), bf16[8,128,6,128]{3,1,2,0:T(8,128)(2,1)}, u32[]{:S(2)}, u32[]{:S(2)}) async-start(bf16[8,128,6,128]{3,1,2,0:T(8,128)(2,1)} %copy.245), calls=%async_computation | async-start | bytes 3145728 | tf_op jit(solution)/shard_map/all_to_all | solution.py:50
  23.3 37.3 %all-gather.2.cloned.1.call-start = ((), (), s32[]{:S(2)}) async-start(), calls=%async_computation.6 | async-start | bytes 2621440 | tf_op jit(solution)/shard_map/all_gather | solution.py:106
  24.0 143.2 %reduce-scatter.3.cloned.1.call-start = ((), (), s32[]{:S(2)}) async-start(), calls=%async_computation.7 | async-start | bytes 4718592 | tf_op jit(solution)/shard_map/reduce_scatter | solution.py:192
  24.9 41.6 %copy-start.23 = (pred[256,512]{0,1:T(8,128)(4,1)}, pred[256,512]{0,1:T(8,128)(4,1)S(1)}, u32[]{:S(2)}) copy-start(pred[256,512]{0,1:T(8,128)(4,1)S(1)} %compare_and_fusion.1) | copy-start | bytes 393220
  25.2 37.6 %copy-start.27 = (pred[256,512]{0,1:T(8,128)(4,1)}, pred[256,512]{0,1:T(8,128)(4,1)S(1)}, u32[]{:S(2)}) copy-start(pred[256,512]{0,1:T(8,128)(4,1)S(1)} %get-tuple-element.52) | copy-start | bytes 393220
  25.2 39.5 %copy-start.25 = (pred[256,512]{0,1:T(8,128)(4,1)}, pred[256,512]{0,1:T(8,128)(4,1)S(1)}, u32[]{:S(2)}) copy-start(pred[256,512]{0,1:T(8,128)(4,1)S(1)} %get-tuple-element.53) | copy-start | bytes 393220
  45.7 3.8 %copy-start.2 = (bf16[8,128,6,128]{3,1,0,2:T(8,128)(2,1)}, bf16[8,128,6,128]{3,1,0,2:T(8,128)(2,1)S(1)}, u32[]{:S(2)}) copy-start(bf16[8,128,6,128]{3,1,0,2:T(8,128)(2,1)S(1)} %copy.246) | copy-start | bytes 4718596
  46.0 3.0 %copy-start.5 = (f32[1,4,256,256]{2,3,1,0:T(8,128)}, f32[1,4,256,256]{2,3,1,0:T(8,128)S(1)}, u32[]{:S(2)}) copy-start(f32[1,4,256,256]{2,3,1,0:T(8,128)S(1)} %get-tuple-element.51) | copy-start | bytes 3145732
  46.2 82.3 %copy-start.34 = (f32[4,256]{1,0:T(4,128)}, f32[4,256]{1,0:T(4,128)S(1)}, u32[]{:S(2)}) copy-start(f32[4,256]{1,0:T(4,128)S(1)} %fusion.71) | copy-start | bytes 12292
  46.7 1.3 copy-start.15
  46.7 79.1 %copy-start.36 = (f32[4,256]{1,0:T(4,128)}, f32[4,256]{1,0:T(4,128)S(1)}, u32[]{:S(2)}) copy-start(f32[4,256]{1,0:T(4,128)S(1)} %get-tuple-element.48) | copy-start | bytes 12292
  48.1 77.8 %copy-start.38 = (f32[4,256]{1,0:T(4,128)}, f32[4,256]{1,0:T(4,128)S(1)}, u32[]{:S(2)}) copy-start(f32[4,256]{1,0:T(4,128)S(1)} %fusion.23) | copy-start | bytes 12292
  48.6 1.3 copy-start.12
  49.0 15.7 %copy-start.32 = (f32[4,256]{1,0:T(4,128)}, f32[4,256]{1,0:T(4,128)S(1)}, u32[]{:S(2)}) copy-start(f32[4,256]{1,0:T(4,128)S(1)} %fusion.27) | copy-start | bytes 12292
  60.6 2.2 %copy-start.16 = (f32[512,256,4]{1,0,2:T(8,128)S(1)}, f32[512,256,4]{1,0,2:T(8,128)}, u32[]{:S(2)}) copy-start(f32[512,256,4]{1,0,2:T(8,128)} %copy-done.15) | copy-start | bytes 6291460
  60.6 14.8 %collective-permute-start = (bf16[4,128,2048]{2,1,0:T(8,128)(2,1)}, bf16[4,128,2048]{2,1,0:T(8,128)(2,1)}, u32[]{:S(2)}, u32[]{:S(2)}) collective-permute-start(bf16[4,128,2048]{2,1,0:T(8,128)(2,1)} %all-gather.2.cloned.1.call-done), channel_id=1, source_target_pairs={{0,32},{32,0},{1,33},{33,1},{2,34},{34,2},{3,35},{35,3},{4,36},{36... | collective-permute-start | bytes 6291464 | tf_op jit(solution)/shard_map/ppermute | solution.py:107
  62.9 1.8 copy-start.13
  64.7 3.6 %copy-start.21 = (bf16[256,1,4,128]{0,3,2,1:T(8,128)(2,1)}, bf16[256,1,4,128]{0,3,2,1:T(8,128)(2,1)S(1)}, u32[]{:S(2)}) copy-start(bf16[256,1,4,128]{0,3,2,1:T(8,128)(2,1)S(1)} %fusion.51) | copy-start | bytes 786436
  64.7 1.8 copy-start.8
  66.6 1.8 copy-start.19
  68.3 0.7 copy-start.20
  71.9 2.2 %copy-start.10 = (bf16[4,128,2048]{2,1,0:T(8,128)(2,1)S(1)}, bf16[4,128,2048]{2,1,0:T(8,128)(2,1)}, u32[]{:S(2)}) copy-start(bf16[4,128,2048]{2,1,0:T(8,128)(2,1)} %all-gather.2.cloned.1.call-done) | copy-start | bytes 6291460
  90.5 1.2 copy-start.7
  94.1 2.3 %copy-start.11 = (bf16[4,128,2048]{2,1,0:T(8,128)(2,1)S(1)}, bf16[4,128,2048]{2,1,0:T(8,128)(2,1)}, u32[]{:S(2)}) copy-start(bf16[4,128,2048]{2,1,0:T(8,128)(2,1)} %all-gather.2.cloned.1.call-done) | copy-start | bytes 6291460
  119.7 30.5 %all-to-all-start.2 = ((bf16[4,128,2048]{2,1,0:T(8,128)(2,1)}), bf16[4,128,2048]{2,1,0:T(8,128)(2,1)S(1)}, u32[]{:S(2)}, u32[]{:S(2)}) async-start(bf16[4,128,2048]{2,1,0:T(8,128)(2,1)} %reduce_sum.128), calls=%async_computation.2 | async-start | bytes 4194304 | tf_op jit(solution)/shard_map/all_to_all | solution.py:134
  125.9 2.6 %copy-start.3 = (bf16[8,128,6,128]{3,1,0,2:T(8,128)(2,1)S(1)}, bf16[8,128,6,128]{3,1,0,2:T(8,128)(2,1)}, u32[]{:S(2)}) copy-start(bf16[8,128,6,128]{3,1,0,2:T(8,128)(2,1)} %copy-done.2) | copy-start | bytes 4718596
  125.9 2.6 %copy-start.6 = (f32[1,4,256,256]{2,3,1,0:T(8,128)S(1)}, f32[1,4,256,256]{2,3,1,0:T(8,128)}, u32[]{:S(2)}) copy-start(f32[1,4,256,256]{2,3,1,0:T(8,128)} %copy-done.5) | copy-start | bytes 3145732
  129.9 1.9 copy-start.17
  129.9 1.9 copy-start.28
  129.9 1.9 copy-start.37
  129.9 1.9 copy-start.39
  131.8 1.5 copy-start.35
  151.4 2.6 %copy-start.4 = (bf16[8,128,6,128]{3,1,0,2:T(8,128)(2,1)S(1)}, bf16[8,128,6,128]{3,1,0,2:T(8,128)(2,1)}, u32[]{:S(2)}) copy-start(bf16[8,128,6,128]{3,1,0,2:T(8,128)(2,1)} %copy-done.2) | copy-start | bytes 4718596
  151.4 3.0 %copy-start.14 = (f32[512,256,4]{1,0,2:T(8,128)S(1)}, f32[512,256,4]{1,0,2:T(8,128)}, u32[]{:S(2)}) copy-start(f32[512,256,4]{1,0,2:T(8,128)} %copy-done.12) | copy-start | bytes 6291460
  151.4 3.0 %copy-start.26 = (pred[256,512]{0,1:T(8,128)(4,1)S(1)}, pred[256,512]{0,1:T(8,128)(4,1)}, u32[]{:S(2)}) copy-start(pred[256,512]{0,1:T(8,128)(4,1)} %copy-done.25) | copy-start | bytes 393220
  151.4 3.0 %copy-start.33 = (f32[4,256]{1,0:T(4,128)S(1)}, f32[4,256]{1,0:T(4,128)}, u32[]{:S(2)}) copy-start(f32[4,256]{1,0:T(4,128)} %copy-done.32) | copy-start | bytes 12292
  154.4 1.2 copy-start.18
  154.4 1.2 copy-start.22
  157.6 1.6 copy-start.9
  157.6 1.6 copy-start.24
  159.2 1.0 copy-start.30
  159.2 1.0 copy-start.31
  161.6 25.9 %all-to-all-start.3 = ((bf16[8,128,6,128]{1,3,2,0:T(8,128)(2,1)}), bf16[8,128,6,128]{1,3,2,0:T(8,128)(2,1)}, u32[]{:S(2)}, u32[]{:S(2)}) async-start(bf16[8,128,6,128]{1,3,2,0:T(8,128)(2,1)} %pad_maximum_fusion), calls=%async_computation.3 | async-start | bytes 3145728 | tf_op jit(solution)/shard_map/all_to_all | solution.py:179
  167.2 29.5 %reduce-scatter.5.cloned.1.call-start = ((), (), s32[]{:S(2)}) async-start(), calls=%async_computation.8 | async-start | bytes 655360 | tf_op jit(solution)/shard_map/reduce_scatter | solution.py:193
  188.7 8.0 %copy-start.1 = (bf16[512,2048]{1,0:T(8,128)(2,1)S(1)}, bf16[512,2048]{1,0:T(8,128)(2,1)}, u32[]{:S(2)}) copy-start(bf16[512,2048]{1,0:T(8,128)(2,1)} %param.10) | copy-start | bytes 6291460
  (1 other events, 0.7 us)
Sparse Core Ops, SparseCore 0:
  25.9 34.6 all-gather.1
  90.6 55.8 reduce-scatter.2
  171.1 25.5 reduce-scatter.4

commit v8 on v6

--- a/solution.py
+++ b/solution.py
@@ -103,14 +103,23 @@
         .reshape(x_count, core_count, tok, product.shape[1])
         .transpose(1, 0, 2, 3)
     )
-    incoming = lax.all_gather(out_grad.reshape(tok, out_grad.shape[2]), SEQ, axis=0, tiled=True)
+    g_mine = lax.all_gather(out_grad.reshape(tok, out_grad.shape[2]), "x", axis=0, tiled=False)
+    g_other = lax.ppermute(
+        g_mine, "core", perm=[(c, (c + 1) % core_count) for c in range(core_count)]
+    )
+    core_at = lax.axis_index("core")
+    incoming = jnp.where(
+        core_at == 0,
+        jnp.stack([g_mine, g_other], axis=1),
+        jnp.stack([g_other, g_mine], axis=1),
+    ).reshape(win_rows, g_mine.shape[2])
     wo_grad = lax.dot_general(
         a_head, incoming, (((0,), (0,)), ((), ())), preferred_element_type=jnp.float32
     )
     d_rows = lax.dot_general(
         incoming, out_weight, (((1,), (1,)), ((), ())), preferred_element_type=jnp.float32
-    )
-    attention_grad = d_rows.astype(jnp.bfloat16).reshape(win_rows, hk, group_width, HEAD_SIZE)
+    ).astype(jnp.bfloat16)
+    attention_grad = d_rows.reshape(win_rows, hk, group_width, HEAD_SIZE)
     pieces, attention_grad = lax.optimization_barrier((pieces, attention_grad))
     pieces = lax.all_to_all(pieces, "core", split_axis=0, concat_axis=0, tiled=True)
     pieces = jnp.sum(pieces.astype(jnp.float32), axis=0).astype(jnp.bfloat16)

time: 191 us -> 203 us (1.063)
  matrix products: 31.2 us -> 36.6 us
  other arithmetic: 16.2 us -> 20 us
  local copies, waits for them, and re-layouts: 29.4 us -> 31.7 us
    dot_general x4, matrix products: 2.64 us -> 6.72 us  [local(): jnp.einsum('kgqs,skd->qkgd', attn_prob.astype(jnp.bfloat16), v_loc[k_star...]
    unnamed x77 -> x85, local copies, waits for them, and re-layouts: 13.1 us -> 15.4 us
    select_n x0 -> x1, other arithmetic: none -> 2.3 us  [local(): jnp.where(core_at == 0, jnp.stack([g_mine, g_other], axis=1), jnp.stack([...]
  transfers between devices with their start and end apart: 6 -> 7, of which waited for: 4 -> 4; matrix products, arithmetic and copies ran while one was open for 30% -> 32% of each run, Pallas kernels for 0% -> 0%
where the time goes in v8:
time: 203 us; the launch traced here: 202 us
  waiting for transfers between devices  72.9 us (36%)
  matrix products  36.6 us (18%)
  local copies, waits for them, and re-layouts  31.7 us (16%)
  other arithmetic  20 us (10%)
  starting transfers between devices  17.6 us (9%)
  between operations  14.4 us (7%)
  blocking collectives  8.39 us (4%)
    all_to_all x1, waiting for transfers between devices, local(): got = lax.all_to_all(packed, SEQ, split_axis=0, concat_axis=0, tiled=True)  34.4 us
    all_to_all x1, waiting for transfers between devices, local(): lax.all_to_all(packed_out, SEQ, split_axis=0, concat_axis=0, tiled=True)  18.2 us
    unnamed x85, local copies, waits for them, and re-layouts  15.4 us
    all_to_all x1, waiting for transfers between devices, local(): lax.all_to_all(pieces, 'x', split_axis=0, concat_axis=0, tiled=True)  15 us
    all_to_all x1, blocking collectives, local(): lax.all_to_all(pieces, 'core', split_axis=0, concat_axis=0, tiled=True)  8.39 us
    dot_general x4, matrix products, local(): jnp.einsum('kgqs,skd->qkgd', attn_prob.astype(jnp.bfloat16), v_loc[k_star...  6.72 us
    all_to_all x1, starting transfers between devices, local(): got = lax.all_to_all(packed, SEQ, split_axis=0, concat_axis=0, tiled=True)  6.56 us
    dot_general x1, local copies, waits for them, and re-layouts, local(): lax.dot_general(a_head, incoming, (((0,), (0,)), ((), ())), preferred_ele...  6.39 us
  transfers between devices with their start and end apart: 7, of which 4 were waited for; matrix products, arithmetic and copies ran while one was open for 32% of the time, Pallas kernels for 0%

profile of v8, /device:TPU:2, one launch (start us, length us, event | category | flops | bytes accessed | tf_op | source)
XLA Modules:
  0.0 201.6 jit_solution(1661733484020695615)
XLA Ops:
  7.9 1.1 copy.231
  9.0 1.8 copy.232
  10.8 1.6 copy.230
  12.5 2.3 %maximum_bitcast_fusion = bf16[8,128,6,128]{1,3,2,0:T(8,128)(2,1)} fusion(bf16[128,8,1,128]{0,3,2,1:T(8,128)(2,1)} %bitcast.440, bf16[128,8,1,128]{0,3,2,1:T(8,128)(2,1)S(1)} %bitcast.439, bf16[128,8,4,128]{0,3,2,1:T(8,128)(2,1)S(1)} %bitcast.431), kind=kLoop, calls=%fused_computation.37 | loop fusion | flops 1572864 | bytes 3145728 | tf_op jit(solution)/shard_map/transpose | solution.py:49
  14.7 2.6 %copy.235 = bf16[8,128,6,128]{3,1,2,0:T(8,128)(2,1)} copy(bf16[8,128,6,128]{1,3,2,0:T(8,128)(2,1)} %maximum_bitcast_fusion) | data formatting | bytes 3145728 | tf_op jit(solution)/shard_map/transpose | solution.py:49
  17.3 6.6 %all-to-all-start = ((bf16[8,128,6,128]{3,1,2,0:T(8,128)(2,1)}), bf16[8,128,6,128]{3,1,2,0:T(8,128)(2,1)}, u32[]{:S(2)}, u32[]{:S(2)}) async-start(bf16[8,128,6,128]{3,1,2,0:T(8,128)(2,1)} %copy.235), calls=%async_computation | async-start | bytes 3145728 | tf_op jit(solution)/shard_map/all_to_all | solution.py:50
  24.7 0.9 fusion.58
  25.7 34.4 %all-to-all-done = bf16[8,128,6,128]{3,1,2,0:T(8,128)(2,1)} async-done(((bf16[8,128,6,128]{3,1,2,0:T(8,128)(2,1)}), bf16[8,128,6,128]{3,1,2,0:T(8,128)(2,1)}, u32[]{:S(2)}, u32[]{:S(2)}) %all-to-all-start) | async-done | bytes 1572896 | tf_op jit(solution)/shard_map/all_to_all | solution.py:50
  60.1 1.5 copy.236
  62.4 1.3 copy-done.9
  64.8 1.3 copy-done.6
  66.6 1.8 fusion.15
  68.6 2.1 %fusion.19 = f32[4,256]{1,0:T(4,128)S(1)} fusion(f32[512,256,4]{1,0,2:T(8,128)} %get-tuple-element.47, f32[4,256]{1,0:T(4,128)S(1)} %get-tuple-element.46, pred[256,512]{0,1:T(8,128)(4,1)S(1)} %copy-done.30), kind=kLoop, calls=%fused_computation.32 | loop fusion | flops 2096128 | bytes 2236416 | tf_op jit(solution)/shard_map/reduce_sum | solution.py:81
  70.7 1.4 fusion.33
  72.3 1.8 fusion.37
  74.1 1.8 fusion.36
  76.0 1.7 fusion.35
  77.7 1.1 pad_maximum_fusion.1
  78.9 0.9 copy-done.14
  79.8 2.3 %maximum_select_fusion = bf16[4,2,128,2048]{3,2,1,0:T(8,128)(2,1)} fusion(bf16[4,1,128,2048]{3,2,1,0:T(8,128)(2,1)S(1)} %bitcast.438, bf16[4,1,128,2048]{3,2,1,0:T(8,128)(2,1)S(1)} %bitcast.437, pred[]{:T(512)S(6)} %eq.22), kind=kLoop, calls=%fused_computation | loop fusion | flops 6291456 | bytes 8388609 | tf_op jit(solution)/shard_map/jit(_where)/select_n | solution.py:111
  82.1 6.4 %copy.274 = bf16[2048,1024]{1,0:T(8,128)(2,1)} copy(bf16[2048,1024]{0,1:T(8,128)(2,1)} %bitcast.408) | data formatting | bytes 8388608 | tf_op jit(solution)/shard_map/dot_general | solution.py:116
  88.5 4.9 %convolution_bitcast_fusion = f32[512,8,4,64]{0,3,1,2:T(8,128)S(1)} fusion(bf16[1024,512,1,1]{0,1,3,2:T(8,128)(2,1)} %bitcast.451, bf16[4,8,64,1024]{3,2,1,0:T(8,128)(2,1)} %bitcast.433), kind=kOutput, calls=%fused_computation.3 | convolution fusion | flops 2147483648 | bytes 9437184 | tf_op jit(solution)/shard_map/dot_general | solution.py:116
  93.4 2.5 %copy.276 = f32[512,8,4,64]{0,3,2,1:T(8,128)} copy(f32[512,8,4,64]{0,3,1,2:T(8,128)S(1)} %convolution_bitcast_fusion) | data formatting | bytes 8388608 | tf_op jit(solution)/shard_map/transpose | solution.py:181
  95.9 3.6 %convolution_convert_fusion = bf16[1024,2048]{1,0:T(8,128)(2,1)S(1)} fusion(bf16[1024,512]{0,1:T(8,128)(2,1)} %bitcast.452, bf16[512,2048]{1,0:T(8,128)(2,1)S(1)} %copy-done), kind=kOutput, calls=%fused_computation.2 | convolution fusion | flops 2149580800 | bytes 7340032 | tf_op jit(solution)/shard_map/dot_general | solution.py:100
  100.1 1.6 copy-done.2
  101.7 3.4 %convolution_convert_fusion.1 = bf16[1024,512]{0,1:T(8,128)(2,1)} fusion(bf16[1024,2048]{1,0:T(8,128)(2,1)S(1)} %bitcast.409, bf16[512,2048]{1,0:T(8,128)(2,1)S(1)} %copy-done), kind=kOutput, calls=%fused_computation.39 | convolution fusion | flops 2148007936 | bytes 7340032 | tf_op jit(solution)/shard_map/dot_general | solution.py:119
  105.1 8.4 %all_to_all.20 = bf16[2,4,128,2048]{3,2,1,0:T(8,128)(2,1)} all-to-all(bf16[2,4,128,2048]{3,2,1,0:T(8,128)(2,1)S(1)} %bitcast.410), channel_id=1, replica_groups=mesh['x'=4,'core'=2,'dpy'=4,'dpz'=8] {'core'}, dimensions={0} | all-to-all | bytes 8388608 | tf_op jit(solution)/shard_map/all_to_all | solution.py:124
  113.5 5.1 %reduce_sum.128 = bf16[4,128,2048]{2,1,0:T(8,128)(2,1)} reduce(bf16[2,4,128,2048]{3,2,1,0:T(8,128)(2,1)} %all_to_all.20, bf16[]{:T(256)} %constant.30.clone.1), dimensions={0}, to_apply=%region_11.12 | reduce | flops 1048576 | bytes 6291458 | tf_op jit(solution)/shard_map/reduce_sum | solution.py:125
  118.6 5.3 %all-to-all-start.2 = ((bf16[4,128,2048]{2,1,0:T(8,128)(2,1)}), bf16[4,128,2048]{2,1,0:T(8,128)(2,1)S(1)}, u32[]{:S(2)}, u32[]{:S(2)}) async-start(bf16[4,128,2048]{2,1,0:T(8,128)(2,1)} %reduce_sum.128), calls=%async_computation.2 | async-start | bytes 4194304 | tf_op jit(solution)/shard_map/all_to_all | solution.py:126
  124.0 1.3 multiply_reduce_fusion.3
  125.3 2.7 %fusion.24 = bf16[4,256,512]{1,2,0:T(8,128)(2,1)S(1)} fusion(f32[4,256]{1,0:T(4,128)S(1)} %bitcast.459, f32[4,256]{1,0:T(4,128)S(1)} %fusion.19, f32[4,256]{1,0:T(4,128)S(1)} %get-tuple-element.46, f32[512,256,4]{1,0,2:T(8,128)} %get-tuple-element.47, pred[256,512]{0,1:T(8,128)(4,1)} %get-tuple-element.50, bf16[1024,1,4,128]{0,3,2,1:T(8,128)(2,1)} %bitcast.442, ...), kind=kOutput, calls=%fused_computation.40 | convolution fusion | flops 138412032 | bytes 3682304 | tf_op jit(solution)/shard_map/qkgd,skd->kgqs/dot_general | solution.py:143
  128.4 1.0 fusion.34
  129.4 1.0 fusion.38
  130.9 1.0 fusion.43
  133.4 1.0 fusion.44
  134.4 15.0 %all-to-all-done.2 = bf16[4,128,2048]{2,1,0:T(8,128)(2,1)S(1)} async-done(((bf16[4,128,2048]{2,1,0:T(8,128)(2,1)}), bf16[4,128,2048]{2,1,0:T(8,128)(2,1)S(1)}, u32[]{:S(2)}, u32[]{:S(2)}) %all-to-all-start.2) | async-done | bytes 2097184 | tf_op jit(solution)/shard_map/all_to_all | solution.py:126
  149.4 2.5 %convolution_bitcast_fusion.2 = f32[512,1,128]{0,2,1:T(8,128)S(1)} fusion(bf16[1024,1,4,128]{0,3,2,1:T(8,128)(2,1)} %bitcast.443, f32[4,256]{1,0:T(4,128)S(1)} %fusion.23, f32[4,256]{1,0:T(4,128)S(1)} %get-tuple-element.42, f32[512,256,4]{1,0,2:T(8,128)} %copy-done.9, pred[256,512]{0,1:T(8,128)(4,1)} %copy-done.27), kind=kOutput, calls=%fused_computation.67 | convolution fusion | flops 136839168 | bytes 2760704 | tf_op jit(solution)/shard_map/kgqs,qkgd->skd/dot_general | solution.py:153
  152.5 0.8 fusion.26
  158.6 1.4 pad_maximum_fusion
  160.0 5.6 %all-to-all-start.3 = ((bf16[8,128,6,128]{1,3,2,0:T(8,128)(2,1)}), bf16[8,128,6,128]{1,3,2,0:T(8,128)(2,1)}, u32[]{:S(2)}, u32[]{:S(2)}) async-start(bf16[8,128,6,128]{1,3,2,0:T(8,128)(2,1)} %pad_maximum_fusion), calls=%async_computation.3 | async-start | bytes 3145728 | tf_op jit(solution)/shard_map/all_to_all | solution.py:171
  166.3 1.3 reduce_sum.129
  167.6 18.2 %all-to-all-done.3 = bf16[8,128,6,128]{1,3,2,0:T(8,128)(2,1)} async-done(((bf16[8,128,6,128]{1,3,2,0:T(8,128)(2,1)}), bf16[8,128,6,128]{1,3,2,0:T(8,128)(2,1)}, u32[]{:S(2)}, u32[]{:S(2)}) %all-to-all-start.3) | async-done | bytes 1572896 | tf_op jit(solution)/shard_map/all_to_all | solution.py:171
  185.8 1.3 slice.205
  187.1 1.3 copy.277
  188.4 1.1 fusion.101
  189.5 0.9 copy.279
  190.4 0.8 copy.278
  191.2 3.8 %reduce-scatter.5.cloned.1.call-done = f32[512,64]{0,1:T(8,128)} async-done(((f32[512,256]{0,1:T(8,128)}), f32[512,64]{0,1:T(8,128)}) %reduce-scatter.5.cloned.1.call-update) | async-done | bytes 131088 | tf_op jit(solution)/shard_map/reduce_scatter | solution.py:185
  (123 shorter events, 13.5 us)
Async XLA Ops:
  7.2 88.8 %copy-start = (bf16[512,2048]{1,0:T(8,128)(2,1)S(1)}, bf16[512,2048]{1,0:T(8,128)(2,1)}, u32[]{:S(2)}) copy-start(bf16[512,2048]{1,0:T(8,128)(2,1)} %param.10) | copy-start | bytes 6291460
  7.2 61.2 %all-gather.2.cloned.1.call-start = ((), (), s32[]{:S(2)}) async-start(), calls=%async_computation.6 | async-start | bytes 2621440 | tf_op jit(solution)/shard_map/all_gather | solution.py:106
  17.3 6.6 %copy-start.37 = (s32[1,16]{1,0:T(1,128)S(1)}, s32[1,16]{1,0:T(1,128)}, u32[]{:S(2)}) copy-start(s32[1,16]{1,0:T(1,128)} %param.12) | copy-start | bytes 196
  17.3 6.6 %copy-start.38 = (s32[1,16]{1,0:T(1,128)S(1)}, s32[1,16]{1,0:T(1,128)}, u32[]{:S(2)}) copy-start(s32[1,16]{1,0:T(1,128)} %param.13) | copy-start | bytes 196
  17.3 42.8 %all-to-all-start = ((bf16[8,128,6,128]{3,1,2,0:T(8,128)(2,1)}), bf16[8,128,6,128]{3,1,2,0:T(8,128)(2,1)}, u32[]{:S(2)}, u32[]{:S(2)}) async-start(bf16[8,128,6,128]{3,1,2,0:T(8,128)(2,1)} %copy.235), calls=%async_computation | async-start | bytes 3145728 | tf_op jit(solution)/shard_map/all_to_all | solution.py:50
  23.9 141.7 %reduce-scatter.3.cloned.1.call-start = ((), (), s32[]{:S(2)}) async-start(), calls=%async_computation.7 | async-start | bytes 4718592 | tf_op jit(solution)/shard_map/reduce_scatter | solution.py:184
  24.7 40.1 %copy-start.24 = (pred[256,512]{0,1:T(8,128)(4,1)}, pred[256,512]{0,1:T(8,128)(4,1)S(1)}, u32[]{:S(2)}) copy-start(pred[256,512]{0,1:T(8,128)(4,1)S(1)} %compare_and_fusion.1) | copy-start | bytes 393220
  25.7 36.8 %copy-start.27 = (pred[256,512]{0,1:T(8,128)(4,1)}, pred[256,512]{0,1:T(8,128)(4,1)S(1)}, u32[]{:S(2)}) copy-start(pred[256,512]{0,1:T(8,128)(4,1)S(1)} %get-tuple-element.51) | copy-start | bytes 393220
  61.6 5.0 %copy-start.3 = (bf16[8,128,6,128]{3,1,0,2:T(8,128)(2,1)}, bf16[8,128,6,128]{3,1,0,2:T(8,128)(2,1)S(1)}, u32[]{:S(2)}) copy-start(bf16[8,128,6,128]{3,1,0,2:T(8,128)(2,1)S(1)} %copy.236) | copy-start | bytes 4718596
  62.4 1.4 copy-start.9
  64.3 2.3 %copy-start.30 = (pred[256,512]{0,1:T(8,128)(4,1)S(1)}, pred[256,512]{0,1:T(8,128)(4,1)}, u32[]{:S(2)}) copy-start(pred[256,512]{0,1:T(8,128)(4,1)} %get-tuple-element.50) | copy-start | bytes 393220
  64.7 1.3 copy-start.6
  68.4 10.5 %collective-permute-start = (bf16[4,128,2048]{2,1,0:T(8,128)(2,1)}, bf16[4,128,2048]{2,1,0:T(8,128)(2,1)S(1)}, u32[]{:S(2)}, u32[]{:S(2)}) collective-permute-start(bf16[4,128,2048]{2,1,0:T(8,128)(2,1)} %all-gather.2.cloned.1.call-done), channel_id=1, source_target_pairs={{0,32},{32,0},{1,33},{33,1},{2,34},{34,2},{3,35},{35,3},{4,36},{36... | collective-permute-start | bytes 6291464 | tf_op jit(solution)/shard_map/ppermute | solution.py:107
  70.6 1.6 copy-start.10
  70.7 1.6 copy-start.28
  72.3 1.8 copy-start.7
  72.3 1.8 copy-start.25
  74.1 3.6 %copy-start.18 = (bf16[256,1,4,128]{0,3,2,1:T(8,128)(2,1)}, bf16[256,1,4,128]{0,3,2,1:T(8,128)(2,1)S(1)}, u32[]{:S(2)}) copy-start(bf16[256,1,4,128]{0,3,2,1:T(8,128)(2,1)S(1)} %fusion.37) | copy-start | bytes 786436
  74.1 1.8 copy-start.12
  74.1 1.8 copy-start.31
  75.9 1.8 copy-start.20
  77.7 1.1 copy-start.23
  77.7 2.1 %copy-start.14 = (bf16[4,128,2048]{2,1,0:T(8,128)(2,1)S(1)}, bf16[4,128,2048]{2,1,0:T(8,128)(2,1)}, u32[]{:S(2)}) copy-start(bf16[4,128,2048]{2,1,0:T(8,128)(2,1)} %all-gather.2.cloned.1.call-done) | copy-start | bytes 6291460
  99.6 2.2 %copy-start.2 = (bf16[4,2,128,2048]{3,2,1,0:T(8,128)(2,1)S(1)}, bf16[4,2,128,2048]{3,2,1,0:T(8,128)(2,1)}, u32[]{:S(2)}) copy-start(bf16[4,2,128,2048]{3,2,1,0:T(8,128)(2,1)} %maximum_select_fusion) | copy-start | bytes 12582916
  118.6 30.8 %all-to-all-start.2 = ((bf16[4,128,2048]{2,1,0:T(8,128)(2,1)}), bf16[4,128,2048]{2,1,0:T(8,128)(2,1)S(1)}, u32[]{:S(2)}, u32[]{:S(2)}) async-start(bf16[4,128,2048]{2,1,0:T(8,128)(2,1)} %reduce_sum.128), calls=%async_computation.2 | async-start | bytes 4194304 | tf_op jit(solution)/shard_map/all_to_all | solution.py:126
  125.2 2.8 %copy-start.4 = (bf16[8,128,6,128]{3,1,0,2:T(8,128)(2,1)S(1)}, bf16[8,128,6,128]{3,1,0,2:T(8,128)(2,1)}, u32[]{:S(2)}) copy-start(bf16[8,128,6,128]{3,1,0,2:T(8,128)(2,1)} %copy-done.3) | copy-start | bytes 4718596
  125.2 2.8 %copy-start.15 = (bf16[1024,512]{0,1:T(8,128)(2,1)S(1)}, bf16[1024,512]{0,1:T(8,128)(2,1)}, u32[]{:S(2)}) copy-start(bf16[1024,512]{0,1:T(8,128)(2,1)} %convolution_convert_fusion.1) | copy-start | bytes 3145732
  129.4 2.5 %copy-start.13 = (f32[512,256,4]{1,0,2:T(8,128)S(1)}, f32[512,256,4]{1,0,2:T(8,128)}, u32[]{:S(2)}) copy-start(f32[512,256,4]{1,0,2:T(8,128)} %get-tuple-element.47) | copy-start | bytes 6291460
  129.4 2.5 %copy-start.32 = (pred[256,512]{0,1:T(8,128)(4,1)S(1)}, pred[256,512]{0,1:T(8,128)(4,1)}, u32[]{:S(2)}) copy-start(pred[256,512]{0,1:T(8,128)(4,1)} %get-tuple-element.50) | copy-start | bytes 393220
  132.7 0.7 copy-start.34
  134.4 17.6 %copy-start.16 = (bf16[1024,512]{0,1:T(8,128)(2,1)S(1)}, bf16[1024,512]{0,1:T(8,128)(2,1)}, u32[]{:S(2)}) copy-start(bf16[1024,512]{0,1:T(8,128)(2,1)} %convolution_convert_fusion.1) | copy-start | bytes 3145732
  134.4 17.8 %copy-start.29 = (pred[256,512]{0,1:T(8,128)(4,1)S(1)}, pred[256,512]{0,1:T(8,128)(4,1)}, u32[]{:S(2)}) copy-start(pred[256,512]{0,1:T(8,128)(4,1)} %copy-done.27) | copy-start | bytes 393220
  149.4 2.6 %copy-start.19 = (bf16[256,1,4,128]{0,3,2,1:T(8,128)(2,1)S(1)}, bf16[256,1,4,128]{0,3,2,1:T(8,128)(2,1)}, u32[]{:S(2)}) copy-start(bf16[256,1,4,128]{0,3,2,1:T(8,128)(2,1)} %copy-done.18) | copy-start | bytes 786436
  149.4 2.6 %copy-start.21 = (bf16[256,1,4,128]{0,3,2,1:T(8,128)(2,1)S(1)}, bf16[256,1,4,128]{0,3,2,1:T(8,128)(2,1)}, u32[]{:S(2)}) copy-start(bf16[256,1,4,128]{0,3,2,1:T(8,128)(2,1)} %copy-done.20) | copy-start | bytes 786436
  149.4 2.8 %copy-start.5 = (bf16[8,128,6,128]{3,1,0,2:T(8,128)(2,1)S(1)}, bf16[8,128,6,128]{3,1,0,2:T(8,128)(2,1)}, u32[]{:S(2)}) copy-start(bf16[8,128,6,128]{3,1,0,2:T(8,128)(2,1)} %copy-done.3) | copy-start | bytes 4718596
  149.4 3.0 %copy-start.11 = (f32[512,256,4]{1,0,2:T(8,128)S(1)}, f32[512,256,4]{1,0,2:T(8,128)}, u32[]{:S(2)}) copy-start(f32[512,256,4]{1,0,2:T(8,128)} %copy-done.9) | copy-start | bytes 6291460
  153.3 1.6 copy-start.8
  153.3 1.6 copy-start.26
  154.9 1.2 copy-start.17
  154.9 1.2 copy-start.22
  156.7 1.0 copy-start.35
  156.8 1.0 copy-start.36
  157.7 0.8 copy-start.33
  160.0 25.9 %all-to-all-start.3 = ((bf16[8,128,6,128]{1,3,2,0:T(8,128)(2,1)}), bf16[8,128,6,128]{1,3,2,0:T(8,128)(2,1)}, u32[]{:S(2)}, u32[]{:S(2)}) async-start(bf16[8,128,6,128]{1,3,2,0:T(8,128)(2,1)} %pad_maximum_fusion), calls=%async_computation.3 | async-start | bytes 3145728 | tf_op jit(solution)/shard_map/all_to_all | solution.py:171
  165.6 29.4 %reduce-scatter.5.cloned.1.call-start = ((), (), s32[]{:S(2)}) async-start(), calls=%async_computation.8 | async-start | bytes 655360 | tf_op jit(solution)/shard_map/reduce_scatter | solution.py:185
  187.1 7.9 %copy-start.1 = (bf16[512,2048]{1,0:T(8,128)(2,1)S(1)}, bf16[512,2048]{1,0:T(8,128)(2,1)}, u32[]{:S(2)}) copy-start(bf16[512,2048]{1,0:T(8,128)(2,1)} %param.10) | copy-start | bytes 6291460
Sparse Core Ops, SparseCore 0:
  9.8 50.7 all-gather.1
  96.1 55.8 reduce-scatter.2
  169.5 25.5 reduce-scatter.4

commit v9 on v8

--- a/solution.py
+++ b/solution.py
@@ -48,6 +48,7 @@
         axis=2,
     ).transpose(1, 0, 2, 3)
     got = lax.all_to_all(packed, SEQ, split_axis=0, concat_axis=0, tiled=True)
+    got, out_grad = lax.optimization_barrier((got, out_grad))
     win_rows = seq_count * tok
     got = got.reshape(win_rows, hq + 2 * hk, HEAD_SIZE)
     query_head_rows = got[:, :hq].reshape(win_rows, hk, group_width, HEAD_SIZE)

time: 203 us -> 210 us (1.034)
  blocking collectives: 8.39 us -> 35.3 us
  waiting for transfers between devices: 72.9 us -> 60.9 us
  starting transfers between devices: 17.6 us -> 10.8 us
    all_to_all x1 -> x0, waiting for transfers between devices: 34.4 us -> none  [local(): got = lax.all_to_all(packed, SEQ, split_axis=0, concat_axis=0, tiled=True)]
    all_to_all x0 -> x1, blocking collectives: none -> 27 us  [local(): got = lax.all_to_all(packed, SEQ, split_axis=0, concat_axis=0, tiled=True)]
    all_gather x1, waiting for transfers between devices: 0.01 us -> 23.2 us  [local(): lax.all_gather(out_grad.reshape(tok, out_grad.shape[2]), 'x', axis=0, til...]
    all_to_all x1 -> x0, starting transfers between devices: 6.56 us -> none  [local(): got = lax.all_to_all(packed, SEQ, split_axis=0, concat_axis=0, tiled=True)]
  transfers between devices with their start and end apart: 7 -> 6, of which waited for: 4 -> 4; matrix products, arithmetic and copies ran while one was open for 32% -> 26% of each run, Pallas kernels for 0% -> 0%
where the time goes in v9:
time: 210 us; the launch traced here: 209 us
  waiting for transfers between devices  60.9 us (29%)
  matrix products  36.7 us (17%)
  blocking collectives  35.3 us (17%)
  local copies, waits for them, and re-layouts  31.9 us (15%)
  other arithmetic  19.4 us (9%)
  between operations  14.4 us (7%)
  starting transfers between devices  10.8 us (5%)
    all_to_all x1, blocking collectives, local(): got = lax.all_to_all(packed, SEQ, split_axis=0, concat_axis=0, tiled=True)  27 us
    all_gather x1, waiting for transfers between devices, local(): lax.all_gather(out_grad.reshape(tok, out_grad.shape[2]), 'x', axis=0, til...  23.2 us
    all_to_all x1, waiting for transfers between devices, local(): lax.all_to_all(packed_out, SEQ, split_axis=0, concat_axis=0, tiled=True)  18.2 us
    unnamed x85, local copies, waits for them, and re-layouts  15.5 us
    all_to_all x1, waiting for transfers between devices, local(): lax.all_to_all(pieces, 'x', split_axis=0, concat_axis=0, tiled=True)  15 us
    all_to_all x1, blocking collectives, local(): lax.all_to_all(pieces, 'core', split_axis=0, concat_axis=0, tiled=True)  8.38 us
    dot_general x4, matrix products, local(): jnp.einsum('kgqs,skd->qkgd', attn_prob.astype(jnp.bfloat16), v_loc[k_star...  6.72 us
    dot_general x1, local copies, waits for them, and re-layouts, local(): lax.dot_general(a_head, incoming, (((0,), (0,)), ((), ())), preferred_ele...  6.39 us
  transfers between devices with their start and end apart: 6, of which 4 were waited for; matrix products, arithmetic and copies ran while one was open for 26% of the time, Pallas kernels for 0%

profile of v9, /device:TPU:2, one launch (start us, length us, event | category | flops | bytes accessed | tf_op | source)
XLA Modules:
  0.0 209.4 jit_solution(7542001774809897638)
XLA Ops:
  7.2 1.3 copy.231
  8.5 1.8 copy.232
  10.3 1.6 copy.230
  11.9 2.3 %maximum_bitcast_fusion = bf16[8,128,6,128]{1,3,2,0:T(8,128)(2,1)} fusion(bf16[128,8,1,128]{0,3,2,1:T(8,128)(2,1)} %bitcast.440, bf16[128,8,1,128]{0,3,2,1:T(8,128)(2,1)S(1)} %bitcast.439, bf16[128,8,4,128]{0,3,2,1:T(8,128)(2,1)S(1)} %bitcast.431), kind=kLoop, calls=%fused_computation.37 | loop fusion | flops 1572864 | bytes 3145728 | tf_op jit(solution)/shard_map/transpose | solution.py:49
  14.2 2.6 %copy.235 = bf16[8,128,6,128]{3,1,2,0:T(8,128)(2,1)} copy(bf16[8,128,6,128]{1,3,2,0:T(8,128)(2,1)} %maximum_bitcast_fusion) | data formatting | bytes 3145728 | tf_op jit(solution)/shard_map/transpose | solution.py:49
  16.8 27.0 %all_to_all.20 = bf16[8,128,6,128]{3,1,2,0:T(8,128)(2,1)} all-to-all(bf16[8,128,6,128]{3,1,2,0:T(8,128)(2,1)} %copy.235), channel_id=1, replica_groups=mesh['x'=4,'core'=2,'dpy'=4,'dpz'=8] {'x','core'}, dimensions={0} | all-to-all | bytes 3145728 | tf_op jit(solution)/shard_map/all_to_all | solution.py:50
  45.0 1.6 copy.236
  47.4 1.3 copy-done.9
  49.7 1.3 copy-done.6
  51.5 1.8 fusion.15
  53.3 23.2 %all-gather.2.cloned.1.call-done = bf16[4,128,2048]{2,1,0:T(8,128)(2,1)} async-done(((bf16[1,128,2048]{2,1,0:T(8,128)(2,1)}), bf16[4,128,2048]{2,1,0:T(8,128)(2,1)}) %all-gather.2.cloned.1.call-update) | async-done | bytes 2097168 | tf_op jit(solution)/shard_map/all_gather | solution.py:107
  76.8 2.1 fusion.19
  78.8 1.4 fusion.33
  80.5 1.8 fusion.37
  82.3 1.8 fusion.36
  84.1 1.7 fusion.35
  85.9 1.1 pad_maximum_fusion.1
  87.0 0.9 copy-done.14
  88.0 2.3 %maximum_select_fusion = bf16[4,2,128,2048]{3,2,1,0:T(8,128)(2,1)} fusion(bf16[4,1,128,2048]{3,2,1,0:T(8,128)(2,1)S(1)} %bitcast.438, bf16[4,1,128,2048]{3,2,1,0:T(8,128)(2,1)S(1)} %bitcast.437, pred[]{:T(512)S(6)} %eq.22), kind=kLoop, calls=%fused_computation | loop fusion | flops 6291456 | bytes 8388609 | tf_op jit(solution)/shard_map/jit(_where)/select_n | solution.py:112
  90.3 6.4 %copy.274 = bf16[2048,1024]{1,0:T(8,128)(2,1)} copy(bf16[2048,1024]{0,1:T(8,128)(2,1)} %bitcast.408) | data formatting | bytes 8388608 | tf_op jit(solution)/shard_map/dot_general | solution.py:117
  96.7 4.9 %convolution_bitcast_fusion = f32[512,8,4,64]{0,3,1,2:T(8,128)S(1)} fusion(bf16[1024,512,1,1]{0,1,3,2:T(8,128)(2,1)} %bitcast.451, bf16[4,8,64,1024]{3,2,1,0:T(8,128)(2,1)} %bitcast.433), kind=kOutput, calls=%fused_computation.3 | convolution fusion | flops 2147483648 | bytes 9437184 | tf_op jit(solution)/shard_map/dot_general | solution.py:117
  101.6 2.5 %copy.276 = f32[512,8,4,64]{0,3,2,1:T(8,128)} copy(f32[512,8,4,64]{0,3,1,2:T(8,128)S(1)} %convolution_bitcast_fusion) | data formatting | bytes 8388608 | tf_op jit(solution)/shard_map/transpose | solution.py:182
  104.1 3.6 %convolution_convert_fusion = bf16[1024,2048]{1,0:T(8,128)(2,1)S(1)} fusion(bf16[1024,512]{0,1:T(8,128)(2,1)} %bitcast.452, bf16[512,2048]{1,0:T(8,128)(2,1)S(1)} %copy-done), kind=kOutput, calls=%fused_computation.2 | convolution fusion | flops 2149580800 | bytes 7340032 | tf_op jit(solution)/shard_map/dot_general | solution.py:101
  108.3 1.6 copy-done.2
  109.9 3.4 %convolution_convert_fusion.1 = bf16[1024,512]{0,1:T(8,128)(2,1)} fusion(bf16[1024,2048]{1,0:T(8,128)(2,1)S(1)} %bitcast.409, bf16[512,2048]{1,0:T(8,128)(2,1)S(1)} %copy-done), kind=kOutput, calls=%fused_computation.39 | convolution fusion | flops 2148007936 | bytes 7340032 | tf_op jit(solution)/shard_map/dot_general | solution.py:120
  113.3 8.4 %all_to_all.21 = bf16[2,4,128,2048]{3,2,1,0:T(8,128)(2,1)} all-to-all(bf16[2,4,128,2048]{3,2,1,0:T(8,128)(2,1)S(1)} %bitcast.410), channel_id=1, replica_groups=mesh['x'=4,'core'=2,'dpy'=4,'dpz'=8] {'core'}, dimensions={0} | all-to-all | bytes 8388608 | tf_op jit(solution)/shard_map/all_to_all | solution.py:125
  121.6 5.1 %reduce_sum.128 = bf16[4,128,2048]{2,1,0:T(8,128)(2,1)} reduce(bf16[2,4,128,2048]{3,2,1,0:T(8,128)(2,1)} %all_to_all.21, bf16[]{:T(256)} %constant.30.clone.1), dimensions={0}, to_apply=%region_11.12 | reduce | flops 1048576 | bytes 6291458 | tf_op jit(solution)/shard_map/reduce_sum | solution.py:126
  126.8 5.1 %all-to-all-start.2 = ((bf16[4,128,2048]{2,1,0:T(8,128)(2,1)}), bf16[4,128,2048]{2,1,0:T(8,128)(2,1)S(1)}, u32[]{:S(2)}, u32[]{:S(2)}) async-start(bf16[4,128,2048]{2,1,0:T(8,128)(2,1)} %reduce_sum.128), calls=%async_computation.2 | async-start | bytes 4194304 | tf_op jit(solution)/shard_map/all_to_all | solution.py:127
  131.8 1.3 multiply_reduce_fusion.3
  133.1 2.8 %fusion.24 = bf16[4,256,512]{1,2,0:T(8,128)(2,1)S(1)} fusion(f32[4,256]{1,0:T(4,128)S(1)} %bitcast.459, f32[4,256]{1,0:T(4,128)S(1)} %fusion.19, f32[4,256]{1,0:T(4,128)S(1)} %get-tuple-element.50, f32[512,256,4]{1,0,2:T(8,128)} %get-tuple-element.51, pred[256,512]{0,1:T(8,128)(4,1)} %copy-done.30, bf16[1024,1,4,128]{0,3,2,1:T(8,128)(2,1)} %bitcast.442, ...), kind=kOutput, calls=%fused_computation.40 | convolution fusion | flops 138412032 | bytes 3682304 | tf_op jit(solution)/shard_map/qkgd,skd->kgqs/dot_general | solution.py:144
  136.3 1.0 fusion.34
  137.3 1.0 fusion.38
  138.8 1.0 fusion.43
  141.3 1.0 fusion.44
  142.3 15.0 %all-to-all-done.2 = bf16[4,128,2048]{2,1,0:T(8,128)(2,1)S(1)} async-done(((bf16[4,128,2048]{2,1,0:T(8,128)(2,1)}), bf16[4,128,2048]{2,1,0:T(8,128)(2,1)S(1)}, u32[]{:S(2)}, u32[]{:S(2)}) %all-to-all-start.2) | async-done | bytes 2097184 | tf_op jit(solution)/shard_map/all_to_all | solution.py:127
  157.3 2.6 %convolution_bitcast_fusion.2 = f32[512,1,128]{0,2,1:T(8,128)S(1)} fusion(bf16[1024,1,4,128]{0,3,2,1:T(8,128)(2,1)} %bitcast.443, f32[4,256]{1,0:T(4,128)S(1)} %fusion.23, f32[4,256]{1,0:T(4,128)S(1)} %get-tuple-element.46, f32[512,256,4]{1,0,2:T(8,128)} %copy-done.9, pred[256,512]{0,1:T(8,128)(4,1)} %copy-done.27), kind=kOutput, calls=%fused_computation.67 | convolution fusion | flops 136839168 | bytes 2760704 | tf_op jit(solution)/shard_map/kgqs,qkgd->skd/dot_general | solution.py:154
  160.3 0.8 fusion.26
  162.8 0.8 fusion.25
  166.5 1.4 pad_maximum_fusion
  167.9 5.6 %all-to-all-start.3 = ((bf16[8,128,6,128]{1,3,2,0:T(8,128)(2,1)}), bf16[8,128,6,128]{1,3,2,0:T(8,128)(2,1)}, u32[]{:S(2)}, u32[]{:S(2)}) async-start(bf16[8,128,6,128]{1,3,2,0:T(8,128)(2,1)} %pad_maximum_fusion), calls=%async_computation.3 | async-start | bytes 3145728 | tf_op jit(solution)/shard_map/all_to_all | solution.py:172
  174.2 1.3 reduce_sum.129
  175.5 18.2 %all-to-all-done.3 = bf16[8,128,6,128]{1,3,2,0:T(8,128)(2,1)} async-done(((bf16[8,128,6,128]{1,3,2,0:T(8,128)(2,1)}), bf16[8,128,6,128]{1,3,2,0:T(8,128)(2,1)}, u32[]{:S(2)}, u32[]{:S(2)}) %all-to-all-start.3) | async-done | bytes 1572896 | tf_op jit(solution)/shard_map/all_to_all | solution.py:172
  193.7 1.3 slice.205
  195.0 1.3 copy.277
  196.3 1.1 fusion.101
  197.4 0.9 copy.279
  198.3 0.8 copy.278
  199.1 3.7 %reduce-scatter.5.cloned.1.call-done = f32[512,64]{0,1:T(8,128)} async-done(((f32[512,256]{0,1:T(8,128)}), f32[512,64]{0,1:T(8,128)}) %reduce-scatter.5.cloned.1.call-update) | async-done | bytes 131088 | tf_op jit(solution)/shard_map/reduce_scatter | solution.py:186
  (122 shorter events, 12.3 us)
Async XLA Ops:
  7.2 96.9 %copy-start = (bf16[512,2048]{1,0:T(8,128)(2,1)S(1)}, bf16[512,2048]{1,0:T(8,128)(2,1)}, u32[]{:S(2)}) copy-start(bf16[512,2048]{1,0:T(8,128)(2,1)} %param.10) | copy-start | bytes 6291460
  7.2 69.4 %all-gather.2.cloned.1.call-start = ((), (), s32[]{:S(2)}) async-start(), calls=%async_computation.6 | async-start | bytes 2621440 | tf_op jit(solution)/shard_map/all_gather | solution.py:107
  16.8 27.0 %copy-start.37 = (s32[1,16]{1,0:T(1,128)S(1)}, s32[1,16]{1,0:T(1,128)}, u32[]{:S(2)}) copy-start(s32[1,16]{1,0:T(1,128)} %param.12) | copy-start | bytes 196
  16.8 27.0 %copy-start.38 = (s32[1,16]{1,0:T(1,128)S(1)}, s32[1,16]{1,0:T(1,128)}, u32[]{:S(2)}) copy-start(s32[1,16]{1,0:T(1,128)} %param.13) | copy-start | bytes 196
  43.8 129.7 %reduce-scatter.3.cloned.1.call-start = ((), (), s32[]{:S(2)}) async-start(), calls=%async_computation.7 | async-start | bytes 4718592 | tf_op jit(solution)/shard_map/reduce_scatter | solution.py:185
  44.7 5.1 %copy-start.24 = (pred[256,512]{0,1:T(8,128)(4,1)}, pred[256,512]{0,1:T(8,128)(4,1)S(1)}, u32[]{:S(2)}) copy-start(pred[256,512]{0,1:T(8,128)(4,1)S(1)} %compare_and_fusion.1) | copy-start | bytes 393220
  45.0 2.5 %copy-start.27 = (pred[256,512]{0,1:T(8,128)(4,1)}, pred[256,512]{0,1:T(8,128)(4,1)S(1)}, u32[]{:S(2)}) copy-start(pred[256,512]{0,1:T(8,128)(4,1)S(1)} %get-tuple-element.55) | copy-start | bytes 393220
  45.0 6.5 %copy-start.30 = (pred[256,512]{0,1:T(8,128)(4,1)}, pred[256,512]{0,1:T(8,128)(4,1)S(1)}, u32[]{:S(2)}) copy-start(pred[256,512]{0,1:T(8,128)(4,1)S(1)} %get-tuple-element.54) | copy-start | bytes 393220
  46.6 4.9 %copy-start.3 = (bf16[8,128,6,128]{3,1,0,2:T(8,128)(2,1)}, bf16[8,128,6,128]{3,1,0,2:T(8,128)(2,1)S(1)}, u32[]{:S(2)}) copy-start(bf16[8,128,6,128]{3,1,0,2:T(8,128)(2,1)S(1)} %copy.236) | copy-start | bytes 4718596
  47.4 1.4 copy-start.9
  49.7 1.3 copy-start.6
  76.6 10.5 %collective-permute-start = (bf16[4,128,2048]{2,1,0:T(8,128)(2,1)}, bf16[4,128,2048]{2,1,0:T(8,128)(2,1)S(1)}, u32[]{:S(2)}, u32[]{:S(2)}) collective-permute-start(bf16[4,128,2048]{2,1,0:T(8,128)(2,1)} %all-gather.2.cloned.1.call-done), channel_id=1, source_target_pairs={{0,32},{32,0},{1,33},{33,1},{2,34},{34,2},{3,35},{35,3},{4,36},{36... | collective-permute-start | bytes 6291464 | tf_op jit(solution)/shard_map/ppermute | solution.py:108
  78.8 1.6 copy-start.10
  78.8 1.6 copy-start.28
  80.4 1.8 copy-start.7
  80.5 1.8 copy-start.25
  82.3 3.6 %copy-start.18 = (bf16[256,1,4,128]{0,3,2,1:T(8,128)(2,1)}, bf16[256,1,4,128]{0,3,2,1:T(8,128)(2,1)S(1)}, u32[]{:S(2)}) copy-start(bf16[256,1,4,128]{0,3,2,1:T(8,128)(2,1)S(1)} %fusion.37) | copy-start | bytes 786436
  82.3 1.8 copy-start.12
  82.3 1.8 copy-start.31
  84.1 1.8 copy-start.20
  85.9 1.1 copy-start.23
  85.9 2.1 copy-start.14
  107.7 2.2 %copy-start.2 = (bf16[4,2,128,2048]{3,2,1,0:T(8,128)(2,1)S(1)}, bf16[4,2,128,2048]{3,2,1,0:T(8,128)(2,1)}, u32[]{:S(2)}) copy-start(bf16[4,2,128,2048]{3,2,1,0:T(8,128)(2,1)} %maximum_select_fusion) | copy-start | bytes 12582916
  126.8 30.5 %all-to-all-start.2 = ((bf16[4,128,2048]{2,1,0:T(8,128)(2,1)}), bf16[4,128,2048]{2,1,0:T(8,128)(2,1)S(1)}, u32[]{:S(2)}, u32[]{:S(2)}) async-start(bf16[4,128,2048]{2,1,0:T(8,128)(2,1)} %reduce_sum.128), calls=%async_computation.2 | async-start | bytes 4194304 | tf_op jit(solution)/shard_map/all_to_all | solution.py:127
  133.1 2.8 %copy-start.4 = (bf16[8,128,6,128]{3,1,0,2:T(8,128)(2,1)S(1)}, bf16[8,128,6,128]{3,1,0,2:T(8,128)(2,1)}, u32[]{:S(2)}) copy-start(bf16[8,128,6,128]{3,1,0,2:T(8,128)(2,1)} %copy-done.3) | copy-start | bytes 4718596
  133.1 2.8 %copy-start.15 = (bf16[1024,512]{0,1:T(8,128)(2,1)S(1)}, bf16[1024,512]{0,1:T(8,128)(2,1)}, u32[]{:S(2)}) copy-start(bf16[1024,512]{0,1:T(8,128)(2,1)} %convolution_convert_fusion.1) | copy-start | bytes 3145732
  137.3 2.5 %copy-start.13 = (f32[512,256,4]{1,0,2:T(8,128)S(1)}, f32[512,256,4]{1,0,2:T(8,128)}, u32[]{:S(2)}) copy-start(f32[512,256,4]{1,0,2:T(8,128)} %get-tuple-element.51) | copy-start | bytes 6291460
  137.3 2.5 %copy-start.32 = (pred[256,512]{0,1:T(8,128)(4,1)S(1)}, pred[256,512]{0,1:T(8,128)(4,1)}, u32[]{:S(2)}) copy-start(pred[256,512]{0,1:T(8,128)(4,1)} %copy-done.30) | copy-start | bytes 393220
  140.6 0.7 copy-start.34
  142.3 17.6 %copy-start.16 = (bf16[1024,512]{0,1:T(8,128)(2,1)S(1)}, bf16[1024,512]{0,1:T(8,128)(2,1)}, u32[]{:S(2)}) copy-start(bf16[1024,512]{0,1:T(8,128)(2,1)} %convolution_convert_fusion.1) | copy-start | bytes 3145732
  142.3 17.8 %copy-start.29 = (pred[256,512]{0,1:T(8,128)(4,1)S(1)}, pred[256,512]{0,1:T(8,128)(4,1)}, u32[]{:S(2)}) copy-start(pred[256,512]{0,1:T(8,128)(4,1)} %copy-done.27) | copy-start | bytes 393220
  157.3 2.6 %copy-start.19 = (bf16[256,1,4,128]{0,3,2,1:T(8,128)(2,1)S(1)}, bf16[256,1,4,128]{0,3,2,1:T(8,128)(2,1)}, u32[]{:S(2)}) copy-start(bf16[256,1,4,128]{0,3,2,1:T(8,128)(2,1)} %copy-done.18) | copy-start | bytes 786436
  157.3 2.6 %copy-start.21 = (bf16[256,1,4,128]{0,3,2,1:T(8,128)(2,1)S(1)}, bf16[256,1,4,128]{0,3,2,1:T(8,128)(2,1)}, u32[]{:S(2)}) copy-start(bf16[256,1,4,128]{0,3,2,1:T(8,128)(2,1)} %copy-done.20) | copy-start | bytes 786436
  157.3 2.8 %copy-start.5 = (bf16[8,128,6,128]{3,1,0,2:T(8,128)(2,1)S(1)}, bf16[8,128,6,128]{3,1,0,2:T(8,128)(2,1)}, u32[]{:S(2)}) copy-start(bf16[8,128,6,128]{3,1,0,2:T(8,128)(2,1)} %copy-done.3) | copy-start | bytes 4718596
  157.3 3.0 %copy-start.11 = (f32[512,256,4]{1,0,2:T(8,128)S(1)}, f32[512,256,4]{1,0,2:T(8,128)}, u32[]{:S(2)}) copy-start(f32[512,256,4]{1,0,2:T(8,128)} %copy-done.9) | copy-start | bytes 6291460
  161.2 1.6 copy-start.8
  161.2 1.6 copy-start.26
  162.8 1.2 copy-start.17
  162.8 1.2 copy-start.22
  164.6 1.0 copy-start.35
  164.6 1.0 copy-start.36
  165.6 0.8 copy-start.33
  167.9 25.9 %all-to-all-start.3 = ((bf16[8,128,6,128]{1,3,2,0:T(8,128)(2,1)}), bf16[8,128,6,128]{1,3,2,0:T(8,128)(2,1)}, u32[]{:S(2)}, u32[]{:S(2)}) async-start(bf16[8,128,6,128]{1,3,2,0:T(8,128)(2,1)} %pad_maximum_fusion), calls=%async_computation.3 | async-start | bytes 3145728 | tf_op jit(solution)/shard_map/all_to_all | solution.py:172
  173.5 29.4 %reduce-scatter.5.cloned.1.call-start = ((), (), s32[]{:S(2)}) async-start(), calls=%async_computation.8 | async-start | bytes 655360 | tf_op jit(solution)/shard_map/reduce_scatter | solution.py:186
  195.0 7.8 %copy-start.1 = (bf16[512,2048]{1,0:T(8,128)(2,1)S(1)}, bf16[512,2048]{1,0:T(8,128)(2,1)}, u32[]{:S(2)}) copy-start(bf16[512,2048]{1,0:T(8,128)(2,1)} %param.10) | copy-start | bytes 6291460
Sparse Core Ops, SparseCore 0:
  43.9 32.6 all-gather.1
  104.2 56.4 reduce-scatter.2
  177.4 25.4 reduce-scatter.4

commit v10 on v6

--- a/solution.py
+++ b/solution.py
@@ -120,7 +120,7 @@
     dk_blocks = [None] * blk_count
     dv_blocks = [None] * blk_count
     for i in range(blk_count):
-        if i == blk_count // 2:
+        if i == blk_count - 1:
             pieces, attention_grad = lax.optimization_barrier((pieces, attention_grad))
         q_start, k_start, k_end = band(i)
         q_blk = query_head_rows[q_start : q_start + blk]

time: 191 us -> 190 us (level)
  matrix products: 31.2 us -> 36.1 us
  waiting for transfers between devices: 72.8 us -> 68.5 us
    all_to_all x1, waiting for transfers between devices: 15 us -> 10.7 us  [local(): lax.all_to_all(pieces, 'x', split_axis=0, concat_axis=0, tiled=True)]
    unnamed x77 -> x79, local copies, waits for them, and re-layouts: 13.1 us -> 11.9 us
  transfers between devices with their start and end apart: 6 -> 6, of which waited for: 4 -> 4; matrix products, arithmetic and copies ran while one was open for 30% -> 33% of each run, Pallas kernels for 0% -> 0%
where the time goes in v10:
time: 190 us; the launch traced here: 189 us
  waiting for transfers between devices  68.5 us (36%)
  matrix products  36.1 us (19%)
  local copies, waits for them, and re-layouts  28.2 us (15%)
  starting transfers between devices  17.6 us (9%)
  other arithmetic  16.3 us (9%)
  between operations  14.4 us (8%)
  blocking collectives  8.13 us (4%)
    all_to_all x1, waiting for transfers between devices, local(): got = lax.all_to_all(packed, SEQ, split_axis=0, concat_axis=0, tiled=True)  34.4 us
    all_to_all x1, waiting for transfers between devices, local(): lax.all_to_all(packed_out, SEQ, split_axis=0, concat_axis=0, tiled=True)  18.2 us
    unnamed x79, local copies, waits for them, and re-layouts  11.9 us
    all_to_all x1, waiting for transfers between devices, local(): lax.all_to_all(pieces, 'x', split_axis=0, concat_axis=0, tiled=True)  10.7 us
    all_to_all x1, blocking collectives, local(): lax.all_to_all(pieces, 'core', split_axis=0, concat_axis=0, tiled=True)  8.13 us
    all_to_all x1, starting transfers between devices, local(): got = lax.all_to_all(packed, SEQ, split_axis=0, concat_axis=0, tiled=True)  6.55 us
    dot_general x1, local copies, waits for them, and re-layouts, local(): lax.dot_general(a_head, incoming, (((0,), (0,)), ((), ())), preferred_ele...  6.39 us
    dot_general x4, matrix products, local(): jnp.einsum('kgqs,qkgd->skd', attn_prob.astype(jnp.bfloat16), g_blk, prefe...  5.79 us
  transfers between devices with their start and end apart: 6, of which 4 were waited for; matrix products, arithmetic and copies ran while one was open for 33% of the time, Pallas kernels for 0%

profile of v10, /device:TPU:2, one launch (start us, length us, event | category | flops | bytes accessed | tf_op | source)
XLA Modules:
  0.0 189.2 jit_solution(9799127696638732278)
XLA Ops:
  7.9 1.1 copy.190
  9.0 1.8 copy.191
  10.8 1.6 copy.189
  12.5 2.3 %maximum_bitcast_fusion = bf16[8,128,6,128]{1,3,2,0:T(8,128)(2,1)} fusion(bf16[128,8,1,128]{0,3,2,1:T(8,128)(2,1)} %bitcast.438, bf16[128,8,1,128]{0,3,2,1:T(8,128)(2,1)S(1)} %bitcast.437, bf16[128,8,4,128]{0,3,2,1:T(8,128)(2,1)S(1)} %bitcast.430), kind=kLoop, calls=%fused_computation.38 | loop fusion | flops 1572864 | bytes 3145728 | tf_op jit(solution)/shard_map/transpose | solution.py:49
  14.7 2.6 %copy.194 = bf16[8,128,6,128]{3,1,2,0:T(8,128)(2,1)} copy(bf16[8,128,6,128]{1,3,2,0:T(8,128)(2,1)} %maximum_bitcast_fusion) | data formatting | bytes 3145728 | tf_op jit(solution)/shard_map/transpose | solution.py:49
  17.3 6.5 %all-to-all-start = ((bf16[8,128,6,128]{3,1,2,0:T(8,128)(2,1)}), bf16[8,128,6,128]{3,1,2,0:T(8,128)(2,1)}, u32[]{:S(2)}, u32[]{:S(2)}) async-start(bf16[8,128,6,128]{3,1,2,0:T(8,128)(2,1)} %copy.194), calls=%async_computation | async-start | bytes 3145728 | tf_op jit(solution)/shard_map/all_to_all | solution.py:50
  24.7 0.9 fusion.63
  25.7 34.4 %all-to-all-done = bf16[8,128,6,128]{3,1,2,0:T(8,128)(2,1)} async-done(((bf16[8,128,6,128]{3,1,2,0:T(8,128)(2,1)}), bf16[8,128,6,128]{3,1,2,0:T(8,128)(2,1)}, u32[]{:S(2)}, u32[]{:S(2)}) %all-to-all-start) | async-done | bytes 1572896 | tf_op jit(solution)/shard_map/all_to_all | solution.py:50
  60.0 1.5 copy.195
  66.1 0.7 fusion.42
  67.0 0.7 fusion.41
  67.8 0.7 fusion.40
  69.3 1.1 pad_maximum_fusion.1
  70.4 6.4 %copy.233 = bf16[2048,1024]{1,0:T(8,128)(2,1)} copy(bf16[2048,1024]{0,1:T(8,128)(2,1)} %bitcast.431) | data formatting | bytes 8388608 | tf_op jit(solution)/shard_map/dot_general | solution.py:107
  76.8 4.9 %convolution_bitcast_fusion = f32[512,8,4,64]{0,3,1,2:T(8,128)S(1)} fusion(bf16[1024,512,1,1]{0,1,3,2:T(8,128)(2,1)} %bitcast.449, bf16[4,8,64,1024]{3,2,1,0:T(8,128)(2,1)} %bitcast.433), kind=kOutput, calls=%fused_computation.4 | convolution fusion | flops 2147483648 | bytes 9437184 | tf_op jit(solution)/shard_map/dot_general | solution.py:107
  81.7 2.5 %copy.235 = f32[512,8,4,64]{0,3,2,1:T(8,128)} copy(f32[512,8,4,64]{0,3,1,2:T(8,128)S(1)} %convolution_bitcast_fusion) | data formatting | bytes 8388608 | tf_op jit(solution)/shard_map/transpose | solution.py:172
  84.2 3.6 %convolution_convert_fusion = bf16[1024,2048]{1,0:T(8,128)(2,1)S(1)} fusion(bf16[1024,512]{0,1:T(8,128)(2,1)} %bitcast.450, bf16[512,2048]{1,0:T(8,128)(2,1)S(1)} %copy-done), kind=kOutput, calls=%fused_computation.3 | convolution fusion | flops 2149580800 | bytes 7340032 | tf_op jit(solution)/shard_map/dot_general | solution.py:100
  88.4 1.6 copy-done.4
  90.0 3.4 %fusion.26 = bf16[1024,512]{0,1:T(8,128)(2,1)} fusion(bf16[512,2048]{1,0:T(8,128)(2,1)S(1)} %copy-done, bf16[1,1024,2048]{2,1,0:T(8,128)(2,1)S(1)} %copy-done.4), kind=kOutput, calls=%fused_computation.40 | convolution fusion | flops 2148007936 | bytes 7340032 | tf_op jit(solution)/shard_map/dot_general | solution.py:110
  93.4 8.1 %all_to_all.20 = bf16[2,4,128,2048]{3,2,1,0:T(8,128)(2,1)} all-to-all(bf16[2,4,128,2048]{3,2,1,0:T(8,128)(2,1)S(1)} %bitcast.409), channel_id=1, replica_groups=mesh['x'=4,'core'=2,'dpy'=4,'dpz'=8] {'core'}, dimensions={0} | all-to-all | bytes 8388608 | tf_op jit(solution)/shard_map/all_to_all | solution.py:115
  101.5 5.1 %reduce_sum.128 = bf16[4,128,2048]{2,1,0:T(8,128)(2,1)} reduce(bf16[2,4,128,2048]{3,2,1,0:T(8,128)(2,1)} %all_to_all.20, bf16[]{:T(256)} %constant.24.clone.1), dimensions={0}, to_apply=%region_11.12 | reduce | flops 1048576 | bytes 6291458 | tf_op jit(solution)/shard_map/reduce_sum | solution.py:116
  106.7 5.3 %all-to-all-start.2 = ((bf16[4,128,2048]{2,1,0:T(8,128)(2,1)}), bf16[4,128,2048]{2,1,0:T(8,128)(2,1)S(1)}, u32[]{:S(2)}, u32[]{:S(2)}) async-start(bf16[4,128,2048]{2,1,0:T(8,128)(2,1)} %reduce_sum.128), calls=%async_computation.2 | async-start | bytes 4194304 | tf_op jit(solution)/shard_map/all_to_all | solution.py:117
  112.0 1.5 multiply_reduce_fusion.3
  113.5 2.7 %fusion.29 = bf16[4,256,512]{1,2,0:T(8,128)(2,1)S(1)} fusion(f32[4,256]{1,0:T(4,128)S(1)} %bitcast.456, f32[4,256]{1,0:T(4,128)S(1)} %fusion.21, f32[4,256]{1,0:T(4,128)S(1)} %get-tuple-element.45, f32[512,256,4]{1,0,2:T(8,128)} %copy-done.9, pred[256,512]{0,1:T(8,128)(4,1)} %get-tuple-element.49, bf16[1024,1,4,128]{0,3,2,1:T(8,128)(2,1)} %bitcast.440, ...), kind=kOutput, calls=%fused_computation.41 | convolution fusion | flops 138412032 | bytes 3682304 | tf_op jit(solution)/shard_map/qkgd,skd->kgqs/dot_general | solution.py:134
  116.3 1.0 fusion.43
  118.2 0.9 fusion.48
  119.4 0.8 fusion.30
  120.2 1.0 fusion.44
  121.3 1.0 fusion.39
  122.3 1.2 convolution_bitcast_fusion.6
  123.5 0.8 convolution_bitcast_fusion.4
  124.3 1.0 fusion.49
  125.3 1.5 convolution_bitcast_fusion.3
  126.8 10.7 %all-to-all-done.2 = bf16[4,128,2048]{2,1,0:T(8,128)(2,1)S(1)} async-done(((bf16[4,128,2048]{2,1,0:T(8,128)(2,1)}), bf16[4,128,2048]{2,1,0:T(8,128)(2,1)S(1)}, u32[]{:S(2)}, u32[]{:S(2)}) %all-to-all-start.2) | async-done | bytes 2097184 | tf_op jit(solution)/shard_map/all_to_all | solution.py:117
  137.5 2.5 %convolution_bitcast_fusion.2 = f32[512,1,128]{0,2,1:T(8,128)S(1)} fusion(bf16[1024,1,4,128]{0,3,2,1:T(8,128)(2,1)S(1)} %bitcast.446, f32[4,256]{1,0:T(4,128)S(1)} %fusion.25, f32[4,256]{1,0:T(4,128)S(1)} %get-tuple-element.41, f32[512,256,4]{1,0,2:T(8,128)} %copy-done.5, pred[256,512]{0,1:T(8,128)(4,1)S(1)} %copy-done.23), kind=kOutput, calls=%fused_computation.68 | convolution fusion | flops 136839168 | bytes 2760704 | tf_op jit(solution)/shard_map/kgqs,qkgd->skd/dot_general | solution.py:144
  140.1 1.7 fusion.31
  141.9 1.5 convolution_bitcast_fusion.5
  143.4 1.2 fusion.45
  146.2 1.4 pad_maximum_fusion
  147.6 5.6 %all-to-all-start.3 = ((bf16[8,128,6,128]{1,3,2,0:T(8,128)(2,1)}), bf16[8,128,6,128]{1,3,2,0:T(8,128)(2,1)}, u32[]{:S(2)}, u32[]{:S(2)}) async-start(bf16[8,128,6,128]{1,3,2,0:T(8,128)(2,1)} %pad_maximum_fusion), calls=%async_computation.3 | async-start | bytes 3145728 | tf_op jit(solution)/shard_map/all_to_all | solution.py:162
  154.0 1.3 reduce_sum.129
  155.3 18.2 %all-to-all-done.3 = bf16[8,128,6,128]{1,3,2,0:T(8,128)(2,1)} async-done(((bf16[8,128,6,128]{1,3,2,0:T(8,128)(2,1)}), bf16[8,128,6,128]{1,3,2,0:T(8,128)(2,1)}, u32[]{:S(2)}, u32[]{:S(2)}) %all-to-all-start.3) | async-done | bytes 1572896 | tf_op jit(solution)/shard_map/all_to_all | solution.py:162
  173.5 1.3 slice.205
  174.8 1.3 copy.236
  176.1 1.1 fusion.106
  177.2 0.9 copy.238
  178.0 0.8 copy.237
  178.9 3.9 %reduce-scatter.5.cloned.1.call-done = f32[512,64]{0,1:T(8,128)} async-done(((f32[512,256]{0,1:T(8,128)}), f32[512,64]{0,1:T(8,128)}) %reduce-scatter.5.cloned.1.call-update) | async-done | bytes 131088 | tf_op jit(solution)/shard_map/reduce_scatter | solution.py:176
  (114 shorter events, 10.9 us)
Async XLA Ops:
  7.2 77.1 %copy-start = (bf16[512,2048]{1,0:T(8,128)(2,1)S(1)}, bf16[512,2048]{1,0:T(8,128)(2,1)}, u32[]{:S(2)}) copy-start(bf16[512,2048]{1,0:T(8,128)(2,1)} %param.10) | copy-start | bytes 6291460
  7.2 63.2 %all-gather.3.cloned.1.call-start = ((), (), s32[]{:S(2)}) async-start(), calls=%async_computation.8 | async-start | bytes 4718592 | tf_op jit(solution)/shard_map/all_gather | solution.py:106
  17.3 6.6 %copy-start.34 = (s32[1,16]{1,0:T(1,128)S(1)}, s32[1,16]{1,0:T(1,128)}, u32[]{:S(2)}) copy-start(s32[1,16]{1,0:T(1,128)} %param.12) | copy-start | bytes 196
  17.3 6.6 %copy-start.35 = (s32[1,16]{1,0:T(1,128)S(1)}, s32[1,16]{1,0:T(1,128)}, u32[]{:S(2)}) copy-start(s32[1,16]{1,0:T(1,128)} %param.13) | copy-start | bytes 196
  17.3 42.7 %all-to-all-start = ((bf16[8,128,6,128]{3,1,2,0:T(8,128)(2,1)}), bf16[8,128,6,128]{3,1,2,0:T(8,128)(2,1)}, u32[]{:S(2)}, u32[]{:S(2)}) async-start(bf16[8,128,6,128]{3,1,2,0:T(8,128)(2,1)} %copy.194), calls=%async_computation | async-start | bytes 3145728 | tf_op jit(solution)/shard_map/all_to_all | solution.py:50
  23.9 129.3 %reduce-scatter.3.cloned.1.call-start = ((), (), s32[]{:S(2)}) async-start(), calls=%async_computation.6 | async-start | bytes 4718592 | tf_op jit(solution)/shard_map/reduce_scatter | solution.py:175
  24.7 38.9 %copy-start.24 = (pred[256,512]{0,1:T(8,128)(4,1)}, pred[256,512]{0,1:T(8,128)(4,1)S(1)}, u32[]{:S(2)}) copy-start(pred[256,512]{0,1:T(8,128)(4,1)S(1)} %compare_and_fusion.1) | copy-start | bytes 393220
  25.7 36.9 %copy-start.21 = (pred[256,512]{0,1:T(8,128)(4,1)}, pred[256,512]{0,1:T(8,128)(4,1)S(1)}, u32[]{:S(2)}) copy-start(pred[256,512]{0,1:T(8,128)(4,1)S(1)} %get-tuple-element.50) | copy-start | bytes 393220
  61.5 6.2 %copy-start.2 = (bf16[8,128,6,128]{3,1,0,2:T(8,128)(2,1)}, bf16[8,128,6,128]{3,1,0,2:T(8,128)(2,1)S(1)}, u32[]{:S(2)}) copy-start(bf16[8,128,6,128]{3,1,0,2:T(8,128)(2,1)S(1)} %copy.195) | copy-start | bytes 4718596
  62.6 2.9 %copy-start.5 = (f32[512,256,4]{1,0,2:T(8,128)}, f32[512,256,4]{1,0,2:T(8,128)S(1)}, u32[]{:S(2)}) copy-start(f32[512,256,4]{1,0,2:T(8,128)S(1)} %get-tuple-element.42) | copy-start | bytes 6291460
  63.1 1.1 copy-start.27
  63.6 3.3 %copy-start.7 = (f32[512,256,4]{1,0,2:T(8,128)}, f32[512,256,4]{1,0,2:T(8,128)S(1)}, u32[]{:S(2)}) copy-start(f32[512,256,4]{1,0,2:T(8,128)S(1)} %get-tuple-element.44) | copy-start | bytes 6291460
  64.6 3.2 %copy-start.9 = (f32[512,256,4]{1,0,2:T(8,128)}, f32[512,256,4]{1,0,2:T(8,128)S(1)}, u32[]{:S(2)}) copy-start(f32[512,256,4]{1,0,2:T(8,128)S(1)} %get-tuple-element.46) | copy-start | bytes 6291460
  65.1 1.0 copy-start.22
  66.1 0.9 copy-start.25
  67.0 1.5 copy-start.14
  67.8 0.8 copy-start.19
  68.6 0.7 copy-start.20
  87.8 2.2 %copy-start.4 = (bf16[1,1024,2048]{2,1,0:T(8,128)(2,1)S(1)}, bf16[1,1024,2048]{2,1,0:T(8,128)(2,1)}, u32[]{:S(2)}) copy-start(bf16[1,1024,2048]{2,1,0:T(8,128)(2,1)} %all-gather.3.cloned.1.call-done) | copy-start | bytes 12582916
  106.7 30.8 %all-to-all-start.2 = ((bf16[4,128,2048]{2,1,0:T(8,128)(2,1)}), bf16[4,128,2048]{2,1,0:T(8,128)(2,1)S(1)}, u32[]{:S(2)}, u32[]{:S(2)}) async-start(bf16[4,128,2048]{2,1,0:T(8,128)(2,1)} %reduce_sum.128), calls=%async_computation.2 | async-start | bytes 4194304 | tf_op jit(solution)/shard_map/all_to_all | solution.py:117
  113.5 2.7 %copy-start.3 = (bf16[8,128,6,128]{3,1,0,2:T(8,128)(2,1)S(1)}, bf16[8,128,6,128]{3,1,0,2:T(8,128)(2,1)}, u32[]{:S(2)}) copy-start(bf16[8,128,6,128]{3,1,0,2:T(8,128)(2,1)} %copy-done.2) | copy-start | bytes 4718596
  116.2 1.5 copy-start.11
  117.8 1.6 copy-start.8
  117.8 1.6 copy-start.26
  120.2 3.2 %copy-start.10 = (f32[512,256,4]{1,0,2:T(8,128)S(1)}, f32[512,256,4]{1,0,2:T(8,128)}, u32[]{:S(2)}) copy-start(f32[512,256,4]{1,0,2:T(8,128)} %copy-done.9) | copy-start | bytes 6291460
  120.2 3.2 %copy-start.28 = (pred[256,512]{0,1:T(8,128)(4,1)S(1)}, pred[256,512]{0,1:T(8,128)(4,1)}, u32[]{:S(2)}) copy-start(pred[256,512]{0,1:T(8,128)(4,1)} %get-tuple-element.49) | copy-start | bytes 393220
  124.3 1.1 copy-start.31
  125.3 12.2 %copy-start.12 = (bf16[1024,512]{0,1:T(8,128)(2,1)S(1)}, bf16[1024,512]{0,1:T(8,128)(2,1)}, u32[]{:S(2)}) copy-start(bf16[1024,512]{0,1:T(8,128)(2,1)} %fusion.26) | copy-start | bytes 3145732
  125.3 12.2 %copy-start.23 = (pred[256,512]{0,1:T(8,128)(4,1)S(1)}, pred[256,512]{0,1:T(8,128)(4,1)}, u32[]{:S(2)}) copy-start(pred[256,512]{0,1:T(8,128)(4,1)} %copy-done.21) | copy-start | bytes 393220
  137.5 2.5 %copy-start.15 = (bf16[256,1,4,128]{0,3,2,1:T(8,128)(2,1)S(1)}, bf16[256,1,4,128]{0,3,2,1:T(8,128)(2,1)}, u32[]{:S(2)}) copy-start(bf16[256,1,4,128]{0,3,2,1:T(8,128)(2,1)} %copy-done.14) | copy-start | bytes 786436
  137.5 2.6 %copy-start.6 = (f32[512,256,4]{1,0,2:T(8,128)S(1)}, f32[512,256,4]{1,0,2:T(8,128)}, u32[]{:S(2)}) copy-start(f32[512,256,4]{1,0,2:T(8,128)} %copy-done.5) | copy-start | bytes 6291460
  141.8 2.8 %copy-start.16 = (bf16[256,1,4,128]{0,3,2,1:T(8,128)(2,1)S(1)}, bf16[256,1,4,128]{0,3,2,1:T(8,128)(2,1)}, u32[]{:S(2)}) copy-start(bf16[256,1,4,128]{0,3,2,1:T(8,128)(2,1)} %fusion.39) | copy-start | bytes 786436
  141.9 2.8 %copy-start.17 = (bf16[256,1,4,128]{0,3,2,1:T(8,128)(2,1)S(1)}, bf16[256,1,4,128]{0,3,2,1:T(8,128)(2,1)}, u32[]{:S(2)}) copy-start(bf16[256,1,4,128]{0,3,2,1:T(8,128)(2,1)} %fusion.43) | copy-start | bytes 786436
  141.9 2.8 %copy-start.18 = (bf16[256,1,4,128]{0,3,2,1:T(8,128)(2,1)S(1)}, bf16[256,1,4,128]{0,3,2,1:T(8,128)(2,1)}, u32[]{:S(2)}) copy-start(bf16[256,1,4,128]{0,3,2,1:T(8,128)(2,1)} %fusion.44) | copy-start | bytes 786436
  144.8 1.0 copy-start.29
  144.8 1.0 copy-start.32
  144.8 1.1 copy-start.33
  145.1 1.0 copy-start.13
  145.1 1.0 copy-start.30
  147.6 25.9 %all-to-all-start.3 = ((bf16[8,128,6,128]{1,3,2,0:T(8,128)(2,1)}), bf16[8,128,6,128]{1,3,2,0:T(8,128)(2,1)}, u32[]{:S(2)}, u32[]{:S(2)}) async-start(bf16[8,128,6,128]{1,3,2,0:T(8,128)(2,1)} %pad_maximum_fusion), calls=%async_computation.3 | async-start | bytes 3145728 | tf_op jit(solution)/shard_map/all_to_all | solution.py:162
  153.2 29.5 %reduce-scatter.5.cloned.1.call-start = ((), (), s32[]{:S(2)}) async-start(), calls=%async_computation.7 | async-start | bytes 655360 | tf_op jit(solution)/shard_map/reduce_scatter | solution.py:176
  174.8 8.0 %copy-start.1 = (bf16[512,2048]{1,0:T(8,128)(2,1)S(1)}, bf16[512,2048]{1,0:T(8,128)(2,1)}, u32[]{:S(2)}) copy-start(bf16[512,2048]{1,0:T(8,128)(2,1)} %param.10) | copy-start | bytes 6291460
Sparse Core Ops, SparseCore 0:
  9.9 51.8 all-gather.2
  84.3 55.7 reduce-scatter.2
  157.1 25.5 reduce-scatter.4

commit v11 on v10

--- a/solution.py
+++ b/solution.py
@@ -112,8 +112,11 @@
     )
     attention_grad = d_rows.astype(jnp.bfloat16).reshape(win_rows, hk, group_width, HEAD_SIZE)
     pieces, attention_grad = lax.optimization_barrier((pieces, attention_grad))
-    pieces = lax.all_to_all(pieces, "core", split_axis=0, concat_axis=0, tiled=True)
-    pieces = jnp.sum(pieces.astype(jnp.float32), axis=0).astype(jnp.bfloat16)
+    core_at = lax.axis_index("core")
+    kept = lax.dynamic_index_in_dim(pieces, core_at, axis=0, keepdims=False)
+    sent = lax.dynamic_index_in_dim(pieces, 1 - core_at, axis=0, keepdims=False)
+    sent = lax.ppermute(sent, "core", perm=[(0, 1), (1, 0)])
+    pieces = (kept.astype(jnp.float32) + sent.astype(jnp.float32)).astype(jnp.bfloat16)
     pieces = lax.all_to_all(pieces, "x", split_axis=0, concat_axis=0, tiled=True)
 
     dq_blocks = []

time: 190 us -> 184 us (0.968)
  blocking collectives: 8.13 us -> 0 us
  other arithmetic: 16.3 us -> 12 us
  matrix products: 36.1 us -> 38.9 us
  waiting for transfers between devices: 68.5 us -> 70.5 us
    all_to_all x1 -> x0, blocking collectives: 8.13 us -> none  [local(): lax.all_to_all(pieces, 'core', split_axis=0, concat_axis=0, tiled=True)]
    reduce_sum x1 -> x0, other arithmetic: 5.14 us -> none  [local(): pieces = jnp.sum(pieces.astype(jnp.float32), axis=0).astype(jnp.bfloat16)]
    dot_general x4, matrix products: 4.28 us -> 6.83 us  [local(): jnp.einsum('kgqs,skd->qkgd', score_gradient, k_band, preferred_element_ty...]
    convert_element_type x0 -> x1, other arithmetic: none -> 2.12 us  [local(): (kept.astype(jnp.float32) + sent.astype(jnp.float32)).astype(jnp.bfloat16)]
    unnamed x79 -> x97, local copies, waits for them, and re-layouts: 11.9 us -> 13.5 us
  transfers between devices with their start and end apart: 6 -> 7, of which waited for: 4 -> 4; matrix products, arithmetic and copies ran while one was open for 33% -> 33% of each run, Pallas kernels for 0% -> 0%
where the time goes in v11:
time: 184 us; the launch traced here: 183 us
  waiting for transfers between devices  70.5 us (38%)
  matrix products  38.9 us (21%)
  local copies, waits for them, and re-layouts  29.4 us (16%)
  starting transfers between devices  17.5 us (10%)
  between operations  14.5 us (8%)
  other arithmetic  12 us (7%)
    all_to_all x1, waiting for transfers between devices, local(): got = lax.all_to_all(packed, SEQ, split_axis=0, concat_axis=0, tiled=True)  34.4 us
    all_to_all x1, waiting for transfers between devices, local(): lax.all_to_all(packed_out, SEQ, split_axis=0, concat_axis=0, tiled=True)  18.2 us
    unnamed x97, local copies, waits for them, and re-layouts  13.5 us
    all_to_all x1, waiting for transfers between devices, local(): lax.all_to_all(pieces, 'x', split_axis=0, concat_axis=0, tiled=True)  12.3 us
    dot_general x4, matrix products, local(): jnp.einsum('kgqs,skd->qkgd', score_gradient, k_band, preferred_element_ty...  6.83 us
    dot_general x4, matrix products, local(): jnp.einsum('kgqs,qkgd->skd', attn_prob.astype(jnp.bfloat16), g_blk, prefe...  6.8 us
    all_to_all x1, starting transfers between devices, local(): got = lax.all_to_all(packed, SEQ, split_axis=0, concat_axis=0, tiled=True)  6.55 us
    dot_general x1, local copies, waits for them, and re-layouts, local(): lax.dot_general(a_head, incoming, (((0,), (0,)), ((), ())), preferred_ele...  6.39 us
  transfers between devices with their start and end apart: 7, of which 4 were waited for; matrix products, arithmetic and copies ran while one was open for 33% of the time, Pallas kernels for 0%

profile of v11, /device:TPU:2, one launch (start us, length us, event | category | flops | bytes accessed | tf_op | source)
XLA Modules:
  0.0 182.7 jit_solution(16371696627328154023)
XLA Ops:
  7.9 1.1 copy.188
  9.0 1.8 copy.189
  10.8 1.6 copy.187
  12.5 2.3 %maximum_bitcast_fusion = bf16[8,128,6,128]{1,3,2,0:T(8,128)(2,1)} fusion(bf16[128,8,1,128]{0,3,2,1:T(8,128)(2,1)} %bitcast.442, bf16[128,8,1,128]{0,3,2,1:T(8,128)(2,1)S(1)} %bitcast.441, bf16[128,8,4,128]{0,3,2,1:T(8,128)(2,1)S(1)} %bitcast.435), kind=kLoop, calls=%fused_computation.40 | loop fusion | flops 1572864 | bytes 3145728 | tf_op jit(solution)/shard_map/transpose | solution.py:49
  14.7 2.6 %copy.192 = bf16[8,128,6,128]{3,1,2,0:T(8,128)(2,1)} copy(bf16[8,128,6,128]{1,3,2,0:T(8,128)(2,1)} %maximum_bitcast_fusion) | data formatting | bytes 3145728 | tf_op jit(solution)/shard_map/transpose | solution.py:49
  17.4 6.6 %all-to-all-start = ((bf16[8,128,6,128]{3,1,2,0:T(8,128)(2,1)}), bf16[8,128,6,128]{3,1,2,0:T(8,128)(2,1)}, u32[]{:S(2)}, u32[]{:S(2)}) async-start(bf16[8,128,6,128]{3,1,2,0:T(8,128)(2,1)} %copy.192), calls=%async_computation | async-start | bytes 3145728 | tf_op jit(solution)/shard_map/all_to_all | solution.py:50
  24.7 0.9 fusion.64
  25.7 34.4 %all-to-all-done = bf16[8,128,6,128]{3,1,2,0:T(8,128)(2,1)} async-done(((bf16[8,128,6,128]{3,1,2,0:T(8,128)(2,1)}), bf16[8,128,6,128]{3,1,2,0:T(8,128)(2,1)}, u32[]{:S(2)}, u32[]{:S(2)}) %all-to-all-start) | async-done | bytes 1572896 | tf_op jit(solution)/shard_map/all_to_all | solution.py:50
  60.1 1.5 copy.193
  66.2 0.7 fusion.43
  67.1 0.7 fusion.42
  67.9 0.7 fusion.41
  68.7 0.7 copy-done.26
  69.4 1.1 pad_maximum_fusion.1
  70.5 6.4 %copy.230 = bf16[2048,1024]{1,0:T(8,128)(2,1)} copy(bf16[2048,1024]{0,1:T(8,128)(2,1)} %bitcast.436) | data formatting | bytes 8388608 | tf_op jit(solution)/shard_map/dot_general | solution.py:107
  76.9 4.9 %convolution_bitcast_fusion = f32[512,8,4,64]{0,3,1,2:T(8,128)S(1)} fusion(bf16[1024,512,1,1]{0,1,3,2:T(8,128)(2,1)} %bitcast.453, bf16[4,8,64,1024]{3,2,1,0:T(8,128)(2,1)} %bitcast.437), kind=kOutput, calls=%fused_computation.5 | convolution fusion | flops 2147483648 | bytes 9437184 | tf_op jit(solution)/shard_map/dot_general | solution.py:107
  81.8 2.5 %copy.232 = f32[512,8,4,64]{0,3,2,1:T(8,128)} copy(f32[512,8,4,64]{0,3,1,2:T(8,128)S(1)} %convolution_bitcast_fusion) | data formatting | bytes 8388608 | tf_op jit(solution)/shard_map/transpose | solution.py:175
  84.3 3.8 %convolution_convert_fusion = bf16[1024,2048]{1,0:T(8,128)(2,1)S(1)} fusion(bf16[1024,512]{0,1:T(8,128)(2,1)} %bitcast.454, bf16[512,2048]{1,0:T(8,128)(2,1)S(1)} %copy-done), kind=kOutput, calls=%fused_computation.4 | convolution fusion | flops 2149580800 | bytes 7340032 | tf_op jit(solution)/shard_map/dot_general | solution.py:100
  88.1 2.4 %fusion.27 = bf16[1024,512]{0,1:T(8,128)(2,1)S(1)} fusion(bf16[512,2048]{1,0:T(8,128)(2,1)S(1)} %copy-done, bf16[1,1024,2048]{2,1,0:T(8,128)(2,1)S(1)} %copy-done.4), kind=kOutput, calls=%fused_computation.42 | convolution fusion | flops 2148007936 | bytes 7340032 | tf_op jit(solution)/shard_map/dot_general | solution.py:110
  90.8 0.8 copy-done.25
  93.1 0.8 fusion.30
  93.9 1.0 fusion.44
  95.9 0.9 fusion.49
  97.5 1.8 %fusion.31 = bf16[4,256,512]{1,2,0:T(8,128)(2,1)} fusion(f32[4,256]{1,0:T(4,128)S(1)} %bitcast.458, f32[4,256]{1,0:T(4,128)S(1)} %fusion.24, f32[4,256]{1,0:T(4,128)S(1)} %get-tuple-element.43, f32[512,256,4]{1,0,2:T(8,128)S(1)} %copy-done.9, pred[256,512]{0,1:T(8,128)(4,1)S(1)} %copy-done.33, bf16[1024,1,4,128]{0,3,2,1:T(8,128)(2,1)S(1)} %bitcast.446, ...), kind=kOutput, calls=%fused_computation.44 | convolution fusion | flops 138412032 | bytes 3682304 | tf_op jit(solution)/shard_map/qkgd,skd->kgqs/dot_general | solution.py:137
  99.3 2.1 %fusion = bf16[4,128,2048]{2,1,0:T(8,128)(2,1)} fusion(bf16[4,128,2048]{2,1,0:T(8,128)(2,1)S(1)} %collective-permute-done, bf16[2,4,128,2048]{3,2,0,1:T(8,128)(2,1)S(1)} %bitcast.434, s32[]{:T(128)S(6)} %select_n.55), kind=kLoop, calls=%fused_computation.1 | loop fusion | flops 4194304 | bytes 6291460 | tf_op jit(solution)/shard_map/convert_element_type | solution.py:119
  101.5 5.1 %all-to-all-start.1 = ((bf16[4,128,2048]{2,1,0:T(8,128)(2,1)}), bf16[4,128,2048]{2,1,0:T(8,128)(2,1)S(1)}, u32[]{:S(2)}, u32[]{:S(2)}) async-start(bf16[4,128,2048]{2,1,0:T(8,128)(2,1)} %fusion), calls=%async_computation.1 | async-start | bytes 4194304 | tf_op jit(solution)/shard_map/all_to_all | solution.py:120
  106.6 2.5 %fusion.45 = bf16[256,1,4,128]{0,3,2,1:T(8,128)(2,1)} fusion(bf16[4,256,512]{1,2,0:T(8,128)(2,1)} %fusion.31, bf16[1024,6,128]{2,0,1:T(8,128)(2,1)} %bitcast.421), kind=kOutput, calls=%fused_computation.68 | convolution fusion | flops 134348800 | bytes 1441792 | tf_op jit(solution)/shard_map/kgqs,skd->qkgd/dot_general | solution.py:140
  109.1 2.1 %fusion.40 = bf16[256,1,4,128]{0,3,2,1:T(8,128)(2,1)} fusion(bf16[4,256,256]{1,2,0:T(8,128)(2,1)} %copy-done.14, bf16[1024,6,128]{2,0,1:T(8,128)(2,1)} %bitcast.422), kind=kOutput, calls=%fused_computation.63 | convolution fusion | flops 67239936 | bytes 851968 | tf_op jit(solution)/shard_map/kgqs,skd->qkgd/dot_general | solution.py:140
  111.1 2.1 %convolution_bitcast_fusion.6 = f32[512,1,128]{0,2,1:T(8,128)} fusion(bf16[4,256,512]{1,2,0:T(8,128)(2,1)S(1)} %copy-done.5, bf16[1024,6,128]{2,0,1:T(8,128)(2,1)} %bitcast.423), kind=kOutput, calls=%fused_computation.74 | convolution fusion | flops 134217728 | bytes 1572864 | tf_op jit(solution)/shard_map/kgqs,qkgd->skd/dot_general | solution.py:144
  113.3 1.8 convolution_bitcast_fusion.4
  115.1 1.0 fusion.50
  116.8 1.5 convolution_bitcast_fusion.3
  118.3 12.3 %all-to-all-done.1 = bf16[4,128,2048]{2,1,0:T(8,128)(2,1)S(1)} async-done(((bf16[4,128,2048]{2,1,0:T(8,128)(2,1)}), bf16[4,128,2048]{2,1,0:T(8,128)(2,1)S(1)}, u32[]{:S(2)}, u32[]{:S(2)}) %all-to-all-start.1) | async-done | bytes 2097184 | tf_op jit(solution)/shard_map/all_to_all | solution.py:120
  130.6 2.5 %convolution_bitcast_fusion.2 = f32[512,1,128]{0,2,1:T(8,128)S(1)} fusion(bf16[1024,1,4,128]{0,3,2,1:T(8,128)(2,1)S(1)} %bitcast.450, f32[4,256]{1,0:T(4,128)S(1)} %fusion.26, f32[4,256]{1,0:T(4,128)S(1)} %get-tuple-element.41, f32[512,256,4]{1,0,2:T(8,128)} %copy-done.6, pred[256,512]{0,1:T(8,128)(4,1)S(1)} %copy-done.30), kind=kOutput, calls=%fused_computation.70 | convolution fusion | flops 136839168 | bytes 2760704 | tf_op jit(solution)/shard_map/kgqs,qkgd->skd/dot_general | solution.py:147
  133.3 1.7 fusion.32
  135.0 1.5 convolution_bitcast_fusion.5
  136.6 1.2 fusion.46
  139.4 1.4 pad_maximum_fusion
  140.7 5.7 %all-to-all-start.2 = ((bf16[8,128,6,128]{1,3,2,0:T(8,128)(2,1)}), bf16[8,128,6,128]{1,3,2,0:T(8,128)(2,1)}, u32[]{:S(2)}, u32[]{:S(2)}) async-start(bf16[8,128,6,128]{1,3,2,0:T(8,128)(2,1)} %pad_maximum_fusion), calls=%async_computation.2 | async-start | bytes 3145728 | tf_op jit(solution)/shard_map/all_to_all | solution.py:165
  146.4 0.7 reduce-scatter.5.cloned.1.call-update
  147.1 1.3 reduce_sum.116
  148.4 18.2 %all-to-all-done.2 = bf16[8,128,6,128]{1,3,2,0:T(8,128)(2,1)} async-done(((bf16[8,128,6,128]{1,3,2,0:T(8,128)(2,1)}), bf16[8,128,6,128]{1,3,2,0:T(8,128)(2,1)}, u32[]{:S(2)}, u32[]{:S(2)}) %all-to-all-start.2) | async-done | bytes 1572896 | tf_op jit(solution)/shard_map/all_to_all | solution.py:165
  166.6 1.3 slice.205
  168.0 1.3 copy.233
  169.3 1.1 fusion.107
  170.3 0.9 copy.235
  171.2 0.8 copy.234
  172.0 4.2 %reduce-scatter.5.cloned.1.call-done = f32[512,64]{0,1:T(8,128)} async-done(((f32[512,256]{0,1:T(8,128)}), f32[512,64]{0,1:T(8,128)}) %reduce-scatter.5.cloned.1.call-update) | async-done | bytes 131088 | tf_op jit(solution)/shard_map/reduce_scatter | solution.py:179
  (133 shorter events, 11.7 us)
Async XLA Ops:
  7.2 77.1 %copy-start = (bf16[512,2048]{1,0:T(8,128)(2,1)S(1)}, bf16[512,2048]{1,0:T(8,128)(2,1)}, u32[]{:S(2)}) copy-start(bf16[512,2048]{1,0:T(8,128)(2,1)} %param.10) | copy-start | bytes 6291460
  7.2 63.3 %all-gather.3.cloned.1.call-start = ((), (), s32[]{:S(2)}) async-start(), calls=%async_computation.7 | async-start | bytes 4718592 | tf_op jit(solution)/shard_map/all_gather | solution.py:106
  17.4 6.6 %copy-start.43 = (s32[1,16]{1,0:T(1,128)S(1)}, s32[1,16]{1,0:T(1,128)}, u32[]{:S(2)}) copy-start(s32[1,16]{1,0:T(1,128)} %param.12) | copy-start | bytes 196
  17.4 6.6 %copy-start.44 = (s32[1,16]{1,0:T(1,128)S(1)}, s32[1,16]{1,0:T(1,128)}, u32[]{:S(2)}) copy-start(s32[1,16]{1,0:T(1,128)} %param.13) | copy-start | bytes 196
  17.4 42.7 %all-to-all-start = ((bf16[8,128,6,128]{3,1,2,0:T(8,128)(2,1)}), bf16[8,128,6,128]{3,1,2,0:T(8,128)(2,1)}, u32[]{:S(2)}, u32[]{:S(2)}) async-start(bf16[8,128,6,128]{3,1,2,0:T(8,128)(2,1)} %copy.192), calls=%async_computation | async-start | bytes 3145728 | tf_op jit(solution)/shard_map/all_to_all | solution.py:50
  23.9 122.5 %reduce-scatter.3.cloned.1.call-start = ((), (), s32[]{:S(2)}) async-start(), calls=%async_computation.5 | async-start | bytes 4718592 | tf_op jit(solution)/shard_map/reduce_scatter | solution.py:178
  24.7 38.9 %copy-start.31 = (pred[256,512]{0,1:T(8,128)(4,1)}, pred[256,512]{0,1:T(8,128)(4,1)S(1)}, u32[]{:S(2)}) copy-start(pred[256,512]{0,1:T(8,128)(4,1)S(1)} %compare_and_fusion.1) | copy-start | bytes 393220
  25.7 37.0 %copy-start.28 = (pred[256,512]{0,1:T(8,128)(4,1)}, pred[256,512]{0,1:T(8,128)(4,1)S(1)}, u32[]{:S(2)}) copy-start(pred[256,512]{0,1:T(8,128)(4,1)S(1)} %get-tuple-element.50) | copy-start | bytes 393220
  61.6 6.2 %copy-start.2 = (bf16[8,128,6,128]{3,1,0,2:T(8,128)(2,1)}, bf16[8,128,6,128]{3,1,0,2:T(8,128)(2,1)S(1)}, u32[]{:S(2)}) copy-start(bf16[8,128,6,128]{3,1,0,2:T(8,128)(2,1)S(1)} %copy.193) | copy-start | bytes 4718596
  62.6 2.9 %copy-start.6 = (f32[512,256,4]{1,0,2:T(8,128)}, f32[512,256,4]{1,0,2:T(8,128)S(1)}, u32[]{:S(2)}) copy-start(f32[512,256,4]{1,0,2:T(8,128)S(1)} %get-tuple-element.42) | copy-start | bytes 6291460
  63.1 1.1 copy-start.35
  63.6 3.3 %copy-start.8 = (f32[512,256,4]{1,0,2:T(8,128)}, f32[512,256,4]{1,0,2:T(8,128)S(1)}, u32[]{:S(2)}) copy-start(f32[512,256,4]{1,0,2:T(8,128)S(1)} %get-tuple-element.44) | copy-start | bytes 6291460
  64.7 3.2 %copy-start.11 = (f32[512,256,4]{1,0,2:T(8,128)}, f32[512,256,4]{1,0,2:T(8,128)S(1)}, u32[]{:S(2)}) copy-start(f32[512,256,4]{1,0,2:T(8,128)S(1)} %get-tuple-element.46) | copy-start | bytes 6291460
  65.1 1.0 copy-start.29
  67.1 1.5 copy-start.19
  84.3 3.8 %copy-start.4 = (bf16[1,1024,2048]{2,1,0:T(8,128)(2,1)S(1)}, bf16[1,1024,2048]{2,1,0:T(8,128)(2,1)}, u32[]{:S(2)}) copy-start(bf16[1,1024,2048]{2,1,0:T(8,128)(2,1)} %all-gather.3.cloned.1.call-done) | copy-start | bytes 12582916
  90.5 6.4 %copy-start.15 = (bf16[1024,512]{0,1:T(8,128)(2,1)}, bf16[1024,512]{0,1:T(8,128)(2,1)S(1)}, u32[]{:S(2)}) copy-start(bf16[1024,512]{0,1:T(8,128)(2,1)S(1)} %fusion.27) | copy-start | bytes 3145732
  90.5 1.1 copy-start.25
  90.5 1.4 copy-start.27
  90.5 1.9 %copy-start.3 = (bf16[8,128,6,128]{3,1,0,2:T(8,128)(2,1)S(1)}, bf16[8,128,6,128]{3,1,0,2:T(8,128)(2,1)}, u32[]{:S(2)}) copy-start(bf16[8,128,6,128]{3,1,0,2:T(8,128)(2,1)} %copy-done.2) | copy-start | bytes 4718596
  90.5 2.6 %copy-start.12 = (f32[512,256,4]{1,0,2:T(8,128)S(1)}, f32[512,256,4]{1,0,2:T(8,128)}, u32[]{:S(2)}) copy-start(f32[512,256,4]{1,0,2:T(8,128)} %copy-done.11) | copy-start | bytes 6291460
  90.5 2.6 %copy-start.36 = (pred[256,512]{0,1:T(8,128)(4,1)S(1)}, pred[256,512]{0,1:T(8,128)(4,1)}, u32[]{:S(2)}) copy-start(pred[256,512]{0,1:T(8,128)(4,1)} %get-tuple-element.49) | copy-start | bytes 393220
  90.7 8.6 %collective-permute-start = (bf16[4,128,2048]{2,1,0:T(8,128)(2,1)S(1)}, bf16[4,128,2048]{2,1,0:T(8,128)(2,1)S(1)}, u32[]{:S(2)}, u32[]{:S(2)}) collective-permute-start(bf16[4,128,2048]{2,1,0:T(8,128)(2,1)S(1)} %dynamic-slice_bitcast_fusion), channel_id=1, source_target_pairs={{0,32},{32,0},{1,33},{33,1},{2,34},{34,2},{3,35},{35,3},{4,36},{36... | collective-permute-start | bytes 6291464 | tf_op jit(solution)/shard_map/ppermute | solution.py:118
  95.4 2.0 %copy-start.9 = (f32[512,256,4]{1,0,2:T(8,128)S(1)}, f32[512,256,4]{1,0,2:T(8,128)}, u32[]{:S(2)}) copy-start(f32[512,256,4]{1,0,2:T(8,128)} %copy-done.8) | copy-start | bytes 6291460
  95.5 2.0 %copy-start.33 = (pred[256,512]{0,1:T(8,128)(4,1)S(1)}, pred[256,512]{0,1:T(8,128)(4,1)}, u32[]{:S(2)}) copy-start(pred[256,512]{0,1:T(8,128)(4,1)} %copy-done.31) | copy-start | bytes 393220
  95.9 3.4 %copy-start.14 = (bf16[4,256,256]{1,2,0:T(8,128)(2,1)}, bf16[4,256,256]{1,2,0:T(8,128)(2,1)S(1)}, u32[]{:S(2)}) copy-start(bf16[4,256,256]{1,2,0:T(8,128)(2,1)S(1)} %fusion.38) | copy-start | bytes 1572868
  101.5 29.1 %all-to-all-start.1 = ((bf16[4,128,2048]{2,1,0:T(8,128)(2,1)}), bf16[4,128,2048]{2,1,0:T(8,128)(2,1)S(1)}, u32[]{:S(2)}, u32[]{:S(2)}) async-start(bf16[4,128,2048]{2,1,0:T(8,128)(2,1)} %fusion), calls=%async_computation.1 | async-start | bytes 4194304 | tf_op jit(solution)/shard_map/all_to_all | solution.py:120
  106.6 4.6 %copy-start.5 = (bf16[4,256,512]{1,2,0:T(8,128)(2,1)S(1)}, bf16[4,256,512]{1,2,0:T(8,128)(2,1)}, u32[]{:S(2)}) copy-start(bf16[4,256,512]{1,2,0:T(8,128)(2,1)} %fusion.31) | copy-start | bytes 3145732
  106.6 6.7 %copy-start.13 = (f32[512,256,4]{1,0,2:T(8,128)S(1)}, f32[512,256,4]{1,0,2:T(8,128)}, u32[]{:S(2)}) copy-start(f32[512,256,4]{1,0,2:T(8,128)} %copy-done.11) | copy-start | bytes 6291460
  106.6 6.7 %copy-start.37 = (pred[256,512]{0,1:T(8,128)(4,1)S(1)}, pred[256,512]{0,1:T(8,128)(4,1)}, u32[]{:S(2)}) copy-start(pred[256,512]{0,1:T(8,128)(4,1)} %get-tuple-element.49) | copy-start | bytes 393220
  113.3 1.8 copy-start.16
  115.1 1.1 copy-start.40
  115.1 1.7 copy-start.10
  115.1 1.7 copy-start.34
  116.8 13.8 %copy-start.17 = (bf16[1024,512]{0,1:T(8,128)(2,1)S(1)}, bf16[1024,512]{0,1:T(8,128)(2,1)}, u32[]{:S(2)}) copy-start(bf16[1024,512]{0,1:T(8,128)(2,1)} %copy-done.15) | copy-start | bytes 3145732
  116.8 13.8 %copy-start.30 = (pred[256,512]{0,1:T(8,128)(4,1)S(1)}, pred[256,512]{0,1:T(8,128)(4,1)}, u32[]{:S(2)}) copy-start(pred[256,512]{0,1:T(8,128)(4,1)} %copy-done.28) | copy-start | bytes 393220
  130.6 2.5 %copy-start.20 = (bf16[256,1,4,128]{0,3,2,1:T(8,128)(2,1)S(1)}, bf16[256,1,4,128]{0,3,2,1:T(8,128)(2,1)}, u32[]{:S(2)}) copy-start(bf16[256,1,4,128]{0,3,2,1:T(8,128)(2,1)} %copy-done.19) | copy-start | bytes 786436
  130.6 2.6 %copy-start.7 = (f32[512,256,4]{1,0,2:T(8,128)S(1)}, f32[512,256,4]{1,0,2:T(8,128)}, u32[]{:S(2)}) copy-start(f32[512,256,4]{1,0,2:T(8,128)} %copy-done.6) | copy-start | bytes 6291460
  135.0 2.8 %copy-start.21 = (bf16[256,1,4,128]{0,3,2,1:T(8,128)(2,1)S(1)}, bf16[256,1,4,128]{0,3,2,1:T(8,128)(2,1)}, u32[]{:S(2)}) copy-start(bf16[256,1,4,128]{0,3,2,1:T(8,128)(2,1)} %fusion.40) | copy-start | bytes 786436
  135.0 2.8 %copy-start.22 = (bf16[256,1,4,128]{0,3,2,1:T(8,128)(2,1)S(1)}, bf16[256,1,4,128]{0,3,2,1:T(8,128)(2,1)}, u32[]{:S(2)}) copy-start(bf16[256,1,4,128]{0,3,2,1:T(8,128)(2,1)} %fusion.44) | copy-start | bytes 786436
  135.0 2.8 %copy-start.23 = (bf16[256,1,4,128]{0,3,2,1:T(8,128)(2,1)S(1)}, bf16[256,1,4,128]{0,3,2,1:T(8,128)(2,1)}, u32[]{:S(2)}) copy-start(bf16[256,1,4,128]{0,3,2,1:T(8,128)(2,1)} %fusion.45) | copy-start | bytes 786436
  138.0 1.0 copy-start.41
  138.0 1.1 copy-start.42
  138.3 1.0 copy-start.18
  138.3 1.0 copy-start.39
  140.7 25.9 %all-to-all-start.2 = ((bf16[8,128,6,128]{1,3,2,0:T(8,128)(2,1)}), bf16[8,128,6,128]{1,3,2,0:T(8,128)(2,1)}, u32[]{:S(2)}, u32[]{:S(2)}) async-start(bf16[8,128,6,128]{1,3,2,0:T(8,128)(2,1)} %pad_maximum_fusion), calls=%async_computation.2 | async-start | bytes 3145728 | tf_op jit(solution)/shard_map/all_to_all | solution.py:165
  146.4 29.8 %reduce-scatter.5.cloned.1.call-start = ((), (), s32[]{:S(2)}) async-start(), calls=%async_computation.6 | async-start | bytes 655360 | tf_op jit(solution)/shard_map/reduce_scatter | solution.py:179
  167.9 8.3 %copy-start.1 = (bf16[512,2048]{1,0:T(8,128)(2,1)S(1)}, bf16[512,2048]{1,0:T(8,128)(2,1)}, u32[]{:S(2)}) copy-start(bf16[512,2048]{1,0:T(8,128)(2,1)} %param.10) | copy-start | bytes 6291460
  (4 other events, 3.3 us)
Sparse Core Ops, SparseCore 0:
  9.9 51.9 all-gather.2
  84.4 55.7 reduce-scatter.2
  150.3 25.8 reduce-scatter.4
